TPU v7x, 256 devices: a whole 4x4x8 slice. The times are simulated.
256 devices in a mesh: gx: 8 (over z), gy: 32 (over y, x, core).
Axes of the slice: x: 4, y: 4, z: 8, core: 2. Of those that a mesh axis runs over, the one named last changes fastest.
Arguments:
- lengths: int32 [17], replicated, may hold values from 16 to 16384, as said below
- page_table: int32 [1169], replicated, may hold values from 0 to 1287, as said below
- projected: bfloat16 [18432, 9216], P('gx', 'gy'), may hold values from -8 to 8
- residual: bfloat16 [18432, 3072], P('gx', 'gy'), may hold values from -6 to 6
- out_weight: bfloat16 [3072, 3072], P('gx', 'gy'), may hold values from -0.109375 to 0.109375
Outputs:
- hidden: bfloat16 [18432, 3072], P('gx', 'gy')
- cache_pages: bfloat16 [1288, 32, 3072], P('gx', 'gy')
Inputs may be any that keep to these rules, and one draw needn't show every extreme that they name: `lengths`: one prompt of 16384 tokens at a place drawn from the seed and 16 short prompts of 16 to 240 tokens; they sum to 18432. `page_table`: entry g is the physical page of logical page g (the pages of each prompt in order, 16 tokens each, prompts in packing order). Distinct logical pages in use get distinct physical pages, and such a page lies in [d * 161, (d + 1) * 161) where d is the index of gx whose tokens hold the page's first token. Entries past the last logical page in use are arbitrary; the last two entries are never in use and hold 0 and 1287.
All inputs are finite; a program needn't handle non-finite values.
Results may differ from a plain program's by a relative error of at most 0.012.
The roundings to bfloat16 on the way count: a program that leaves them out, or rounds other values in their place, can miss the bound.
Values may be sent and summed in bfloat16 or wider, within the bound.
No kernel may reach another device: no remote copies, remote signals or barrier semaphores. Data moves between devices by JAX's collectives and lax.ppermute only.
A program may use at most 128 MiB of HBM per device.

v0:
```python
from functools import partial
import math

import jax
import jax.numpy as jnp
from jax import lax
from jax.sharding import PartitionSpec as P

HD = 96
PAGE = 16


def passed_along(block, axis, distance):
    devices = range(lax.axis_size(axis))
    route = [(i - distance, i) for i in devices if i - distance in devices]
    return lax.ppermute(block, axis, route)


def segment_of(ends_at, token_index):
    return jnp.sum((ends_at[None, :] <= token_index[:, None]).astype(jnp.int32), axis=1)


def rotate(values, position):
    half_size = HD // 2
    inverse = 10000.0 ** (-(jnp.arange(half_size, dtype=jnp.float32) * 2.0) / HD)
    angle = position.astype(jnp.float32)[:, None, None] * inverse[None, None, :]
    cosine = jnp.cos(angle)
    sine_part = jnp.sin(angle)
    widened = values.astype(jnp.float32)
    front_half = widened[..., :half_size]
    back_half = widened[..., half_size:]
    turned = jnp.concatenate(
        [front_half * cosine - back_half * sine_part, back_half * cosine + front_half * sine_part],
        axis=-1,
    )
    return turned.astype(jnp.bfloat16)


def tile_update(
    query_block,
    query_segment,
    query_index,
    key_block,
    value_block,
    key_segment,
    key_index,
    carry_state,
):
    running_max, running_sum, running_acc = carry_state
    scores = jnp.einsum(
        "qhd,khd->hqk", query_block, key_block, preferred_element_type=jnp.float32
    ) * (1.0 / math.sqrt(HD))
    visible = (query_segment[:, None] == key_segment[None, :]) & (
        query_index[:, None] >= key_index[None, :]
    )
    scores = jnp.where(visible[None], scores, -1e30)
    new_max = jnp.maximum(running_max, jnp.max(scores, axis=2))
    weights = jnp.where(visible[None], jnp.exp(scores - new_max[:, :, None]), 0.0)
    factor = jnp.exp(running_max - new_max)
    new_sum = running_sum * factor + jnp.sum(weights, axis=2)
    new_acc = running_acc * factor[:, :, None] + jnp.einsum(
        "hqk,khd->hqd",
        weights.astype(jnp.bfloat16),
        value_block,
        preferred_element_type=jnp.float32,
    )
    return (new_max, new_sum, new_acc)


def keep_state(carry_state):
    return carry_state


def per_device(lengths, page_table, projected, residual, out_weight):
    row_count = projected.shape[0]
    local_heads = projected.shape[1] // (3 * HD)
    group_size = lax.axis_size("gx")
    group_index = lax.axis_index("gx")
    first_row = group_index * row_count
    ends_at = jnp.cumsum(lengths)
    starts_at = ends_at - lengths
    own_index = first_row + jnp.arange(row_count, dtype=jnp.int32)
    own_segment = segment_of(ends_at, own_index)
    own_position = own_index - starts_at[own_segment]
    split_heads = projected.reshape(row_count, local_heads, 3, HD)
    rotated_queries = rotate(split_heads[:, :, 0], own_position)
    rotated_keys = rotate(split_heads[:, :, 1], own_position)
    key_value = jnp.concatenate([rotated_keys, split_heads[:, :, 2]], axis=-1)
    half_rows = row_count // 2
    query_segment = segment_of(ends_at, own_index)
    query_rows = half_rows // max(1, half_rows // 576)
    block_count = row_count // query_rows
    query_blocks = [
        rotated_queries[number * query_rows : (number + 1) * query_rows]
        for number in range(block_count)
    ]
    initial = tuple(
        (
            (
                jnp.full((local_heads, query_rows), -1e30, jnp.float32),
                jnp.zeros((local_heads, query_rows), jnp.float32),
                jnp.zeros((local_heads, query_rows, HD), jnp.float32),
            )
            for number in range(block_count)
        )
    )
    portion = lax.all_gather(key_value, "gx", axis=0, tiled=True)
    key_count = portion.shape[0]
    key_rows = key_count // max(1, key_count // 1152)
    steps_needed = key_count // key_rows
    key_index = jnp.arange(key_count, dtype=jnp.int32)
    key_segment = segment_of(ends_at, key_index)
    scanned_input = (
        portion.reshape(steps_needed, key_rows, local_heads, 2 * HD),
        key_index.reshape(steps_needed, key_rows),
        key_segment.reshape(steps_needed, key_rows),
    )

    def advance(block_states, scanned):
        key_block, block_index, block_segment = scanned
        updated = []
        for number in range(block_count):
            lower_row = number * query_rows
            upper_row = lower_row + query_rows
            live = (block_index[0] <= own_index[upper_row - 1]) & (
                block_segment[key_rows - 1] >= query_segment[lower_row]
            )
            working = partial(
                tile_update,
                query_blocks[number],
                query_segment[lower_row:upper_row],
                own_index[lower_row:upper_row],
                key_block[:, :, :HD],
                key_block[:, :, HD:],
                block_segment,
                block_index,
            )
            updated.append(lax.cond(live, working, keep_state, block_states[number]))
        return (tuple(updated), None)

    folded = lax.scan(advance, initial, scanned_input)[0]
    pieces = []
    for number in range(block_count):
        running_max, running_sum, running_acc = folded[number]
        normalized = (running_acc / running_sum[:, :, None]).astype(jnp.bfloat16)
        pieces.append(jnp.swapaxes(normalized, 0, 1).reshape(query_rows, local_heads * HD))
    attended = jnp.concatenate(pieces, axis=0)
    weight_columns = lax.all_gather(out_weight, "gx", axis=0, tiled=True)
    update = jnp.dot(
        lax.all_gather(attended, "gy", axis=1, tiled=True),
        weight_columns,
        preferred_element_type=jnp.float32,
    )
    hidden = (residual.astype(jnp.float32) + update).astype(jnp.bfloat16)
    tail_rows = passed_along(key_value[: PAGE - 1], "gx", -1)
    extended = jnp.concatenate([key_value, tail_rows], axis=0)
    extended_index = first_row + jnp.arange(row_count + PAGE - 1, dtype=jnp.int32)
    extended_segment = jnp.minimum(segment_of(ends_at, extended_index), lengths.shape[0] - 1)
    extended_position = extended_index - starts_at[extended_segment]
    page_count = (lengths + PAGE - 1) // PAGE
    page_base = jnp.cumsum(page_count) - page_count
    logical = page_base[extended_segment] + extended_position // PAGE
    page_first = extended_index - extended_position % PAGE
    pages_held = row_count // PAGE + lengths.shape[0]
    owned = (page_first // row_count == group_index) & (extended_index < group_size * row_count)
    target = jnp.where(owned, page_table[logical] - group_index * pages_held, pages_held)
    cache_pages = jnp.zeros((pages_held, local_heads, PAGE, 2 * HD), jnp.bfloat16)
    cache_pages = cache_pages.at[target, :, extended_position % PAGE].set(extended, mode="drop")
    return (hidden, cache_pages.reshape(pages_held, local_heads, PAGE * 2 * HD))


def solution(mesh):
    placed = (P(), P(), P("gx", "gy"), P("gx", "gy"), P("gx", "gy"))
    return jax.shard_map(
        per_device,
        mesh=mesh,
        in_specs=placed,
        out_specs=(P("gx", "gy"), P("gx", "gy", None)),
        check_vma=False,
    )
```

profile of v0, /device:TPU:1, one launch (start us, length us, event | category | flops | bytes accessed | tf_op | source)
XLA Modules:
  0.0 585.7 jit_solution(8751553567018417610)
XLA Ops:
  9.7 4.4 fusion.96
  14.4 1.4 fusion.83
  15.8 6.2 %fusion.92 = f32[2304]{0:T(1024)S(1)} fusion(pred[2304]{0:T(1024)(128)(4,1)S(1)} %get-tuple-element.388, pred[2304]{0:T(1024)(128)(4,1)S(1)} %get-tuple-element.387, pred[2304]{0:T(1024)(128)(4,1)S(1)} %get-tuple-element.386, pred[2304]{0:T(1024)(128)(4,1)S(1)} %get-tuple-element.385, pred[2304]{0:T(1024)(128)(4,1)S(1)} %get-tuple-element.384, ...), kind=kLoop, calls=%fused_computation.184 | loop fusion | flops 29952 | bytes 41516 | tf_op jit(solution)/shard_map/convert_element_type | solution.py:26
  22.0 2.0 fusion.82
  25.7 84.9 %all-gather.3.cloned.1.call-done = bf16[18432,1,192]{0,2,1:T(8,128)(2,1)} async-done(((bf16[2304,1,192]{0,2,1:T(8,128)(2,1)}), bf16[18432,1,192]{0,2,1:T(8,128)(2,1)}) %all-gather.3.cloned.1.call-update) | async-done | bytes 7077904 | tf_op jit(solution)/shard_map/all_gather | solution.py:107
  110.6 7.0 %copy.26 = bf16[1,24,16,8,1152]{4,3,1,0,2:T(8,128)(2,1)} copy(bf16[1,24,16,8,1152]{4,3,2,1,0:T(8,128)(2,1)} %bitcast.168) | data formatting | bytes 14155776 | tf_op jit(solution)/shard_map/reshape | solution.py:114
  117.8 229.6 %while.32 = (s32[]{:T(128)}, f32[1,576]{1,0:T(1,128)S(1)}, f32[1,576]{1,0:T(1,128)S(1)}, f32[1,576,96]{1,2,0:T(8,128)S(1)}, f32[1,576]{1,0:T(1,128)S(1)}, /*inde...) while((s32[]{:T(128)}, f32[1,576]{1,0:T(1,128)S(1)}, ...), condition=%wide.region_20.21_spmd, body=%wide.region_3.20_spmd.sunk | while | flops 1067440896 | bytes 37980108 | solution.py:141
  118.0 1.1 dynamic-slice_bitcast_fusion.2
  123.4 3.1 conditional.11
  129.0 2.9 conditional.10
  134.6 3.1 conditional.9
  140.2 2.9 conditional.8
  143.2 1.1 dynamic-slice_bitcast_fusion.2
  148.6 3.1 conditional.11
  154.2 2.9 conditional.10
  162.4 1.1 dynamic-slice_bitcast_fusion.2
  215.3 1.1 dynamic-slice_bitcast_fusion.2
  228.5 1.1 dynamic-slice_bitcast_fusion.2
  241.7 1.1 dynamic-slice_bitcast_fusion.2
  294.6 1.1 dynamic-slice_bitcast_fusion.2
  307.8 1.1 dynamic-slice_bitcast_fusion.2
  321.0 1.1 dynamic-slice_bitcast_fusion.2
  349.4 1.5 collective-permute-start
  352.0 8.8 %fusion.93 = (s32[2319]{0:T(1024)S(1)}, s32[2319]{0:T(1024)S(1)}, s32[2319,1]{0,1:T(1,128)S(1)}) fusion(s32[]{:T(128)} %bitcast.66, s32[]{:T(128)} %bitcast.67, s32[]{:T(128)} %bitcast.68, s32[]{:T(128)} %bitcast.69, s32[]{:T(128)} %bitcast.70, s32[]{:T(128)} %bitcast.72, s32[]{:T(128)} %bitcast.71, s32[]{:T(128)} %bitcast.46, s32[]{:T(128)} %bitcast.45, ...), kind=kLoop, calls=%fused_computation.187 | loop fusion | flops 48699 | bytes 37160 | tf_op jit(solution)/shard_map/gather | solution.py:162
  361.1 6.2 %select_select_fusion.1 = s32[2319]{0:T(1024)S(1)} fusion(pred[2319]{0:T(1024)(128)(4,1)S(1)} %get-tuple-element.378, pred[2319]{0:T(1024)(128)(4,1)S(1)} %get-tuple-element.377, pred[2319]{0:T(1024)(128)(4,1)S(1)} %get-tuple-element.376, pred[2319]{0:T(1024)(128)(4,1)S(1)} %get-tuple-element.375, pred[2319]{0:T(1024)(128)(4,1)S(1)} %get-tuple-element.374, ...), kind=kLoop, calls=%fused_computation.182 | loop fusion | flops 23190 | bytes 41782 | tf_op jit(solution)/shard_map/gather | solution.py:159
  367.3 6.5 %select_select_fusion = s32[2319]{0:T(1024)S(1)} fusion(pred[2319]{0:T(1024)(128)(4,1)S(1)} %get-tuple-element.378, pred[2319]{0:T(1024)(128)(4,1)S(1)} %get-tuple-element.377, pred[2319]{0:T(1024)(128)(4,1)S(1)} %get-tuple-element.376, pred[2319]{0:T(1024)(128)(4,1)S(1)} %get-tuple-element.375, pred[2319]{0:T(1024)(128)(4,1)S(1)} %get-tuple-element.374, ...), kind=kLoop, calls=%fused_computation.181 | loop fusion | flops 23190 | bytes 41782 | tf_op jit(solution)/shard_map/gather | solution.py:162
  374.0 12.7 %gather_fusion = s32[2319]{0:T(1024)S(1)} fusion(s32[1169]{0:T(1024)S(1)} %copy-done, s32[3072]{0:T(1024)S(1)} %pad_clamp_fusion), kind=kCustom, calls=%fused_computation | custom fusion | bytes 27828 | tf_op jit(solution)/shard_map/gather | solution.py:166
  387.2 165.8 %all_gather.11 = bf16[3072,96]{0,1:T(8,128)(2,1)S(1)} all-gather(bf16[384,96]{0,1:T(8,128)(2,1)S(1)} %copy-done.2), channel_id=1, replica_groups=mesh['gx'=8,'gy'=32] {'gx'}, dimensions={0}, use_global_device_ids=true | all-gather | bytes 663552 | tf_op jit(solution)/shard_map/all_gather | solution.py:148
  553.0 1.6 copy.23
  554.6 13.5 %scatter_custom_fusion = bf16[2576,192]{1,0:T(8,128)(2,1)S(1)} fusion(s32[2319]{0:T(1024)S(1)} %broadcast_select_fusion, bf16[2319,192]{1,0:T(8,128)(2,1)} %copy.23, bf16[]{:T(256)} %constant.123.clone.1), kind=kCustom, calls=%fused_computation.81 | custom fusion | bytes 989696
  568.2 2.5 reshape.620
  570.7 8.2 %fusion.64 = bf16[2304,96]{0,1:T(8,128)(2,1)} fusion(bf16[3072,96]{0,1:T(8,128)(2,1)S(1)} %all_gather.11, bf16[2304,3072]{0,1:T(8,128)(2,1)} %all-gather.5.cloned.1.call-done, bf16[2304,96]{0,1:T(8,128)(2,1)S(1)} %copy-done.1), kind=kOutput, calls=%fused_computation.76 | convolution fusion | flops 1359618048 | bytes 15630336 | tf_op jit(solution)/shard_map/dot_general | solution.py:149
  (260 shorter events, 65.3 us)
Async XLA Ops:
  7.2 366.8 %copy-start = (s32[1169]{0:T(1024)S(1)}, s32[1169]{0:T(1024)}, u32[]{:S(2)}) copy-start(s32[1169]{0:T(1024)} %param.16) | copy-start | bytes 14032
  7.2 103.4 %all-gather.3.cloned.1.call-start = ((), (), s32[]{:S(2)}) async-start(), calls=%async_computation | async-start | bytes 7962624 | tf_op jit(solution)/shard_map/all_gather | solution.py:107
  25.0 545.6 %all-gather.5.cloned.1.call-start = ((), (), s32[]{:S(2)}) async-start(), calls=%async_computation.1 | async-start | bytes 14598144 | tf_op jit(solution)/shard_map/all_gather | solution.py:150
  349.4 203.6 %collective-permute-start = (bf16[15,1,192]{0,2,1:T(8,128)(2,1)S(1)}, bf16[15,1,192]{0,2,1:T(8,128)(2,1)S(1)}, u32[]{:S(2)}, u32[]{:S(2)}) collective-permute-start(bf16[15,1,192]{0,2,1:T(8,128)(2,1)S(1)} %slice.201), channel_id=1, source_target_pairs={{32,0},{64,32},{96,64},{128,96},{160,128},{192,160},{224,192},{33,... | collective-permute-start | bytes 17288 | tf_op jit(solution)/shard_map/ppermute | solution.py:16
  374.0 12.9 %copy-start.3 = (s32[2]{0:T(128)S(1)}, s32[2]{0:T(128)}, u32[]{:S(2)}) copy-start(s32[2]{0:T(128)} %constant.132) | copy-start | bytes 28
  374.0 13.0 %copy-start.4 = (s32[2]{0:T(128)S(1)}, s32[2]{0:T(128)}, u32[]{:S(2)}) copy-start(s32[2]{0:T(128)} %constant.135) | copy-start | bytes 28
  374.0 13.1 %copy-start.2 = (bf16[384,96]{0,1:T(8,128)(2,1)S(1)}, bf16[384,96]{0,1:T(8,128)(2,1)}, u32[]{:S(2)}) copy-start(bf16[384,96]{0,1:T(8,128)(2,1)} %param.19) | copy-start | bytes 221188
  553.0 17.6 %copy-start.1 = (bf16[2304,96]{0,1:T(8,128)(2,1)S(1)}, bf16[2304,96]{0,1:T(8,128)(2,1)}, u32[]{:S(2)}) copy-start(bf16[2304,96]{0,1:T(8,128)(2,1)} %param.18) | copy-start | bytes 1327108
Sparse Core Ops, SparseCore 0:
  25.2 85.3 all-gather.2
  348.7 213.4 all-gather.4
where the time goes:
time: 593 us; the launch traced here: 586 us
  blocking collectives  166 us (28%)
  loops' own time  164 us (28%)
  local copies, waits for them, and re-layouts  89.9 us (15%)
  waiting for transfers between devices  85 us (14%)
  other arithmetic  45.2 us (8%)
  matrix products  19.9 us (3%)
  between operations  14.4 us (2%)
    all_gather x1, blocking collectives, per_device(): weight_columns = lax.all_gather(out_weight, 'gx', axis=0, tiled=True)  166 us
    another operation x1, loops' own time, per_device(): folded = lax.scan(advance, initial, scanned_input)[0]  163 us
    all_gather x1, waiting for transfers between devices, per_device(): portion = lax.all_gather(key_value, 'gx', axis=0, tiled=True)  84.9 us
    squeeze x16, local copies, waits for them, and re-layouts, per_device(): folded = lax.scan(advance, initial, scanned_input)[0]  16.9 us
    gather x2, other arithmetic, per_device(): logical = page_base[extended_segment] + extended_position // PAGE  15.4 us
    unnamed x11, local copies, waits for them, and re-layouts  13.6 us
    gather x1, local copies, waits for them, and re-layouts, per_device(): page_table[logical] - group_index * pages_held  12.7 us
  transfers between devices with their start and end apart: 3, of which 1 were waited for; matrix products, arithmetic and copies ran while one was open for 9% of the time, Pallas kernels for 0%

commit v1 on v0

v1 whole, which is shorter than its diff:
```python
from functools import partial
import math

import jax
import jax.numpy as jnp
from jax import lax
from jax.experimental import pallas as pl
from jax.experimental.pallas import tpu as pltpu
from jax.sharding import PartitionSpec as P

HD = 96
PAGE = 16
BQ = 256
BK = 768
NEG = -1e30


def passed_along(block, axis, distance):
    devices = range(lax.axis_size(axis))
    route = [(i - distance, i) for i in devices if i - distance in devices]
    return lax.ppermute(block, axis, route)


def segment_of(ends_at, token_index):
    return jnp.sum((ends_at[None, :] <= token_index[:, None]).astype(jnp.int32), axis=1)


def rotate(values, position):
    half_size = HD // 2
    inverse = 10000.0 ** (-(jnp.arange(half_size, dtype=jnp.float32) * 2.0) / HD)
    angle = position.astype(jnp.float32)[:, None, None] * inverse[None, None, :]
    cosine = jnp.cos(angle)
    sine_part = jnp.sin(angle)
    widened = values.astype(jnp.float32)
    front_half = widened[..., :half_size]
    back_half = widened[..., half_size:]
    turned = jnp.concatenate(
        [front_half * cosine - back_half * sine_part, back_half * cosine + front_half * sine_part],
        axis=-1,
    )
    return turned.astype(jnp.bfloat16)


def attention_kernel(table_ref, q_ref, lo_ref, kv_ref, *rest, has_init, finalize):
    if has_init:
        m_in, l_in, acc_in = rest[:3]
        rest = rest[3:]
    i = pl.program_id(0)
    b0 = table_ref[i * 8 + 0]
    b1 = table_ref[i * 8 + 1]
    b2 = table_ref[i * 8 + 2]
    b3 = table_ref[i * 8 + 3]
    q_first = table_ref[i * 8 + 4]
    key_offset = table_ref[i * 8 + 5]
    q = q_ref[...]
    lo = lo_ref[...]
    q_index = q_first + lax.broadcasted_iota(jnp.int32, (BQ, 1), 0)
    scale = 1.0 / math.sqrt(HD)

    def step(kb, carry, masked):
        m, l, acc = carry
        start = pl.multiple_of(kb * BK, BK)
        keys = kv_ref[pl.ds(start, BK), pl.ds(0, HD)]
        vals = kv_ref[pl.ds(start, BK), pl.ds(HD, HD)]
        s = lax.dot_general(q, keys, (((1,), (1,)), ((), ())), preferred_element_type=jnp.float32) * scale
        if masked:
            k_index = key_offset + start + lax.broadcasted_iota(jnp.int32, (1, BK), 1)
            visible = (k_index >= lo) & (k_index <= q_index)
            s = jnp.where(visible, s, NEG)
        m_new = jnp.maximum(m, jnp.max(s, axis=1, keepdims=True))
        p = jnp.exp(s - m_new)
        if masked:
            p = jnp.where(visible, p, 0.0)
        alpha = jnp.exp(m - m_new)
        l_new = l * alpha + jnp.sum(p, axis=1, keepdims=True)
        acc_new = acc * alpha + jnp.dot(p.astype(jnp.bfloat16), vals, preferred_element_type=jnp.float32)
        return (m_new, l_new, acc_new)

    if has_init:
        carry = (m_in[...], l_in[...], acc_in[...])
    else:
        carry = (
            jnp.full((BQ, 1), NEG, jnp.float32),
            jnp.zeros((BQ, 1), jnp.float32),
            jnp.zeros((BQ, HD), jnp.float32),
        )
    carry = lax.fori_loop(b0, b1, partial(step, masked=True), carry)
    carry = lax.fori_loop(b1, b2, partial(step, masked=False), carry)
    carry = lax.fori_loop(b2, b3, partial(step, masked=True), carry)
    m, l, acc = carry
    if finalize:
        (out_ref,) = rest
        out_ref[...] = (acc / l).astype(out_ref.dtype)
    else:
        m_out, l_out, acc_out = rest
        m_out[...] = m
        l_out[...] = l
        acc_out[...] = acc


def block_table(q_first_rows, lo_first, lo_last, key_offset, key_rows):
    q_last = q_first_rows + BQ - 1
    local_lo = jnp.clip(lo_first - key_offset, 0, key_rows)
    local_hi = jnp.clip(q_last + 1 - key_offset, 0, key_rows)
    b0 = local_lo // BK
    b3 = jnp.maximum((local_hi + BK - 1) // BK, b0)
    full_lo = (jnp.maximum(lo_last - key_offset, 0) + BK - 1) // BK
    full_hi = (q_first_rows + 1 - key_offset) // BK
    b1 = jnp.clip(full_lo, b0, b3)
    b2 = jnp.clip(full_hi, b1, b3)
    offsets = jnp.broadcast_to(key_offset, q_first_rows.shape)
    zero = jnp.zeros_like(b0)
    table = jnp.stack([b0, b1, b2, b3, q_first_rows, offsets, zero, zero], axis=1)
    return table.reshape(-1).astype(jnp.int32)


def attend(table, queries, lows, kv, state, finalize):
    rows = queries.shape[0]
    key_rows = kv.shape[0]
    grid = (rows // BQ,)
    row_spec = lambda width: pl.BlockSpec((BQ, width), lambda i, t: (i, 0))
    in_specs = [row_spec(HD), row_spec(1), pl.BlockSpec((key_rows, 2 * HD), lambda i, t: (0, 0))]
    operands = [queries, lows, kv]
    if state is not None:
        in_specs += [row_spec(1), row_spec(1), row_spec(HD)]
        operands += list(state)
    if finalize:
        out_shape = jax.ShapeDtypeStruct((rows, HD), jnp.bfloat16)
        out_specs = row_spec(HD)
    else:
        out_shape = (
            jax.ShapeDtypeStruct((rows, 1), jnp.float32),
            jax.ShapeDtypeStruct((rows, 1), jnp.float32),
            jax.ShapeDtypeStruct((rows, HD), jnp.float32),
        )
        out_specs = (row_spec(1), row_spec(1), row_spec(HD))
    kernel = partial(attention_kernel, has_init=state is not None, finalize=finalize)
    return pl.pallas_call(
        kernel,
        grid_spec=pltpu.PrefetchScalarGridSpec(
            num_scalar_prefetch=1,
            grid=grid,
            in_specs=in_specs,
            out_specs=out_specs,
        ),
        out_shape=out_shape,
        compiler_params=pltpu.CompilerParams(vmem_limit_bytes=48 * 1024 * 1024),
    )(table, *operands)


def per_device(lengths, page_table, projected, residual, out_weight):
    row_count = projected.shape[0]
    local_heads = projected.shape[1] // (3 * HD)
    group_size = lax.axis_size("gx")
    group_index = lax.axis_index("gx")
    first_row = group_index * row_count
    ends_at = jnp.cumsum(lengths)
    starts_at = ends_at - lengths
    own_index = first_row + jnp.arange(row_count, dtype=jnp.int32)
    own_segment = segment_of(ends_at, own_index)
    own_position = own_index - starts_at[own_segment]
    split_heads = projected.reshape(row_count, local_heads, 3, HD)
    rotated_queries = rotate(split_heads[:, :, 0], own_position)
    rotated_keys = rotate(split_heads[:, :, 1], own_position)
    key_value = jnp.concatenate([rotated_keys, split_heads[:, :, 2]], axis=-1)
    weight_columns = lax.all_gather(out_weight, "gx", axis=0, tiled=True)
    queries = rotated_queries.reshape(row_count, HD)
    local_kv = key_value.reshape(row_count, 2 * HD)
    queries, local_kv, weight_columns = lax.optimization_barrier((queries, local_kv, weight_columns))
    portion = lax.all_gather(local_kv, "gx", axis=0, tiled=True)
    key_count = portion.shape[0]

    lows = starts_at[own_segment]
    q_first_rows = first_row + jnp.arange(0, row_count, BQ, dtype=jnp.int32)
    lo_first = lows[0::BQ]
    lo_last = lows[BQ - 1 :: BQ]
    lows = lows.reshape(row_count, 1)
    own_table = block_table(q_first_rows, lo_first, lo_last, first_row, row_count)
    state = attend(own_table, queries, lows, local_kv, None, False)
    rest_table = block_table(q_first_rows, lo_first, lo_last, jnp.int32(0), jnp.minimum(first_row, key_count))
    attended = attend(rest_table, queries, lows, portion, state, True)

    update = jnp.dot(
        lax.all_gather(attended, "gy", axis=1, tiled=True),
        weight_columns,
        preferred_element_type=jnp.float32,
    )
    hidden = (residual.astype(jnp.float32) + update).astype(jnp.bfloat16)
    tail_rows = passed_along(key_value[: PAGE - 1], "gx", -1)
    extended = jnp.concatenate([key_value, tail_rows], axis=0)
    extended_index = first_row + jnp.arange(row_count + PAGE - 1, dtype=jnp.int32)
    extended_segment = jnp.minimum(segment_of(ends_at, extended_index), lengths.shape[0] - 1)
    extended_position = extended_index - starts_at[extended_segment]
    page_count = (lengths + PAGE - 1) // PAGE
    page_base = jnp.cumsum(page_count) - page_count
    logical = page_base[extended_segment] + extended_position // PAGE
    page_first = extended_index - extended_position % PAGE
    pages_held = row_count // PAGE + lengths.shape[0]
    owned = (page_first // row_count == group_index) & (extended_index < group_size * row_count)
    target = jnp.where(owned, page_table[logical] - group_index * pages_held, pages_held)
    cache_pages = jnp.zeros((pages_held, local_heads, PAGE, 2 * HD), jnp.bfloat16)
    cache_pages = cache_pages.at[target, :, extended_position % PAGE].set(extended, mode="drop")
    return (hidden, cache_pages.reshape(pages_held, local_heads, PAGE * 2 * HD))


def solution(mesh):
    placed = (P(), P(), P("gx", "gy"), P("gx", "gy"), P("gx", "gy"))
    return jax.shard_map(
        per_device,
        mesh=mesh,
        in_specs=placed,
        out_specs=(P("gx", "gy"), P("gx", "gy", None)),
        check_vma=False,
    )
```

time: 593 us -> 386 us (0.65); the launches traced: 586 us -> 388 us
  loops' own time: 164 us -> 0 us
  waiting for transfers between devices: 85 us -> 225 us
  blocking collectives: 166 us -> 26.5 us
  local copies, waits for them, and re-layouts: 89.9 us -> 28.4 us
  Pallas kernels: 0 us -> 25 us
  other arithmetic: 45.2 us -> 59.5 us
  matrix products: 19.9 us -> 8.19 us
    another operation x65 -> x0, loops' own time: 164 us -> none  [the longest x1 163 us: per_device(): folded = lax.scan(advance, initial, scanned_input)[0]]
    all_gather x1, blocking collectives: 166 us -> 26.5 us  [per_device(): weight_columns = lax.all_gather(out_weight, 'gx', axis=0, tiled=True)]
    all_gather x1, waiting for transfers between devices: 0.01 us -> 139 us  [per_device(): lax.all_gather(attended, 'gy', axis=1, tiled=True)]
    slice x76 -> x3, local copies, waits for them, and re-layouts: 30.9 us -> 1.55 us  [the longest x1 1.37 us: per_device(): rotated_keys = rotate(split_heads[:, :, 1], own_position)]
    pallas_call x0 -> x2, Pallas kernels: none -> 25 us  [attend(): pl.pallas_call(kernel, grid_spec=pltpu.PrefetchScalarGridSpec(num_scalar_...]
    squeeze x16 -> x0, local copies, waits for them, and re-layouts: 16.9 us -> none  [per_device(): folded = lax.scan(advance, initial, scanned_input)[0]]
    unnamed x3 -> x4, other arithmetic: 0.22 us -> 15.2 us
    dot_general x12 -> x0, matrix products: 11.7 us -> none  [the longest x6 5.91 us: tile_update(): jnp.einsum('hqk,khd->hqd', weights.astype(jnp.bfloat16), value_block, pre...]
  transfers between devices with their start and end apart: 3 -> 3, of which waited for: 1 -> 2; matrix products, arithmetic and copies ran while one was open for 9% -> 15% of each run, Pallas kernels for 0% -> 5%
where the time goes in v1:
time: 386 us; the launch traced here: 388 us
  waiting for transfers between devices  225 us (58%)
  other arithmetic  59.5 us (15%)
  local copies, waits for them, and re-layouts  28.4 us (7%)
  blocking collectives  26.5 us (7%)
  Pallas kernels  25 us (6%)
  between operations  14.5 us (4%)
  matrix products  8.19 us (2%)
    all_gather x1, waiting for transfers between devices, per_device(): lax.all_gather(attended, 'gy', axis=1, tiled=True)  139 us
    all_gather x1, waiting for transfers between devices, per_device(): portion = lax.all_gather(local_kv, 'gx', axis=0, tiled=True)  86.3 us
    all_gather x1, blocking collectives, per_device(): weight_columns = lax.all_gather(out_weight, 'gx', axis=0, tiled=True)  26.5 us
    pallas_call x2, Pallas kernels, attend(): pl.pallas_call(kernel, grid_spec=pltpu.PrefetchScalarGridSpec(num_scalar_...  25 us
    unnamed x4, other arithmetic  15.2 us
    gather x2, other arithmetic, per_device(): logical = page_base[extended_segment] + extended_position // PAGE  15.1 us
    gather x1, local copies, waits for them, and re-layouts, per_device(): page_table[logical] - group_index * pages_held  12.7 us
    dot_general x1, matrix products, per_device(): jnp.dot(lax.all_gather(attended, 'gy', axis=1, tiled=True), weight_column...  8.19 us
  transfers between devices with their start and end apart: 3, of which 2 were waited for; matrix products, arithmetic and copies ran while one was open for 15% of the time, Pallas kernels for 5%

profile of v1, /device:TPU:1, one launch (start us, length us, event | category | flops | bytes accessed | tf_op | source)
XLA Modules:
  0.0 388.4 jit_solution(3923728338285133737)
XLA Ops:
  7.2 0.7 copy.48
  8.2 1.2 and_select_fusion.4
  9.3 0.7 fusion.39
  10.2 4.5 %fusion.30 = (s32[2304]{0:T(1024)S(1)}, s32[2304,1]{0,1:T(1,128)S(1)}) fusion(s32[]{:T(128)} %bitcast.11, s32[]{:T(128)} %bitcast.12, s32[]{:T(128)} %bitcast.13, s32[]{:T(128)} %bitcast.14, s32[]{:T(128)} %bitcast.15, s32[]{:T(128)} %bitcast.17, s32[]{:T(128)} %bitcast.16, s32[2304]{0:T(1024)S(1)} %convert_reduce_fusion.1), kind=kLoop, calls=%fused_computation.104 | loop fusion | flops 34560 | bytes 27676 | tf_op jit(solution)/shard_map/gather | solution.py:173
  14.9 1.4 fusion.37
  17.5 26.5 %all_gather.9 = bf16[3072,96]{0,1:T(8,128)(2,1)} all-gather(bf16[384,96]{0,1:T(8,128)(2,1)S(1)} %copy-done.13), channel_id=1, replica_groups=mesh['gx'=8,'gy'=32] {'gx'}, dimensions={0}, use_global_device_ids=true | all-gather | bytes 663552 | tf_op jit(solution)/shard_map/all_gather | solution.py:166
  44.2 6.1 %subtract_convert_fusion = (f32[2304]{0:T(1024)S(1)}, s32[2304]{0:T(1024)S(1)}) fusion(s32[]{:T(128)S(6)} %mul.82, pred[2304]{0:T(1024)(128)(4,1)S(1)} %get-tuple-element.35, pred[2304]{0:T(1024)(128)(4,1)S(1)} %get-tuple-element.34, pred[2304]{0:T(1024)(128)(4,1)S(1)} %get-tuple-element.33, pred[2304]{0:T(1024)(128)(4,1)S(1)} %get-tuple-element.32, ...), kind=kLoop, calls=%fused_computation.97 | loop fusion | flops 29952 | bytes 50732 | tf_op jit(solution)/shard_map/convert_element_type | solution.py:31
  50.3 5.6 %fusion.21 = (bf16[2304,1,48]{2,0,1:T(8,128)(2,1)S(1)}, bf16[2304,1,48]{2,0,1:T(8,128)(2,1)S(1)}, bf16[2304,48]{1,0:T(8,128)(2,1)S(1)}, bf16[2304,48]{1,0:T(8,128)(2,1)S(1)}) fusion(f32[2304,1,96]{2,0,1:T(8,128)S(1)} %get-tuple-element.100, f32[48]{0:T(128)S(1)} %multiply_power_fusion, f32[2304]{0:T(1024)S(1)} %get-tuple-element.45, ...), kind=kLoop, calls=%fused_computation.27 | loop fusion | flops 1880064 | bytes 2663616 | tf_op jit(solution)/shard_map/convert.2
  55.9 0.3 pad_maximum_fusion.1.q_ref
  56.3 0.5 copy-done.7
  57.0 1.9 fusion.42.kv_ref
  59.1 0.4 reshape.682.lo_ref
  60.6 18.5 %shard_map.68 = (f32[2304,1]{1,0:T(8,128)S(1)}, f32[2304,1]{1,0:T(8,128)S(1)}, f32[2304,96]{1,0:T(8,128)S(1)}) custom-call(s32[72]{0:T(128)S(1)} %reshape.471.table_ref, bf16[2304,96]{1,0:T(8,128)(2,1)S(1)} %pad_maximum_fusion.1.q_ref, s32[2304,1]{1,0:T(8,128)S(1)} %reshape.682.lo_ref, bf16[2304,192]{1,0:T(8,128)(2,1)} %fusion.42.kv_ref), custom_call_target="tpu_custom_call" | custom-call | tf_op jit(solution)/shard_map/pallas_call | solution.py:138
  79.1 1.0 copy-done.1
  80.2 1.1 copy-done.3
  81.2 86.3 %all-gather.3.cloned.1.call-done.kv_ref = bf16[18432,192]{1,0:T(8,128)(2,1)} async-done(((bf16[2304,192]{1,0:T(8,128)(2,1)}), bf16[18432,192]{1,0:T(8,128)(2,1)}) %all-gather.3.cloned.1.call-update) | async-done | bytes 7077904 | tf_op jit(solution)/shard_map/all_gather | solution.py:170
  167.5 1.3 copy-done.2
  168.8 1.3 copy-done.4
  170.0 6.5 %shard_map.69 = bf16[2304,96]{1,0:T(8,128)(2,1)S(1)} custom-call(s32[72]{0:T(128)S(1)} %reshape.467.table_ref, bf16[2304,96]{1,0:T(8,128)(2,1)S(1)} %pad_maximum_fusion.1.q_ref, s32[2304,1]{1,0:T(8,128)S(1)} %reshape.682.lo_ref, bf16[18432,192]{1,0:T(8,128)(2,1)} %all-gather.3.cloned.1.call-done.kv_ref, f32[2304,1]{1,0:T(8,128)S(1)} %get-tuple-element.10.rest_0_, ...), custom_call_target="tpu_custom_call" | custom-call | tf_op jit(solution)/shard_map/pallas_call | solution.py:138
  176.6 1.0 copy.62
  177.6 0.3 copy-done.8
  178.0 2.0 pad_maximum_fusion
  179.9 1.5 collective-permute-start
  181.7 0.7 fusion.38
  182.6 8.9 %fusion.27 = (s32[2319]{0:T(1024)S(1)}, s32[2319]{0:T(1024)S(1)}, s32[2319,1]{0,1:T(1,128)S(1)}) fusion(s32[]{:T(128)} %bitcast.46, s32[]{:T(128)} %bitcast.47, s32[]{:T(128)} %bitcast.48, s32[]{:T(128)} %bitcast.49, s32[]{:T(128)} %bitcast.50, s32[]{:T(128)} %bitcast.52, s32[]{:T(128)} %bitcast.51, s32[]{:T(128)} %bitcast.17, s32[]{:T(128)} %bitcast.16, ...), kind=kLoop, calls=%fused_computation.99 | loop fusion | flops 48699 | bytes 37160 | tf_op jit(solution)/shard_map/gather | solution.py:196
  191.7 6.1 %select_select_fusion.1 = s32[2319]{0:T(1024)S(1)} fusion(pred[2319]{0:T(1024)(128)(4,1)S(1)} %get-tuple-element.25, pred[2319]{0:T(1024)(128)(4,1)S(1)} %get-tuple-element.24, pred[2319]{0:T(1024)(128)(4,1)S(1)} %get-tuple-element.23, pred[2319]{0:T(1024)(128)(4,1)S(1)} %get-tuple-element.22, pred[2319]{0:T(1024)(128)(4,1)S(1)} %get-tuple-element.21, ...), kind=kLoop, calls=%fused_computation.94 | loop fusion | flops 23190 | bytes 41782 | tf_op jit(solution)/shard_map/gather | solution.py:193
  197.8 6.2 %select_select_fusion = s32[2319]{0:T(1024)S(1)} fusion(pred[2319]{0:T(1024)(128)(4,1)S(1)} %get-tuple-element.25, pred[2319]{0:T(1024)(128)(4,1)S(1)} %get-tuple-element.24, pred[2319]{0:T(1024)(128)(4,1)S(1)} %get-tuple-element.23, pred[2319]{0:T(1024)(128)(4,1)S(1)} %get-tuple-element.22, pred[2319]{0:T(1024)(128)(4,1)S(1)} %get-tuple-element.21, ...), kind=kLoop, calls=%fused_computation.93 | loop fusion | flops 23190 | bytes 41782 | tf_op jit(solution)/shard_map/gather | solution.py:196
  204.2 12.7 %gather_fusion = s32[2319]{0:T(1024)S(1)} fusion(s32[1169]{0:T(1024)S(1)} %copy-done, s32[3072]{0:T(1024)S(1)} %pad_clamp_fusion), kind=kCustom, calls=%fused_computation | custom fusion | bytes 27828 | tf_op jit(solution)/shard_map/gather | solution.py:200
  217.3 15.0 %scatter_custom_fusion = bf16[2576,192]{1,0:T(8,128)(2,1)S(1)} fusion(s32[2319]{0:T(1024)S(1)} %broadcast_select_fusion, bf16[15,1,192]{2,0,1:T(8,128)(2,1)S(1)} %collective-permute-done, bf16[]{:T(256)} %constant.217, bf16[2304,1,96]{2,0,1:T(8,128)(2,1)S(1)} %bitcast.67, bf16[2304,1,48]{2,0,1:T(8,128)(2,1)S(1)} %copy-done.10, ...), kind=kCustom, calls=%fused_computation.15 | custom fusion | flops 3561984 | bytes 2766852
  232.4 2.5 reshape.474
  234.9 138.5 %all-gather.5.cloned.1.call-done = bf16[2304,3072]{0,1:T(8,128)(2,1)} async-done(((bf16[2304,96]{0,1:T(8,128)(2,1)}), bf16[2304,3072]{0,1:T(8,128)(2,1)}) %all-gather.5.cloned.1.call-update) | async-done | bytes 14155792 | tf_op jit(solution)/shard_map/all_gather | solution.py:184
  373.4 8.2 %fusion = bf16[2304,96]{0,1:T(8,128)(2,1)} fusion(bf16[3072,96]{0,1:T(8,128)(2,1)S(1)} %copy-done.11, bf16[2304,3072]{0,1:T(8,128)(2,1)} %all-gather.5.cloned.1.call-done, bf16[2304,96]{0,1:T(8,128)(2,1)S(1)} %copy-done.12), kind=kOutput, calls=%fused_computation.3 | convolution fusion | flops 1359618048 | bytes 15630336 | tf_op jit(solution)/shard_map/dot_general | solution.py:183
  (82 shorter events, 4.7 us)
Async XLA Ops:
  7.2 197.0 %copy-start = (s32[1169]{0:T(1024)S(1)}, s32[1169]{0:T(1024)}, u32[]{:S(2)}) copy-start(s32[1169]{0:T(1024)} %param.6) | copy-start | bytes 14032
  7.2 160.3 %all-gather.3.cloned.1.call-start = ((), (), s32[]{:S(2)}) async-start(), calls=%async_computation | async-start | bytes 10616832 | tf_op jit(solution)/shard_map/all_gather | solution.py:170
  8.1 8.2 %copy-start.14 = (s32[17]{0:T(128)}, s32[17]{0:T(128)S(1)}, u32[]{:S(2)}) copy-start(s32[17]{0:T(128)S(1)} %reduce.2) | copy-start | bytes 208
  16.6 0.9 copy-start.13
  17.5 38.8 %copy-start.5 = (bf16[2304,1,1,96]{3,0,2,1:T(8,128)(2,1)}, bf16[2304,1,1,96]{3,0,2,1:T(8,128)(2,1)S(1)}, u32[]{:S(2)}) copy-start(bf16[2304,1,1,96]{3,0,2,1:T(8,128)(2,1)S(1)} %copy.66) | copy-start | bytes 1327108
  55.9 0.8 copy-start.7
  55.9 1.0 copy-start.9
  58.9 314.5 %all-gather.5.cloned.1.call-start = ((), (), s32[]{:S(2)}) async-start(), calls=%async_computation.1 | async-start | bytes 14598144 | tf_op jit(solution)/shard_map/all_gather | solution.py:184
  79.1 1.0 copy-start.1
  80.2 1.1 copy-start.3
  167.5 1.3 copy-start.2
  168.8 1.3 copy-start.4
  176.6 1.1 copy-start.6
  176.6 1.4 copy-start.8
  178.0 3.5 copy-start.16
  178.0 4.5 %copy-start.15 = (s32[17]{0:T(128)S(1)}, s32[17]{0:T(128)}, u32[]{:S(2)}) copy-start(s32[17]{0:T(128)} %copy-done.14) | copy-start | bytes 208
  179.9 37.4 %collective-permute-start = (bf16[15,1,192]{2,0,1:T(8,128)(2,1)S(1)}, bf16[15,1,192]{2,0,1:T(8,128)(2,1)S(1)}, u32[]{:S(2)}, u32[]{:S(2)}) collective-permute-start(bf16[15,1,192]{2,0,1:T(8,128)(2,1)S(1)} %slice.103), channel_id=1, source_target_pairs={{32,0},{64,32},{96,64},{128,96},{160,128},{192,160},{224,192},{33,... | collective-permute-start | bytes 17288 | tf_op jit(solution)/shard_map/ppermute | solution.py:21
  204.2 12.9 %copy-start.17 = (s32[2]{0:T(128)S(1)}, s32[2]{0:T(128)}, u32[]{:S(2)}) copy-start(s32[2]{0:T(128)} %constant.132) | copy-start | bytes 28
  204.2 13.0 %copy-start.18 = (s32[2]{0:T(128)S(1)}, s32[2]{0:T(128)}, u32[]{:S(2)}) copy-start(s32[2]{0:T(128)} %constant.135) | copy-start | bytes 28
  204.2 13.1 %copy-start.10 = (bf16[2304,1,48]{2,0,1:T(8,128)(2,1)S(1)}, bf16[2304,1,48]{2,0,1:T(8,128)(2,1)}, u32[]{:S(2)}) copy-start(bf16[2304,1,48]{2,0,1:T(8,128)(2,1)} %copy-done.9) | copy-start | bytes 663556
  232.3 141.1 %copy-start.11 = (bf16[3072,96]{0,1:T(8,128)(2,1)S(1)}, bf16[3072,96]{0,1:T(8,128)(2,1)}, u32[]{:S(2)}) copy-start(bf16[3072,96]{0,1:T(8,128)(2,1)} %all_gather.9) | copy-start | bytes 1769476
  232.3 141.0 %copy-start.12 = (bf16[2304,96]{0,1:T(8,128)(2,1)S(1)}, bf16[2304,96]{0,1:T(8,128)(2,1)}, u32[]{:S(2)}) copy-start(bf16[2304,96]{0,1:T(8,128)(2,1)} %param.8) | copy-start | bytes 1327108
Sparse Core Ops, SparseCore 0:
  59.0 108.4 all-gather.2
  177.7 195.6 all-gather.4

commit v2 on v1

--- a/solution.py
+++ b/solution.py
@@ -41,7 +41,7 @@
     return turned.astype(jnp.bfloat16)
 
 
-def attention_kernel(table_ref, q_ref, lo_ref, kv_ref, *rest, has_init, finalize):
+def attention_kernel(table_ref, q_ref, lo_ref, kv_ref, *rest, has_init, finalize, per_source):
     if has_init:
         m_in, l_in, acc_in = rest[:3]
         rest = rest[3:]
@@ -60,8 +60,10 @@
     def step(kb, carry, masked):
         m, l, acc = carry
         start = pl.multiple_of(kb * BK, BK)
-        keys = kv_ref[pl.ds(start, BK), pl.ds(0, HD)]
-        vals = kv_ref[pl.ds(start, BK), pl.ds(HD, HD)]
+        source = kb // per_source
+        within = pl.multiple_of((kb % per_source) * BK, BK)
+        keys = kv_ref[source, pl.ds(within, BK), pl.ds(0, HD)]
+        vals = kv_ref[source, pl.ds(within, BK), pl.ds(HD, HD)]
         s = lax.dot_general(q, keys, (((1,), (1,)), ((), ())), preferred_element_type=jnp.float32) * scale
         if masked:
             k_index = key_offset + start + lax.broadcasted_iota(jnp.int32, (1, BK), 1)
@@ -116,10 +118,9 @@
 
 def attend(table, queries, lows, kv, state, finalize):
     rows = queries.shape[0]
-    key_rows = kv.shape[0]
     grid = (rows // BQ,)
     row_spec = lambda width: pl.BlockSpec((BQ, width), lambda i, t: (i, 0))
-    in_specs = [row_spec(HD), row_spec(1), pl.BlockSpec((key_rows, 2 * HD), lambda i, t: (0, 0))]
+    in_specs = [row_spec(HD), row_spec(1), pl.BlockSpec(kv.shape, lambda i, t: (0, 0, 0))]
     operands = [queries, lows, kv]
     if state is not None:
         in_specs += [row_spec(1), row_spec(1), row_spec(HD)]
@@ -134,7 +135,7 @@
             jax.ShapeDtypeStruct((rows, HD), jnp.float32),
         )
         out_specs = (row_spec(1), row_spec(1), row_spec(HD))
-    kernel = partial(attention_kernel, has_init=state is not None, finalize=finalize)
+    kernel = partial(attention_kernel, has_init=state is not None, finalize=finalize, per_source=rows // BK)
     return pl.pallas_call(
         kernel,
         grid_spec=pltpu.PrefetchScalarGridSpec(
@@ -163,12 +164,12 @@
     rotated_queries = rotate(split_heads[:, :, 0], own_position)
     rotated_keys = rotate(split_heads[:, :, 1], own_position)
     key_value = jnp.concatenate([rotated_keys, split_heads[:, :, 2]], axis=-1)
-    weight_columns = lax.all_gather(out_weight, "gx", axis=0, tiled=True)
     queries = rotated_queries.reshape(row_count, HD)
     local_kv = key_value.reshape(row_count, 2 * HD)
-    queries, local_kv, weight_columns = lax.optimization_barrier((queries, local_kv, weight_columns))
-    portion = lax.all_gather(local_kv, "gx", axis=0, tiled=True)
-    key_count = portion.shape[0]
+    weight_rows = out_weight.reshape(-1, 2 * HD)
+    gathered = lax.all_gather(jnp.concatenate([local_kv, weight_rows], axis=0)[None], "gx", axis=0, tiled=True)
+    weight_columns = gathered[:, row_count:].reshape(-1, out_weight.shape[1])
+    key_count = group_size * row_count
 
     lows = starts_at[own_segment]
     q_first_rows = first_row + jnp.arange(0, row_count, BQ, dtype=jnp.int32)
@@ -176,16 +177,8 @@
     lo_last = lows[BQ - 1 :: BQ]
     lows = lows.reshape(row_count, 1)
     own_table = block_table(q_first_rows, lo_first, lo_last, first_row, row_count)
-    state = attend(own_table, queries, lows, local_kv, None, False)
-    rest_table = block_table(q_first_rows, lo_first, lo_last, jnp.int32(0), jnp.minimum(first_row, key_count))
-    attended = attend(rest_table, queries, lows, portion, state, True)
-
-    update = jnp.dot(
-        lax.all_gather(attended, "gy", axis=1, tiled=True),
-        weight_columns,
-        preferred_element_type=jnp.float32,
-    )
-    hidden = (residual.astype(jnp.float32) + update).astype(jnp.bfloat16)
+    state = attend(own_table, queries, lows, local_kv[None], None, False)
+
     tail_rows = passed_along(key_value[: PAGE - 1], "gx", -1)
     extended = jnp.concatenate([key_value, tail_rows], axis=0)
     extended_index = first_row + jnp.arange(row_count + PAGE - 1, dtype=jnp.int32)
@@ -200,6 +193,17 @@
     target = jnp.where(owned, page_table[logical] - group_index * pages_held, pages_held)
     cache_pages = jnp.zeros((pages_held, local_heads, PAGE, 2 * HD), jnp.bfloat16)
     cache_pages = cache_pages.at[target, :, extended_position % PAGE].set(extended, mode="drop")
+
+    gathered, cache_pages, state = lax.optimization_barrier((gathered, cache_pages, state))
+    rest_table = block_table(q_first_rows, lo_first, lo_last, jnp.int32(0), jnp.minimum(first_row, key_count))
+    attended = attend(rest_table, queries, lows, gathered, state, True)
+
+    update = jnp.dot(
+        lax.all_gather(attended, "gy", axis=1, tiled=True),
+        weight_columns,
+        preferred_element_type=jnp.float32,
+    )
+    hidden = (residual.astype(jnp.float32) + update).astype(jnp.bfloat16)
     return (hidden, cache_pages.reshape(pages_held, local_heads, PAGE * 2 * HD))
 
 

time: 386 us -> 363 us (0.940)
  blocking collectives: 26.5 us -> 0 us
  waiting for transfers between devices: 225 us -> 204 us
  local copies, waits for them, and re-layouts: 28.4 us -> 45.8 us
    all_gather x1, waiting for transfers between devices: 86.3 us -> 10.5 us  [per_device(): lax.all_gather(jnp.concatenate([local_kv, weight_rows], axis=0)[None], 'g...]
    all_gather x1, waiting for transfers between devices: 139 us -> 193 us  [per_device(): lax.all_gather(attended, 'gy', axis=1, tiled=True)]
    all_gather x1 -> x0, blocking collectives: 26.5 us -> none  [per_device(): weight_columns = lax.all_gather(out_weight, 'gx', axis=0, tiled=True)]
    optimization_barrier x0 -> x1, local copies, waits for them, and re-layouts: none -> 12.8 us  [per_device(): lax.optimization_barrier((gathered, cache_pages, state))]
    another operation x5 -> x6, other arithmetic: 5.91 us -> 8.58 us
    unnamed x41 -> x47, local copies, waits for them, and re-layouts: 6.91 us -> 8.97 us
    unnamed x4 -> x5, other arithmetic: 15.2 us -> 17.1 us
  transfers between devices with their start and end apart: 3 -> 3, of which waited for: 2 -> 2; matrix products, arithmetic and copies ran while one was open for 15% -> 17% of each run, Pallas kernels for 5% -> 6%
where the time goes in v2:
time: 363 us
  waiting for transfers between devices  204 us (56%)
  other arithmetic  62.2 us (17%)
  local copies, waits for them, and re-layouts  45.8 us (13%)
  Pallas kernels  26.7 us (7%)
  between operations  14.4 us (4%)
  matrix products  8.25 us (2%)
    all_gather x1, waiting for transfers between devices, per_device(): lax.all_gather(attended, 'gy', axis=1, tiled=True)  193 us
    pallas_call x2, Pallas kernels, attend(): pl.pallas_call(kernel, grid_spec=pltpu.PrefetchScalarGridSpec(num_scalar_...  26.7 us
    unnamed x5, other arithmetic  17.1 us
    gather x2, other arithmetic, per_device(): logical = page_base[extended_segment] + extended_position // PAGE  15.1 us
    optimization_barrier x1, local copies, waits for them, and re-layouts, per_device(): lax.optimization_barrier((gathered, cache_pages, state))  12.8 us
    gather x1, local copies, waits for them, and re-layouts, per_device(): page_table[logical] - group_index * pages_held  12.7 us
    all_gather x1, waiting for transfers between devices, per_device(): lax.all_gather(jnp.concatenate([local_kv, weight_rows], axis=0)[None], 'g...  10.5 us
    unnamed x47, local copies, waits for them, and re-layouts  8.97 us
  transfers between devices with their start and end apart: 3, of which 2 were waited for; matrix products, arithmetic and copies ran while one was open for 17% of the time, Pallas kernels for 6%

profile of v2, /device:TPU:1, one launch (start us, length us, event | category | flops | bytes accessed | tf_op | source)
XLA Modules:
  0.0 362.5 jit_solution(15700480924699758627)
XLA Ops:
  7.2 0.7 copy.54
  8.2 0.7 and_select_fusion.8
  8.8 0.7 fusion.39
  9.7 4.4 %fusion.30 = (s32[2304]{0:T(1024)S(1)}, s32[2304,1]{0,1:T(1,128)S(1)}) fusion(s32[]{:T(128)} %bitcast.11, s32[]{:T(128)} %bitcast.12, s32[]{:T(128)} %bitcast.13, s32[]{:T(128)} %bitcast.14, s32[]{:T(128)} %bitcast.15, s32[]{:T(128)} %bitcast.17, s32[]{:T(128)} %bitcast.16, s32[2304]{0:T(1024)S(1)} %convert_reduce_fusion.1), kind=kLoop, calls=%fused_computation.105 | loop fusion | flops 34560 | bytes 27676 | tf_op jit(solution)/shard_map/gather | solution.py:174
  14.4 1.0 copy.62
  15.5 1.4 fusion.37
  18.0 6.2 %subtract_convert_fusion = (f32[2304]{0:T(1024)S(1)}, s32[2304]{0:T(1024)S(1)}) fusion(s32[]{:T(128)S(6)} %mul.82, pred[2304]{0:T(1024)(128)(4,1)S(1)} %get-tuple-element.39, pred[2304]{0:T(1024)(128)(4,1)S(1)} %get-tuple-element.38, pred[2304]{0:T(1024)(128)(4,1)S(1)} %get-tuple-element.37, pred[2304]{0:T(1024)(128)(4,1)S(1)} %get-tuple-element.36, ...), kind=kLoop, calls=%fused_computation.98 | loop fusion | flops 29952 | bytes 50732 | tf_op jit(solution)/shard_map/convert_element_type | solution.py:31
  24.2 6.4 %fusion.21 = (bf16[2304,1,48]{2,0,1:T(8,128)(2,1)S(1)}, bf16[2304,1,48]{2,0,1:T(8,128)(2,1)S(1)}, bf16[2304,48]{1,0:T(8,128)(2,1)}, bf16[2304,48]{1,0:T(8,128)(2,1)}) fusion(f32[2304,1,96]{2,0,1:T(8,128)S(1)} %get-tuple-element.104, f32[48]{0:T(128)S(1)} %multiply_power_fusion, f32[2304]{0:T(1024)S(1)} %get-tuple-element.45, ...), kind=kLoop, calls=%fused_computation.28 | loop fusion | flops 1880064 | bytes 2663616 | tf_op jit(solution)/shard_map/convert.2
  30.6 0.9 fusion.43
  31.7 1.6 copy.63
  33.4 0.9 pad_maximum_fusion
  34.9 1.5 collective-permute-start
  36.9 0.7 fusion.38
  37.7 8.9 %fusion.27 = (s32[2319]{0:T(1024)S(1)}, s32[2319]{0:T(1024)S(1)}, s32[2319,1]{0,1:T(1,128)S(1)}) fusion(s32[]{:T(128)} %bitcast.43, s32[]{:T(128)} %bitcast.44, s32[]{:T(128)} %bitcast.45, s32[]{:T(128)} %bitcast.46, s32[]{:T(128)} %bitcast.47, s32[]{:T(128)} %bitcast.49, s32[]{:T(128)} %bitcast.48, s32[]{:T(128)} %bitcast.17, s32[]{:T(128)} %bitcast.16, ...), kind=kLoop, calls=%fused_computation.100 | loop fusion | flops 48699 | bytes 37160 | tf_op jit(solution)/shard_map/gather | solution.py:189
  46.9 6.2 %select_select_fusion.1 = s32[2319]{0:T(1024)S(1)} fusion(pred[2319]{0:T(1024)(128)(4,1)S(1)} %get-tuple-element.29, pred[2319]{0:T(1024)(128)(4,1)S(1)} %get-tuple-element.28, pred[2319]{0:T(1024)(128)(4,1)S(1)} %get-tuple-element.27, pred[2319]{0:T(1024)(128)(4,1)S(1)} %get-tuple-element.26, pred[2319]{0:T(1024)(128)(4,1)S(1)} %get-tuple-element.25, ...), kind=kLoop, calls=%fused_computation.95 | loop fusion | flops 23190 | bytes 41782 | tf_op jit(solution)/shard_map/gather | solution.py:186
  53.2 6.2 %select_select_fusion = s32[2319]{0:T(1024)S(1)} fusion(pred[2319]{0:T(1024)(128)(4,1)S(1)} %get-tuple-element.29, pred[2319]{0:T(1024)(128)(4,1)S(1)} %get-tuple-element.28, pred[2319]{0:T(1024)(128)(4,1)S(1)} %get-tuple-element.27, pred[2319]{0:T(1024)(128)(4,1)S(1)} %get-tuple-element.26, pred[2319]{0:T(1024)(128)(4,1)S(1)} %get-tuple-element.25, ...), kind=kLoop, calls=%fused_computation.94 | loop fusion | flops 23190 | bytes 41782 | tf_op jit(solution)/shard_map/gather | solution.py:189
  59.5 12.7 %gather_fusion = s32[2319]{0:T(1024)S(1)} fusion(s32[1169]{0:T(1024)S(1)} %copy-done, s32[3072]{0:T(1024)S(1)} %pad_clamp_fusion), kind=kCustom, calls=%fused_computation | custom fusion | bytes 27828 | tf_op jit(solution)/shard_map/gather | solution.py:193
  74.2 1.9 fusion.42.kv_ref
  77.8 20.0 %shard_map.68 = (f32[2304,1]{1,0:T(8,128)S(1)}, f32[2304,1]{1,0:T(8,128)S(1)}, f32[2304,96]{1,0:T(8,128)S(1)}) custom-call(s32[72]{0:T(128)S(1)} %reshape.480.table_ref, bf16[2304,96]{1,0:T(8,128)(2,1)S(1)} %pad_maximum_fusion.1.q_ref, s32[2304,1]{1,0:T(8,128)S(1)} %reshape.693.lo_ref, bf16[1,2304,192]{2,1,0:T(8,128)(2,1)} %fusion.42.kv_ref), custom_call_target="tpu_custom_call" | custom-call | tf_op jit(solution)/shard_map/pallas_call | solution.py:139
  97.8 1.0 copy-done.1
  98.8 1.0 copy-done.3
  99.8 16.0 %scatter_custom_fusion = bf16[2576,192]{1,0:T(8,128)(2,1)} fusion(s32[2319]{0:T(1024)} %broadcast_select_fusion, bf16[15,1,192]{2,0,1:T(8,128)(2,1)} %collective-permute-done, bf16[]{:T(256)} %constant.217, bf16[2304,1,96]{2,0,1:T(8,128)(2,1)S(1)} %bitcast.78, bf16[2304,1,48]{2,0,1:T(8,128)(2,1)} %copy-done.6, bf16[2304,1,48]{2,0,1:T(8,128)(2,1)} %copy-done.5, ...), kind=kCustom, calls=%fused_computation.16 | custom fusion | flops 3561984 | bytes 2620416
  115.9 10.5 %all-gather.7.cloned.1.call-done = bf16[8,2496,192]{1,2,0:T(8,128)(2,1)} async-done(((bf16[1,2496,192]{1,2,0:T(8,128)(2,1)}), bf16[8,2496,192]{1,2,0:T(8,128)(2,1)}) %all-gather.7.cloned.1.call-update) | async-done | bytes 7667728 | tf_op jit(solution)/shard_map/all_gather | solution.py:170
  126.3 12.8 %copy.71.kv_ref = bf16[8,2496,192]{2,1,0:T(8,128)(2,1)} copy(bf16[8,2496,192]{1,2,0:T(8,128)(2,1)} %all-gather.7.cloned.1.call-done) | data formatting | bytes 15335424 | tf_op jit(solution)/shard_map/optimization_barrier | solution.py:197
  139.1 1.3 copy-done.2
  140.4 1.3 copy-done.4
  141.7 6.7 %shard_map.69 = bf16[2304,96]{1,0:T(8,128)(2,1)S(1)} custom-call(s32[72]{0:T(128)S(1)} %reshape.473.table_ref, bf16[2304,96]{1,0:T(8,128)(2,1)S(1)} %pad_maximum_fusion.1.q_ref, s32[2304,1]{1,0:T(8,128)S(1)} %reshape.693.lo_ref, bf16[8,2496,192]{2,1,0:T(8,128)(2,1)} %copy.71.kv_ref, f32[2304,1]{1,0:T(8,128)S(1)} %get-tuple-element.14.rest_0_, ...), custom_call_target="tpu_custom_call" | custom-call | tf_op jit(solution)/shard_map/pallas_call | solution.py:139
  148.4 1.0 copy.72
  149.4 1.1 slice-done
  151.9 2.5 reshape.482
  154.4 193.0 %all-gather.5.cloned.1.call-done = bf16[2304,3072]{0,1:T(8,128)(2,1)} async-done(((bf16[2304,96]{0,1:T(8,128)(2,1)}), bf16[2304,3072]{0,1:T(8,128)(2,1)}) %all-gather.5.cloned.1.call-update) | async-done | bytes 14155792 | tf_op jit(solution)/shard_map/all_gather | solution.py:202
  347.4 8.2 %fusion = bf16[2304,96]{0,1:T(8,128)(2,1)} fusion(bf16[2304,3072]{0,1:T(8,128)(2,1)} %all-gather.5.cloned.1.call-done, bf16[3072,96]{1,0:T(8,128)(2,1)S(1)} %reshape.481, bf16[2304,96]{0,1:T(8,128)(2,1)S(1)} %copy-done.20), kind=kOutput, calls=%fused_computation.3 | convolution fusion | flops 1359618048 | bytes 15630336 | tf_op jit(solution)/shard_map/dot_general | solution.py:201
  (95 shorter events, 8.5 us)
Async XLA Ops:
  7.2 52.3 %copy-start = (s32[1169]{0:T(1024)S(1)}, s32[1169]{0:T(1024)}, u32[]{:S(2)}) copy-start(s32[1169]{0:T(1024)} %param.6) | copy-start | bytes 14032
  7.2 119.2 %all-gather.7.cloned.1.call-start = ((), (), s32[]{:S(2)}) async-start(), calls=%async_computation.1 | async-start | bytes 8847360 | tf_op jit(solution)/shard_map/all_gather | solution.py:170
  24.2 12.3 %copy-start.10 = (s32[2304]{0:T(1024)}, s32[2304]{0:T(1024)S(1)}, u32[]{:S(2)}) copy-start(s32[2304]{0:T(1024)S(1)} %get-tuple-element.46) | copy-start | bytes 27652
  30.6 43.6 %copy-start.5 = (bf16[2304,1,48]{2,0,1:T(8,128)(2,1)}, bf16[2304,1,48]{2,0,1:T(8,128)(2,1)S(1)}, u32[]{:S(2)}) copy-start(bf16[2304,1,48]{2,0,1:T(8,128)(2,1)S(1)} %get-tuple-element.56) | copy-start | bytes 663556
  30.6 43.6 %copy-start.6 = (bf16[2304,1,48]{2,0,1:T(8,128)(2,1)}, bf16[2304,1,48]{2,0,1:T(8,128)(2,1)S(1)}, u32[]{:S(2)}) copy-start(bf16[2304,1,48]{2,0,1:T(8,128)(2,1)S(1)} %get-tuple-element.57) | copy-start | bytes 663556
  33.4 314.0 %all-gather.5.cloned.1.call-start = ((), (), s32[]{:S(2)}) async-start(), calls=%async_computation | async-start | bytes 14598144 | tf_op jit(solution)/shard_map/all_gather | solution.py:202
  34.9 64.9 %collective-permute-start = (bf16[15,1,192]{2,0,1:T(8,128)(2,1)}, bf16[15,1,192]{2,0,1:T(8,128)(2,1)}, u32[]{:S(2)}, u32[]{:S(2)}) collective-permute-start(bf16[15,1,192]{2,0,1:T(8,128)(2,1)} %slice.107), channel_id=1, source_target_pairs={{32,0},{64,32},{96,64},{128,96},{160,128},{192,160},{224,192},{33,... | collective-permute-start | bytes 17288 | tf_op jit(solution)/shard_map/ppermute | solution.py:21
  59.5 12.9 %copy-start.18 = (s32[2]{0:T(128)S(1)}, s32[2]{0:T(128)}, u32[]{:S(2)}) copy-start(s32[2]{0:T(128)} %constant.132) | copy-start | bytes 28
  59.5 13.0 %copy-start.19 = (s32[2]{0:T(128)S(1)}, s32[2]{0:T(128)}, u32[]{:S(2)}) copy-start(s32[2]{0:T(128)} %constant.135) | copy-start | bytes 28
  59.5 14.4 %copy-start.8 = (bf16[2304,48]{1,0:T(8,128)(2,1)S(1)}, bf16[2304,48]{1,0:T(8,128)(2,1)}, u32[]{:S(2)}) copy-start(bf16[2304,48]{1,0:T(8,128)(2,1)} %get-tuple-element.60) | copy-start | bytes 663556
  59.5 14.4 %copy-start.9 = (bf16[2304,48]{1,0:T(8,128)(2,1)S(1)}, bf16[2304,48]{1,0:T(8,128)(2,1)}, u32[]{:S(2)}) copy-start(bf16[2304,48]{1,0:T(8,128)(2,1)} %get-tuple-element.61) | copy-start | bytes 663556
  74.2 1.9 copy-start.11
  76.1 0.6 copy-start.17
  76.1 0.7 copy-start.16
  76.1 0.8 copy-start.15
  76.1 0.9 copy-start.14
  76.1 1.2 copy-start.13
  76.1 1.2 copy-start.12
  97.8 1.0 copy-start.1
  98.8 1.0 copy-start.3
  139.1 1.3 copy-start.2
  140.4 1.3 copy-start.4
  149.4 1.1 slice-start
  150.6 1.3 copy-start.7
  151.9 195.5 %copy-start.20 = (bf16[2304,96]{0,1:T(8,128)(2,1)S(1)}, bf16[2304,96]{0,1:T(8,128)(2,1)}, u32[]{:S(2)}) copy-start(bf16[2304,96]{0,1:T(8,128)(2,1)} %param.8) | copy-start | bytes 1327108
Sparse Core Ops, SparseCore 0:
  33.5 92.7 all-gather.6
  149.6 197.8 all-gather.4

commit v3 on v2

--- a/solution.py
+++ b/solution.py
@@ -12,6 +12,7 @@
 PAGE = 16
 BQ = 256
 BK = 768
+CHUNK_BLOCKS = 3
 NEG = -1e30
 
 
@@ -62,9 +63,9 @@
         start = pl.multiple_of(kb * BK, BK)
         source = kb // per_source
         within = pl.multiple_of((kb % per_source) * BK, BK)
-        keys = kv_ref[source, pl.ds(within, BK), pl.ds(0, HD)]
-        vals = kv_ref[source, pl.ds(within, BK), pl.ds(HD, HD)]
-        s = lax.dot_general(q, keys, (((1,), (1,)), ((), ())), preferred_element_type=jnp.float32) * scale
+        keys = kv_ref[source, pl.ds(0, HD), pl.ds(within, BK)]
+        vals = kv_ref[source, pl.ds(HD, HD), pl.ds(within, BK)]
+        s = jnp.dot(q, keys, preferred_element_type=jnp.float32) * scale
         if masked:
             k_index = key_offset + start + lax.broadcasted_iota(jnp.int32, (1, BK), 1)
             visible = (k_index >= lo) & (k_index <= q_index)
@@ -75,7 +76,9 @@
             p = jnp.where(visible, p, 0.0)
         alpha = jnp.exp(m - m_new)
         l_new = l * alpha + jnp.sum(p, axis=1, keepdims=True)
-        acc_new = acc * alpha + jnp.dot(p.astype(jnp.bfloat16), vals, preferred_element_type=jnp.float32)
+        acc_new = acc * alpha + lax.dot_general(
+            p.astype(jnp.bfloat16), vals, (((1,), (1,)), ((), ())), preferred_element_type=jnp.float32
+        )
         return (m_new, l_new, acc_new)
 
     if has_init:
@@ -116,7 +119,7 @@
     return table.reshape(-1).astype(jnp.int32)
 
 
-def attend(table, queries, lows, kv, state, finalize):
+def attend(table, queries, lows, kv, state, finalize, source_rows):
     rows = queries.shape[0]
     grid = (rows // BQ,)
     row_spec = lambda width: pl.BlockSpec((BQ, width), lambda i, t: (i, 0))
@@ -135,7 +138,7 @@
             jax.ShapeDtypeStruct((rows, HD), jnp.float32),
         )
         out_specs = (row_spec(1), row_spec(1), row_spec(HD))
-    kernel = partial(attention_kernel, has_init=state is not None, finalize=finalize, per_source=rows // BK)
+    kernel = partial(attention_kernel, has_init=state is not None, finalize=finalize, per_source=source_rows // BK)
     return pl.pallas_call(
         kernel,
         grid_spec=pltpu.PrefetchScalarGridSpec(
@@ -167,7 +170,9 @@
     queries = rotated_queries.reshape(row_count, HD)
     local_kv = key_value.reshape(row_count, 2 * HD)
     weight_rows = out_weight.reshape(-1, 2 * HD)
-    gathered = lax.all_gather(jnp.concatenate([local_kv, weight_rows], axis=0)[None], "gx", axis=0, tiled=True)
+    stacked_rows = row_count + weight_rows.shape[0]
+    gathered = lax.all_gather(jnp.concatenate([local_kv, weight_rows], axis=0), "gx", axis=0, tiled=True)
+    gathered = gathered.reshape(group_size, stacked_rows, 2 * HD)
     weight_columns = gathered[:, row_count:].reshape(-1, out_weight.shape[1])
     key_count = group_size * row_count
 
@@ -177,7 +182,7 @@
     lo_last = lows[BQ - 1 :: BQ]
     lows = lows.reshape(row_count, 1)
     own_table = block_table(q_first_rows, lo_first, lo_last, first_row, row_count)
-    state = attend(own_table, queries, lows, local_kv[None], None, False)
+    state = attend(own_table, queries, lows, local_kv.T[None], None, False, row_count)
 
     tail_rows = passed_along(key_value[: PAGE - 1], "gx", -1)
     extended = jnp.concatenate([key_value, tail_rows], axis=0)
@@ -194,15 +199,24 @@
     cache_pages = jnp.zeros((pages_held, local_heads, PAGE, 2 * HD), jnp.bfloat16)
     cache_pages = cache_pages.at[target, :, extended_position % PAGE].set(extended, mode="drop")
 
-    gathered, cache_pages, state = lax.optimization_barrier((gathered, cache_pages, state))
+    key_columns = jnp.swapaxes(gathered, 1, 2)
+    key_columns, cache_pages, state = lax.optimization_barrier((key_columns, cache_pages, state))
     rest_table = block_table(q_first_rows, lo_first, lo_last, jnp.int32(0), jnp.minimum(first_row, key_count))
-    attended = attend(rest_table, queries, lows, gathered, state, True)
-
-    update = jnp.dot(
-        lax.all_gather(attended, "gy", axis=1, tiled=True),
-        weight_columns,
-        preferred_element_type=jnp.float32,
-    )
+    chunk_rows = CHUNK_BLOCKS * BQ
+    updates = []
+    for chunk in range(row_count // chunk_rows):
+        rows = slice(chunk * chunk_rows, (chunk + 1) * chunk_rows)
+        table_part = rest_table[chunk * CHUNK_BLOCKS * 8 : (chunk + 1) * CHUNK_BLOCKS * 8]
+        state_part = tuple(piece[rows] for piece in state)
+        attended = attend(table_part, queries[rows], lows[rows], key_columns, state_part, True, row_count)
+        updates.append(
+            jnp.dot(
+                lax.all_gather(attended, "gy", axis=1, tiled=True),
+                weight_columns,
+                preferred_element_type=jnp.float32,
+            )
+        )
+    update = jnp.concatenate(updates, axis=0)
     hidden = (residual.astype(jnp.float32) + update).astype(jnp.bfloat16)
     return (hidden, cache_pages.reshape(pages_held, local_heads, PAGE * 2 * HD))
 

time: 363 us -> 350 us (0.964)
  other arithmetic: 62.2 us -> 45.3 us
  local copies, waits for them, and re-layouts: 45.8 us -> 56.5 us
  waiting for transfers between devices: 204 us -> 198 us
    unnamed x5 -> x4, other arithmetic: 17.1 us -> 1.84 us
    all_gather x1 -> x3, waiting for transfers between devices: 193 us -> 179 us  [per_device(): lax.all_gather(attended, 'gy', axis=1, tiled=True)]
    unnamed x47 -> x48, local copies, waits for them, and re-layouts: 8.97 us -> 22.6 us
    optimization_barrier x1 -> x0, local copies, waits for them, and re-layouts: 12.8 us -> none  [per_device(): lax.optimization_barrier((gathered, cache_pages, state))]
    all_gather x1, waiting for transfers between devices: 10.5 us -> 18.9 us  [per_device(): lax.all_gather(jnp.concatenate([local_kv, weight_rows], axis=0), 'gx', ax...]
    slice x0 -> x11, local copies, waits for them, and re-layouts: none -> 4.17 us  [the longest x4 1.76 us: per_device(): lows[rows]]
    pallas_call x2 -> x4, Pallas kernels: 26.7 us -> 24.8 us  [attend(): pl.pallas_call(kernel, grid_spec=pltpu.PrefetchScalarGridSpec(num_scalar_...]
    another operation x6 -> x5, other arithmetic: 8.58 us -> 6.67 us
  transfers between devices with their start and end apart: 3 -> 5, of which waited for: 2 -> 4; matrix products, arithmetic and copies ran while one was open for 17% -> 20% of each run, Pallas kernels for 6% -> 6%
where the time goes in v3:
time: 350 us
  waiting for transfers between devices  198 us (57%)
  local copies, waits for them, and re-layouts  56.5 us (16%)
  other arithmetic  45.3 us (13%)
  Pallas kernels  24.8 us (7%)
  between operations  14.3 us (4%)
  matrix products  9.82 us (3%)
    all_gather x3, waiting for transfers between devices, per_device(): lax.all_gather(attended, 'gy', axis=1, tiled=True)  179 us
    pallas_call x4, Pallas kernels, attend(): pl.pallas_call(kernel, grid_spec=pltpu.PrefetchScalarGridSpec(num_scalar_...  24.8 us
    unnamed x48, local copies, waits for them, and re-layouts  22.6 us
    all_gather x1, waiting for transfers between devices, per_device(): lax.all_gather(jnp.concatenate([local_kv, weight_rows], axis=0), 'gx', ax...  18.9 us
    gather x2, other arithmetic, per_device(): logical = page_base[extended_segment] + extended_position // PAGE  15.1 us
    gather x1, local copies, waits for them, and re-layouts, per_device(): page_table[logical] - group_index * pages_held  12.7 us
    dot_general x3, matrix products, per_device(): jnp.dot(lax.all_gather(attended, 'gy', axis=1, tiled=True), weight_column...  9.82 us
  transfers between devices with their start and end apart: 5, of which 4 were waited for; matrix products, arithmetic and copies ran while one was open for 20% of the time, Pallas kernels for 6%

profile of v3, /device:TPU:1, one launch (start us, length us, event | category | flops | bytes accessed | tf_op | source)
XLA Modules:
  0.0 350.0 jit_solution(1653171784355528233)
XLA Ops:
  9.7 4.2 %fusion.27 = (s32[2304]{0:T(1024)S(1)}, s32[2304,1]{0,1:T(1,128)S(1)}) fusion(s32[]{:T(128)} %bitcast.11, s32[]{:T(128)} %bitcast.12, s32[]{:T(128)} %bitcast.13, s32[]{:T(128)} %bitcast.14, s32[]{:T(128)} %bitcast.15, s32[]{:T(128)} %bitcast.17, s32[]{:T(128)} %bitcast.16, s32[2304]{0:T(1024)S(1)} %convert_reduce_fusion.1), kind=kLoop, calls=%fused_computation.108 | loop fusion | flops 34560 | bytes 27676 | tf_op jit(solution)/shard_map/gather | solution.py:179
  15.4 1.4 fusion.36
  17.6 6.1 %subtract_convert_fusion = (f32[2304]{0:T(1024)S(1)}, s32[2304]{0:T(1024)S(1)}) fusion(s32[]{:T(128)S(6)} %mul.82, pred[2304]{0:T(1024)(128)(4,1)S(1)} %get-tuple-element.39, pred[2304]{0:T(1024)(128)(4,1)S(1)} %get-tuple-element.38, pred[2304]{0:T(1024)(128)(4,1)S(1)} %get-tuple-element.37, pred[2304]{0:T(1024)(128)(4,1)S(1)} %get-tuple-element.36, ...), kind=kLoop, calls=%fused_computation.101 | loop fusion | flops 29952 | bytes 50732 | tf_op jit(solution)/shard_map/convert_element_type | solution.py:32
  23.7 6.4 %fusion.13 = (bf16[2304,1,48]{2,0,1:T(8,128)(2,1)}, bf16[2304,1,48]{2,0,1:T(8,128)(2,1)S(1)}, bf16[2304,1,48]{2,0,1:T(8,128)(2,1)S(1)}, bf16[2304,1,48]{2,0,1:T(8,128)(2,1)S(1)}) fusion(f32[2304,1,96]{2,0,1:T(8,128)S(1)} %get-tuple-element.125, f32[2304]{0:T(1024)S(1)} %get-tuple-element.45, f32[48]{0:T(128)S(1)} %multiply_power_fusion, ...), kind=kLoop, calls=%fused_computation.17 | loop fusion | flops 1880064 | bytes 2663616 | tf_op jit(solution)/shard_map/convert.6
  30.0 1.3 copy.122
  31.6 1.2 fusion.32
  32.8 1.0 maximum_bitcast_fusion
  34.7 1.3 collective-permute-start
  37.7 8.8 %fusion.24 = (s32[2319]{0:T(1024)S(1)}, s32[2319]{0:T(1024)S(1)}, s32[2319,1]{0,1:T(1,128)S(1)}) fusion(s32[]{:T(128)} %bitcast.43, s32[]{:T(128)} %bitcast.44, s32[]{:T(128)} %bitcast.45, s32[]{:T(128)} %bitcast.46, s32[]{:T(128)} %bitcast.47, s32[]{:T(128)} %bitcast.49, s32[]{:T(128)} %bitcast.48, s32[]{:T(128)} %bitcast.17, s32[]{:T(128)} %bitcast.16, ...), kind=kLoop, calls=%fused_computation.103 | loop fusion | flops 48699 | bytes 37160 | tf_op jit(solution)/shard_map/gather | solution.py:194
  46.7 6.1 %select_select_fusion.1 = s32[2319]{0:T(1024)S(1)} fusion(pred[2319]{0:T(1024)(128)(4,1)S(1)} %get-tuple-element.29, pred[2319]{0:T(1024)(128)(4,1)S(1)} %get-tuple-element.28, pred[2319]{0:T(1024)(128)(4,1)S(1)} %get-tuple-element.27, pred[2319]{0:T(1024)(128)(4,1)S(1)} %get-tuple-element.26, pred[2319]{0:T(1024)(128)(4,1)S(1)} %get-tuple-element.25, ...), kind=kLoop, calls=%fused_computation.98 | loop fusion | flops 23190 | bytes 41782 | tf_op jit(solution)/shard_map/gather | solution.py:191
  52.8 6.3 %select_select_fusion = s32[2319]{0:T(1024)S(1)} fusion(pred[2319]{0:T(1024)(128)(4,1)S(1)} %get-tuple-element.29, pred[2319]{0:T(1024)(128)(4,1)S(1)} %get-tuple-element.28, pred[2319]{0:T(1024)(128)(4,1)S(1)} %get-tuple-element.27, pred[2319]{0:T(1024)(128)(4,1)S(1)} %get-tuple-element.26, pred[2319]{0:T(1024)(128)(4,1)S(1)} %get-tuple-element.25, ...), kind=kLoop, calls=%fused_computation.97 | loop fusion | flops 23190 | bytes 41782 | tf_op jit(solution)/shard_map/gather | solution.py:194
  59.3 12.7 %gather_fusion = s32[2319]{0:T(1024)S(1)} fusion(s32[1169]{0:T(1024)S(1)} %copy-done, s32[3072]{0:T(1024)S(1)} %pad_clamp_fusion), kind=kCustom, calls=%fused_computation | custom fusion | bytes 27828 | tf_op jit(solution)/shard_map/gather | solution.py:198
  77.5 11.1 %shard_map.68 = (f32[2304,1]{1,0:T(8,128)S(1)}, f32[2304,1]{1,0:T(8,128)S(1)}, f32[2304,96]{1,0:T(8,128)S(1)}) custom-call(s32[72]{0:T(128)S(1)} %reshape.508.table_ref, bf16[2304,96]{1,0:T(8,128)(2,1)S(1)} %pad_maximum_fusion.1.q_ref, s32[2304,1]{1,0:T(8,128)S(1)} %reshape.721.lo_ref, bf16[1,192,2304]{2,1,0:T(8,128)(2,1)S(1)} %get-tuple-element.72.kv_ref), custom_call_target="tpu_custom_call" | custom-call | tf_op jit(solution)/shard_map/pallas_call | solution.py:142
  88.7 1.0 copy-done.1
  90.7 1.0 copy-done.5
  91.9 1.6 copy.127
  93.4 14.4 %scatter_custom_fusion = bf16[2576,192]{1,0:T(8,128)(2,1)} fusion(s32[2319]{0:T(1024)} %broadcast_select_fusion, bf16[2319,192]{1,0:T(8,128)(2,1)} %copy.127, bf16[]{:T(256)} %constant.126.clone.1), kind=kCustom, calls=%fused_computation.25 | custom fusion | bytes 989696
  107.8 18.9 %all-gather.12.cloned.1.call-done = bf16[8,2496,192]{1,2,0:T(8,128)(2,1)} async-done(((bf16[1,2496,192]{1,2,0:T(8,128)(2,1)}), bf16[8,2496,192]{1,2,0:T(8,128)(2,1)}) %all-gather.12.cloned.1.call-update) | async-done | bytes 7667728 | tf_op jit(solution)/shard_map/all_gather | solution.py:174
  126.7 1.4 fusion.39
  128.4 1.2 copy-done.2
  130.5 4.5 %shard_map.71 = bf16[768,96]{1,0:T(8,128)(2,1)S(1)} custom-call(s32[24]{0:T(128)S(1)} %slice.144.table_ref, bf16[768,96]{1,0:T(8,128)(2,1)S(1)} %copy-done.6, s32[768,1]{1,0:T(8,128)S(1)} %slice.208.lo_ref, bf16[8,192,2496]{2,1,0:T(8,128)(2,1)} %bitcast.87, f32[768,1]{1,0:T(8,128)S(1)} %get-tuple-element.67.rest_0_, f32[768,1]{1,0:T(8,128)S(1)} %get-tuple-element.64.rest_1_, ...), custom_call_target="tpu_custom_call" | custom-call | tf_op jit(solution)/shard_map/pallas_call | solution.py:142
  135.8 1.7 copy.139
  137.8 4.5 %shard_map.69 = bf16[768,96]{1,0:T(8,128)(2,1)S(1)} custom-call(s32[24]{0:T(128)S(1)} %slice.117.table_ref, bf16[768,96]{1,0:T(8,128)(2,1)S(1)} %get-tuple-element.69.q_ref, s32[768,1]{1,0:T(8,128)S(1)} %slice.206.lo_ref, bf16[8,192,2496]{2,1,0:T(8,128)(2,1)} %bitcast.88, f32[768,1]{1,0:T(8,128)S(1)} %get-tuple-element.66.rest_0_, ...), custom_call_target="tpu_custom_call" | custom-call | tf_op jit(solution)/shard_map/pallas_call | solution.py:142
  143.5 4.5 %shard_map.70 = bf16[768,96]{1,0:T(8,128)(2,1)S(1)} custom-call(s32[24]{0:T(128)S(1)} %slice.135.table_ref, bf16[768,96]{1,0:T(8,128)(2,1)S(1)} %get-tuple-element.71.q_ref, s32[768,1]{1,0:T(8,128)S(1)} %slice.207.lo_ref, bf16[8,192,2496]{2,1,0:T(8,128)(2,1)} %bitcast.89, f32[768,1]{1,0:T(8,128)S(1)} %get-tuple-element.68.rest_0_, ...), custom_call_target="tpu_custom_call" | custom-call | tf_op jit(solution)/shard_map/pallas_call | solution.py:142
  148.9 1.2 slice.223
  151.4 2.5 reshape.511
  153.9 77.8 %all-gather.10.cloned.1.call-done = bf16[768,3072]{0,1:T(8,128)(2,1)} async-done(((bf16[768,96]{0,1:T(8,128)(2,1)}), bf16[768,3072]{0,1:T(8,128)(2,1)}) %all-gather.10.cloned.1.call-update) | async-done | bytes 4718608 | tf_op jit(solution)/shard_map/all_gather | solution.py:214
  231.6 3.3 fusion.46
  234.9 50.4 %all-gather.6.cloned.1.call-done = bf16[768,3072]{0,1:T(8,128)(2,1)} async-done(((bf16[768,96]{0,1:T(8,128)(2,1)}), bf16[768,3072]{0,1:T(8,128)(2,1)}) %all-gather.6.cloned.1.call-update) | async-done | bytes 4718608 | tf_op jit(solution)/shard_map/all_gather | solution.py:214
  285.3 3.3 fusion.44
  288.6 50.8 %all-gather.8.cloned.1.call-done = bf16[768,3072]{0,1:T(8,128)(2,1)} async-done(((bf16[768,96]{0,1:T(8,128)(2,1)}), bf16[768,3072]{0,1:T(8,128)(2,1)}) %all-gather.8.cloned.1.call-update) | async-done | bytes 4718608 | tf_op jit(solution)/shard_map/all_gather | solution.py:214
  339.3 3.3 fusion.45
  (120 shorter events, 20.7 us)
Async XLA Ops:
  7.2 52.1 %copy-start = (s32[1169]{0:T(1024)S(1)}, s32[1169]{0:T(1024)}, u32[]{:S(2)}) copy-start(s32[1169]{0:T(1024)} %param.6) | copy-start | bytes 14032
  7.2 119.5 %all-gather.12.cloned.1.call-start = ((), (), s32[]{:S(2)}) async-start(), calls=%async_computation.3 | async-start | bytes 8847360 | tf_op jit(solution)/shard_map/all_gather | solution.py:174
  16.8 14.8 %copy-start.9 = (bf16[2304,1,96]{0,2,1:T(8,128)(2,1)}, bf16[2304,1,96]{0,2,1:T(8,128)(2,1)S(1)}, u32[]{:S(2)}) copy-start(bf16[2304,1,96]{0,2,1:T(8,128)(2,1)S(1)} %get-tuple-element.55) | copy-start | bytes 1327108
  31.3 1.4 copy-start.11
  31.6 1.2 copy-start.13
  33.8 197.9 %all-gather.10.cloned.1.call-start = ((), (), s32[]{:S(2)}) async-start(), calls=%async_computation.2 | async-start | bytes 4866048 | tf_op jit(solution)/shard_map/all_gather | solution.py:214
  34.7 57.1 %collective-permute-start = (bf16[15,1,192]{0,2,1:T(8,128)(2,1)S(1)}, bf16[15,1,192]{0,2,1:T(8,128)(2,1)S(1)}, u32[]{:S(2)}, u32[]{:S(2)}) collective-permute-start(bf16[15,1,192]{0,2,1:T(8,128)(2,1)S(1)} %slice.222), channel_id=1, source_target_pairs={{32,0},{64,32},{96,64},{128,96},{160,128},{192,160},{224,192},{33,... | collective-permute-start | bytes 17288 | tf_op jit(solution)/shard_map/ppermute | solution.py:22
  59.3 13.0 %copy-start.20 = (s32[2]{0:T(128)S(1)}, s32[2]{0:T(128)}, u32[]{:S(2)}) copy-start(s32[2]{0:T(128)} %constant.132) | copy-start | bytes 28
  59.3 13.1 %copy-start.21 = (s32[2]{0:T(128)S(1)}, s32[2]{0:T(128)}, u32[]{:S(2)}) copy-start(s32[2]{0:T(128)} %constant.135) | copy-start | bytes 28
  77.5 14.2 %copy-start.10 = (bf16[2304,1,96]{0,2,1:T(8,128)(2,1)S(1)}, bf16[2304,1,96]{0,2,1:T(8,128)(2,1)}, u32[]{:S(2)}) copy-start(bf16[2304,1,96]{0,2,1:T(8,128)(2,1)} %copy-done.9) | copy-start | bytes 1327108
  77.5 14.2 %copy-start.12 = (bf16[2304,1,48]{0,2,1:T(8,128)(2,1)S(1)}, bf16[2304,1,48]{0,2,1:T(8,128)(2,1)}, u32[]{:S(2)}) copy-start(bf16[2304,1,48]{0,2,1:T(8,128)(2,1)} %copy-done.11) | copy-start | bytes 663556
  77.5 14.2 %copy-start.14 = (bf16[2304,1,48]{0,2,1:T(8,128)(2,1)S(1)}, bf16[2304,1,48]{0,2,1:T(8,128)(2,1)}, u32[]{:S(2)}) copy-start(bf16[2304,1,48]{0,2,1:T(8,128)(2,1)} %copy-done.13) | copy-start | bytes 663556
  88.7 1.0 copy-start.1
  89.7 1.0 copy-start.3
  90.7 1.0 copy-start.5
  126.7 1.6 copy-start.4
  128.3 1.3 copy-start.2
  129.6 0.9 copy-start.6
  130.5 7.0 %copy-start.19 = (s32[3,8]{1,0:T(4,128)S(1)}, s32[3,8]{1,0:T(4,128)}, u32[]{:S(2)}) copy-start(s32[3,8]{1,0:T(4,128)} %get-tuple-element.82) | copy-start | bytes 292
  130.5 7.1 %copy-start.17 = (s32[768]{0:T(1024)S(1)}, s32[768]{0:T(1024)}, u32[]{:S(2)}) copy-start(s32[768]{0:T(1024)} %get-tuple-element.77) | copy-start | bytes 9220
  135.1 0.7 copy-start.7
  137.5 147.8 %all-gather.6.cloned.1.call-start = ((), (), s32[]{:S(2)}) async-start(), calls=%async_computation | async-start | bytes 4866048 | tf_op jit(solution)/shard_map/all_gather | solution.py:214
  137.8 5.4 %copy-start.18 = (s32[3,8]{1,0:T(4,128)S(1)}, s32[3,8]{1,0:T(4,128)}, u32[]{:S(2)}) copy-start(s32[3,8]{1,0:T(4,128)} %get-tuple-element.84) | copy-start | bytes 292
  137.8 5.5 %copy-start.16 = (s32[768]{0:T(1024)S(1)}, s32[768]{0:T(1024)}, u32[]{:S(2)}) copy-start(s32[768]{0:T(1024)} %get-tuple-element.78) | copy-start | bytes 9220
  143.2 196.1 %all-gather.8.cloned.1.call-start = ((), (), s32[]{:S(2)}) async-start(), calls=%async_computation.1 | async-start | bytes 4866048 | tf_op jit(solution)/shard_map/all_gather | solution.py:214
  150.1 1.3 copy-start.8
  288.6 54.1 %copy-start.15 = (bf16[2304,96]{0,1:T(8,128)(2,1)S(1)}, bf16[2304,96]{0,1:T(8,128)(2,1)}, u32[]{:S(2)}) copy-start(bf16[2304,96]{0,1:T(8,128)(2,1)} %param.8) | copy-start | bytes 1327108
Sparse Core Ops, SparseCore 0:
  33.9 92.7 all-gather.11
  137.6 93.9 all-gather.9
  234.2 51.0 all-gather.5
  288.3 51.0 all-gather.7

commit v4 on v3

--- a/solution.py
+++ b/solution.py
@@ -10,9 +10,8 @@
 
 HD = 96
 PAGE = 16
-BQ = 256
+BQ = 384
 BK = 768
-CHUNK_BLOCKS = 3
 NEG = -1e30
 
 
@@ -176,13 +175,29 @@
     weight_columns = gathered[:, row_count:].reshape(-1, out_weight.shape[1])
     key_count = group_size * row_count
 
+    half = row_count // 2
+    half_blocks = half // BQ
     lows = starts_at[own_segment]
-    q_first_rows = first_row + jnp.arange(0, row_count, BQ, dtype=jnp.int32)
-    lo_first = lows[0::BQ]
-    lo_last = lows[BQ - 1 :: BQ]
+    q_first_rows = first_row + jnp.arange(0, half, BQ, dtype=jnp.int32)
+    lo_first = lows[0:half:BQ]
+    lo_last = lows[BQ - 1 : half : BQ]
     lows = lows.reshape(row_count, 1)
     own_table = block_table(q_first_rows, lo_first, lo_last, first_row, row_count)
-    state = attend(own_table, queries, lows, local_kv.T[None], None, False, row_count)
+    state = attend(own_table, queries[:half], lows[:half], local_kv.T[None], None, False, row_count)
+
+    partners = [(i, group_size - 1 - i) for i in range(group_size)]
+    partner_queries = lax.ppermute(queries[half:], "gx", partners)
+    partner_first = (group_size - 1 - group_index) * row_count + half
+    partner_index = partner_first + jnp.arange(half, dtype=jnp.int32)
+    partner_lows = starts_at[segment_of(ends_at, partner_index)]
+    partner_table = block_table(
+        partner_first + jnp.arange(0, half, BQ, dtype=jnp.int32),
+        partner_lows[0::BQ],
+        partner_lows[BQ - 1 :: BQ],
+        jnp.int32(0),
+        key_count,
+    )
+    partner_lows = partner_lows.reshape(half, 1)
 
     tail_rows = passed_along(key_value[: PAGE - 1], "gx", -1)
     extended = jnp.concatenate([key_value, tail_rows], axis=0)
@@ -201,21 +216,18 @@
 
     key_columns = jnp.swapaxes(gathered, 1, 2)
     key_columns, cache_pages, state = lax.optimization_barrier((key_columns, cache_pages, state))
+    partner_out = attend(partner_table, partner_queries, partner_lows, key_columns, None, True, row_count)
+    second_half = lax.ppermute(partner_out, "gx", partners)
     rest_table = block_table(q_first_rows, lo_first, lo_last, jnp.int32(0), jnp.minimum(first_row, key_count))
-    chunk_rows = CHUNK_BLOCKS * BQ
-    updates = []
-    for chunk in range(row_count // chunk_rows):
-        rows = slice(chunk * chunk_rows, (chunk + 1) * chunk_rows)
-        table_part = rest_table[chunk * CHUNK_BLOCKS * 8 : (chunk + 1) * CHUNK_BLOCKS * 8]
-        state_part = tuple(piece[rows] for piece in state)
-        attended = attend(table_part, queries[rows], lows[rows], key_columns, state_part, True, row_count)
-        updates.append(
-            jnp.dot(
-                lax.all_gather(attended, "gy", axis=1, tiled=True),
-                weight_columns,
-                preferred_element_type=jnp.float32,
-            )
-        )
+    first_half = attend(rest_table, queries[:half], lows[:half], key_columns, state, True, row_count)
+    updates = [
+        jnp.dot(
+            lax.all_gather(piece, "gy", axis=1, tiled=True),
+            weight_columns,
+            preferred_element_type=jnp.float32,
+        )
+        for piece in (first_half, second_half)
+    ]
     update = jnp.concatenate(updates, axis=0)
     hidden = (residual.astype(jnp.float32) + update).astype(jnp.bfloat16)
     return (hidden, cache_pages.reshape(pages_held, local_heads, PAGE * 2 * HD))

time: 350 us -> 331 us (0.946)
  waiting for transfers between devices: 198 us -> 96.3 us
  starting transfers between devices: 1.44 us -> 62.2 us
  Pallas kernels: 24.8 us -> 42.4 us
  other arithmetic: 45.3 us -> 58.4 us
  local copies, waits for them, and re-layouts: 56.5 us -> 46.1 us
    all_gather x3 -> x2, waiting for transfers between devices: 179 us -> 62.7 us  [per_device(): lax.all_gather(piece, 'gy', axis=1, tiled=True)]
    ppermute x0 -> x2, starting transfers between devices: none -> 60.6 us  [the longest x1 60.2 us: per_device(): partner_queries = lax.ppermute(queries[half:], 'gx', partners)]
    pallas_call x4 -> x3, Pallas kernels: 24.8 us -> 42.4 us  [attend(): pl.pallas_call(kernel, grid_spec=pltpu.PrefetchScalarGridSpec(num_scalar_...]
    gather x0 -> x3, other arithmetic: none -> 10.9 us  [per_device(): partner_lows = starts_at[segment_of(ends_at, partner_index)]]
    ppermute x0 -> x2, waiting for transfers between devices: none -> 8.64 us  [the longest x1 8.64 us: per_device(): second_half = lax.ppermute(partner_out, 'gx', partners)]
    all_gather x1, waiting for transfers between devices: 18.9 us -> 24.9 us  [per_device(): lax.all_gather(jnp.concatenate([local_kv, weight_rows], axis=0), 'gx', ax...]
    unnamed x48 -> x34, local copies, waits for them, and re-layouts: 22.6 us -> 16.7 us
    slice x13 -> x6, local copies, waits for them, and re-layouts: 4.35 us -> 0.56 us  [the longest x2 0.21 us: per_device(): lows[:half]]
  transfers between devices with their start and end apart: 5 -> 6, of which waited for: 4 -> 3; matrix products, arithmetic and copies ran while one was open for 20% -> 25% of each run, Pallas kernels for 6% -> 11%
where the time goes in v4:
time: 331 us; the launch traced here: 328 us
  waiting for transfers between devices  96.3 us (29%)
  starting transfers between devices  62.2 us (19%)
  other arithmetic  58.4 us (18%)
  local copies, waits for them, and re-layouts  46.1 us (14%)
  Pallas kernels  42.4 us (13%)
  between operations  14.2 us (4%)
  matrix products  8.64 us (3%)
    all_gather x2, waiting for transfers between devices, per_device(): lax.all_gather(piece, 'gy', axis=1, tiled=True)  62.7 us
    ppermute x1, starting transfers between devices, per_device(): partner_queries = lax.ppermute(queries[half:], 'gx', partners)  60.2 us
    pallas_call x3, Pallas kernels, attend(): pl.pallas_call(kernel, grid_spec=pltpu.PrefetchScalarGridSpec(num_scalar_...  42.4 us
    all_gather x1, waiting for transfers between devices, per_device(): lax.all_gather(jnp.concatenate([local_kv, weight_rows], axis=0), 'gx', ax...  24.9 us
    unnamed x34, local copies, waits for them, and re-layouts  16.7 us
    gather x2, other arithmetic, per_device(): logical = page_base[extended_segment] + extended_position // PAGE  15.3 us
    gather x1, local copies, waits for them, and re-layouts, per_device(): page_table[logical] - group_index * pages_held  12.7 us
    gather x3, other arithmetic, per_device(): partner_lows = starts_at[segment_of(ends_at, partner_index)]  10.9 us
  transfers between devices with their start and end apart: 6, of which 3 were waited for; matrix products, arithmetic and copies ran while one was open for 25% of the time, Pallas kernels for 11%

profile of v4, /device:TPU:1, one launch (start us, length us, event | category | flops | bytes accessed | tf_op | source)
XLA Modules:
  0.0 328.4 jit_solution(14650108152945351044)
XLA Ops:
  9.7 4.4 %fusion.25 = (s32[2304]{0:T(1024)S(1)}, s32[2304,1]{0,1:T(1,128)S(1)}) fusion(s32[]{:T(128)} %bitcast.11, s32[]{:T(128)} %bitcast.12, s32[]{:T(128)} %bitcast.13, s32[]{:T(128)} %bitcast.14, s32[]{:T(128)} %bitcast.15, s32[]{:T(128)} %bitcast.17, s32[]{:T(128)} %bitcast.16, s32[2304]{0:T(1024)S(1)} %convert_reduce_fusion.1), kind=kLoop, calls=%fused_computation.121 | loop fusion | flops 34560 | bytes 27676 | tf_op jit(solution)/shard_map/gather | solution.py:180
  14.3 1.4 fusion.41
  16.5 6.4 %subtract_convert_fusion = (f32[2304]{0:T(1024)S(1)}, s32[2304]{0:T(1024)S(1)}) fusion(s32[]{:T(128)S(6)} %mul.94, pred[2304]{0:T(1024)(128)(4,1)S(1)} %get-tuple-element.39, pred[2304]{0:T(1024)(128)(4,1)S(1)} %get-tuple-element.38, pred[2304]{0:T(1024)(128)(4,1)S(1)} %get-tuple-element.37, pred[2304]{0:T(1024)(128)(4,1)S(1)} %get-tuple-element.36, ...), kind=kLoop, calls=%fused_computation.114 | loop fusion | flops 29952 | bytes 50732 | tf_op jit(solution)/shard_map/convert_element_type | solution.py:31
  22.9 5.6 %fusion.13 = (bf16[2304,1,48]{2,0,1:T(8,128)(2,1)S(1)}, bf16[2304,1,48]{2,0,1:T(8,128)(2,1)S(1)}, bf16[2304,1,48]{2,0,1:T(8,128)(2,1)S(1)}, bf16[2304,1,48]{2,0,1:T(8,128)(2,1)S(1)}) fusion(f32[2304,1,96]{2,0,1:T(8,128)S(1)} %get-tuple-element.125, f32[2304]{0:T(1024)S(1)} %get-tuple-element.59, f32[48]{0:T(128)S(1)} %multiply_power_fusion, ...), kind=kLoop, calls=%fused_computation.17 | loop fusion | flops 1880064 | bytes 2663616 | tf_op jit(solution)/shard_map/convert.2
  29.8 1.2 fusion.36
  30.9 1.0 maximum_bitcast_fusion
  32.0 1.4 slice.163
  33.4 1.5 collective-permute-start
  36.2 8.9 %fusion.22 = (s32[2319]{0:T(1024)S(1)}, s32[2319]{0:T(1024)S(1)}, s32[2319,1]{0,1:T(1,128)S(1)}) fusion(s32[]{:T(128)} %bitcast.43, s32[]{:T(128)} %bitcast.44, s32[]{:T(128)} %bitcast.45, s32[]{:T(128)} %bitcast.46, s32[]{:T(128)} %bitcast.47, s32[]{:T(128)} %bitcast.49, s32[]{:T(128)} %bitcast.48, s32[]{:T(128)} %bitcast.17, s32[]{:T(128)} %bitcast.16, ...), kind=kLoop, calls=%fused_computation.116 | loop fusion | flops 48699 | bytes 37160 | tf_op jit(solution)/shard_map/gather | solution.py:209
  45.4 6.4 %select_select_fusion.1 = s32[2319]{0:T(1024)S(1)} fusion(pred[2319]{0:T(1024)(128)(4,1)S(1)} %get-tuple-element.29, pred[2319]{0:T(1024)(128)(4,1)S(1)} %get-tuple-element.28, pred[2319]{0:T(1024)(128)(4,1)S(1)} %get-tuple-element.27, pred[2319]{0:T(1024)(128)(4,1)S(1)} %get-tuple-element.26, pred[2319]{0:T(1024)(128)(4,1)S(1)} %get-tuple-element.25, ...), kind=kLoop, calls=%fused_computation.111 | loop fusion | flops 23190 | bytes 41782 | tf_op jit(solution)/shard_map/gather | solution.py:206
  51.8 6.4 %select_select_fusion = s32[2319]{0:T(1024)S(1)} fusion(pred[2319]{0:T(1024)(128)(4,1)S(1)} %get-tuple-element.29, pred[2319]{0:T(1024)(128)(4,1)S(1)} %get-tuple-element.28, pred[2319]{0:T(1024)(128)(4,1)S(1)} %get-tuple-element.27, pred[2319]{0:T(1024)(128)(4,1)S(1)} %get-tuple-element.26, pred[2319]{0:T(1024)(128)(4,1)S(1)} %get-tuple-element.25, ...), kind=kLoop, calls=%fused_computation.110 | loop fusion | flops 23190 | bytes 41782 | tf_op jit(solution)/shard_map/gather | solution.py:209
  58.3 12.7 %gather_fusion = s32[2319]{0:T(1024)S(1)} fusion(s32[1169]{0:T(1024)S(1)} %copy-done, s32[3072]{0:T(1024)S(1)} %pad_clamp_fusion), kind=kCustom, calls=%fused_computation | custom fusion | bytes 27828 | tf_op jit(solution)/shard_map/gather | solution.py:213
  72.1 1.0 fusion.20
  75.0 5.9 %shard_map.68 = (f32[1152,1]{1,0:T(8,128)S(1)}, f32[1152,1]{1,0:T(8,128)S(1)}, f32[1152,96]{1,0:T(8,128)S(1)}) custom-call(s32[24]{0:T(128)S(1)} %reshape.526.table_ref, bf16[1152,96]{1,0:T(8,128)(2,1)S(1)} %get-tuple-element.76.q_ref, s32[1152,1]{1,0:T(8,128)S(1)} %slice.150.lo_ref, bf16[1,192,2304]{2,1,0:T(8,128)(2,1)S(1)} %get-tuple-element.78.kv_ref), custom_call_target="tpu_custom_call" | custom-call | tf_op jit(solution)/shard_map/pallas_call | solution.py:141
  80.9 2.3 maximum_bitcast_fusion.1
  83.2 2.4 copy.138
  85.6 14.4 %scatter_custom_fusion = bf16[2576,192]{1,0:T(8,128)(2,1)} fusion(s32[2319]{0:T(1024)} %broadcast_select_fusion, bf16[2319,192]{1,0:T(8,128)(2,1)} %copy.138, bf16[]{:T(256)} %constant.149.clone.1), kind=kCustom, calls=%fused_computation.25 | custom fusion | bytes 989696
  100.0 24.9 %all-gather.9.cloned.1.call-done = bf16[8,2496,192]{1,2,0:T(8,128)(2,1)} async-done(((bf16[1,2496,192]{1,2,0:T(8,128)(2,1)}), bf16[8,2496,192]{1,2,0:T(8,128)(2,1)}) %all-gather.9.cloned.1.call-update) | async-done | bytes 7667728 | tf_op jit(solution)/shard_map/all_gather | solution.py:173
  124.9 4.9 %shard_map.69 = bf16[1152,96]{1,0:T(8,128)(2,1)S(1)} custom-call(s32[24]{0:T(128)S(1)} %reshape.519.table_ref, bf16[1152,96]{1,0:T(8,128)(2,1)S(1)} %get-tuple-element.76.q_ref, s32[1152,1]{1,0:T(8,128)S(1)} %slice.150.lo_ref, bf16[8,192,2496]{2,1,0:T(8,128)(2,1)} %bitcast.85, f32[1152,1]{1,0:T(8,128)S(1)} %get-tuple-element.14.rest_0_, ...), custom_call_target="tpu_custom_call" | custom-call | tf_op jit(solution)/shard_map/pallas_call | solution.py:141
  129.8 0.9 copy.145
  130.7 60.2 %collective-permute-start.1 = (bf16[1152,96]{1,0:T(8,128)(2,1)}, bf16[1152,96]{1,0:T(8,128)(2,1)S(1)}, u32[]{:S(2)}, u32[]{:S(2)}) collective-permute-start(bf16[1152,96]{1,0:T(8,128)(2,1)} %get-tuple-element.77), channel_id=1, source_target_pairs={{0,224},{32,192},{64,160},{96,128},{128,96},{160,64},{192,32},{224... | collective-permute-start | bytes 663560 | tf_op jit(solution)/shard_map/ppermute | solution.py:189
  191.1 4.4 %fusion.26 = (s32[1152]{0:T(1024)S(1)}, s32[1152,1]{0,1:T(1,128)S(1)}) fusion(s32[]{:T(128)} %bitcast.11, s32[]{:T(128)} %bitcast.12, s32[]{:T(128)} %bitcast.13, s32[]{:T(128)} %bitcast.14, s32[]{:T(128)} %bitcast.15, s32[]{:T(128)} %bitcast.17, s32[]{:T(128)} %bitcast.16, s32[1152]{0:T(1024)S(1)} %convert_reduce_fusion.2), kind=kLoop, calls=%fused_computation.127 | loop fusion | flops 17280 | bytes 13852 | tf_op jit(solution)/shard_map/gather | solution.py:192
  195.6 6.4 %select_select_fusion.3 = s32[1152]{0:T(1024)S(1)} fusion(pred[1152]{0:T(1024)(128)(4,1)S(1)} %get-tuple-element.49, pred[1152]{0:T(1024)(128)(4,1)S(1)} %get-tuple-element.48, pred[1152]{0:T(1024)(128)(4,1)S(1)} %get-tuple-element.47, pred[1152]{0:T(1024)(128)(4,1)S(1)} %get-tuple-element.46, pred[1152]{0:T(1024)(128)(4,1)S(1)} %get-tuple-element.45, ...), kind=kLoop, calls=%fused_computation.122 | loop fusion | flops 11520 | bytes 20776 | tf_op jit(solution)/shard_map/gather | solution.py:192
  203.0 31.7 %shard_map.70 = bf16[1152,96]{1,0:T(8,128)(2,1)S(1)} custom-call(s32[24]{0:T(128)S(1)} %reshape.528.table_ref, bf16[1152,96]{1,0:T(8,128)(2,1)S(1)} %collective-permute-done.1.q_ref, s32[1152,1]{1,0:T(8,128)S(1)} %reshape.811.lo_ref, bf16[8,192,2496]{2,1,0:T(8,128)(2,1)} %bitcast.86), custom_call_target="tpu_custom_call" | custom-call | tf_op jit(solution)/shard_map/pallas_call | solution.py:141
  235.1 8.6 %collective-permute-done.2 = bf16[1152,96]{1,0:T(8,128)(2,1)S(1)} collective-permute-done((bf16[1152,96]{1,0:T(8,128)(2,1)S(1)}, bf16[1152,96]{1,0:T(8,128)(2,1)S(1)}, u32[]{:S(2)}, u32[]{:S(2)}) %collective-permute-start.2) | collective-permute-done | bytes 221216 | tf_op jit(solution)/shard_map/ppermute | solution.py:220
  243.7 0.9 copy.152
  244.6 1.2 slice.164
  247.1 2.5 reshape.530
  249.6 4.3 %fusion.44 = f32[1152,96]{0,1:T(8,128)S(1)} fusion(bf16[1152,3072]{0,1:T(8,128)(2,1)} %all-gather.5.cloned.1.call-done, bf16[3072,96]{1,0:T(8,128)(2,1)S(1)} %reshape.527), kind=kOutput, calls=%fused_computation.167 | convolution fusion | flops 679477248 | bytes 8110080 | tf_op jit(solution)/shard_map/dot_general | solution.py:224
  254.0 62.7 %all-gather.7.cloned.1.call-done = bf16[1152,3072]{0,1:T(8,128)(2,1)} async-done(((bf16[1152,96]{0,1:T(8,128)(2,1)}), bf16[1152,3072]{0,1:T(8,128)(2,1)}) %all-gather.7.cloned.1.call-update) | async-done | bytes 7077904 | tf_op jit(solution)/shard_map/all_gather | solution.py:225
  316.7 4.3 %fusion.45 = f32[1152,96]{0,1:T(8,128)S(1)} fusion(bf16[1152,3072]{0,1:T(8,128)(2,1)} %all-gather.7.cloned.1.call-done, bf16[3072,96]{1,0:T(8,128)(2,1)S(1)} %reshape.527), kind=kOutput, calls=%fused_computation.168 | convolution fusion | flops 679477248 | bytes 8110080 | tf_op jit(solution)/shard_map/dot_general | solution.py:224
  321.0 0.8 fusion.16
  (110 shorter events, 12.2 us)
Async XLA Ops:
  7.2 51.1 %copy-start = (s32[1169]{0:T(1024)S(1)}, s32[1169]{0:T(1024)}, u32[]{:S(2)}) copy-start(s32[1169]{0:T(1024)} %param.6) | copy-start | bytes 14032
  7.2 117.7 %all-gather.9.cloned.1.call-start = ((), (), s32[]{:S(2)}) async-start(), calls=%async_computation.2 | async-start | bytes 8847360 | tf_op jit(solution)/shard_map/all_gather | solution.py:173
  8.1 27.9 %copy-start.11 = (s32[17]{0:T(128)}, s32[17]{0:T(128)S(1)}, u32[]{:S(2)}) copy-start(s32[17]{0:T(128)S(1)} %reduce.2) | copy-start | bytes 208
  15.7 14.0 %copy-start.2 = (bf16[2304,1,96]{0,2,1:T(8,128)(2,1)}, bf16[2304,1,96]{0,2,1:T(8,128)(2,1)S(1)}, u32[]{:S(2)}) copy-start(bf16[2304,1,96]{0,2,1:T(8,128)(2,1)S(1)} %get-tuple-element.71) | copy-start | bytes 1327108
  28.5 0.9 copy-start.6
  28.8 4.7 %copy-start.3 = (bf16[2304,1,48]{0,2,1:T(8,128)(2,1)}, bf16[2304,1,48]{0,2,1:T(8,128)(2,1)S(1)}, u32[]{:S(2)}) copy-start(bf16[2304,1,48]{0,2,1:T(8,128)(2,1)S(1)} %copy.133) | copy-start | bytes 663556
  29.4 1.5 copy-start.4
  32.0 217.6 %all-gather.5.cloned.1.call-start = ((), (), s32[]{:S(2)}) async-start(), calls=%async_computation | async-start | bytes 7299072 | tf_op jit(solution)/shard_map/all_gather | solution.py:225
  33.4 47.5 %collective-permute-start = (bf16[15,1,192]{0,2,1:T(8,128)(2,1)}, bf16[15,1,192]{0,2,1:T(8,128)(2,1)}, u32[]{:S(2)}, u32[]{:S(2)}) collective-permute-start(bf16[15,1,192]{0,2,1:T(8,128)(2,1)} %slice.163), channel_id=1, source_target_pairs={{32,0},{64,32},{96,64},{128,96},{160,128},{192,160},{224,192},{33,... | collective-permute-start | bytes 17288 | tf_op jit(solution)/shard_map/ppermute | solution.py:21
  58.3 12.9 %copy-start.13 = (s32[2]{0:T(128)S(1)}, s32[2]{0:T(128)}, u32[]{:S(2)}) copy-start(s32[2]{0:T(128)} %constant.157) | copy-start | bytes 28
  58.3 13.0 %copy-start.14 = (s32[2]{0:T(128)S(1)}, s32[2]{0:T(128)}, u32[]{:S(2)}) copy-start(s32[2]{0:T(128)} %constant.160) | copy-start | bytes 28
  73.5 1.2 copy-start.7
  73.5 0.5 copy-start.9
  124.9 66.1 %copy-start.12 = (s32[17]{0:T(128)S(1)}, s32[17]{0:T(128)}, u32[]{:S(2)}) copy-start(s32[17]{0:T(128)} %copy-done.11) | copy-start | bytes 208
  129.8 73.0 %copy-start.8 = (s32[3,2]{1,0:T(4,128)S(1)}, s32[3,2]{1,0:T(4,128)}, u32[]{:S(2)}) copy-start(s32[3,2]{1,0:T(4,128)} %copy-done.7) | copy-start | bytes 76
  129.8 73.0 %copy-start.10 = (s32[3,1]{1,0:T(4,128)S(1)}, s32[3,1]{1,0:T(4,128)}, u32[]{:S(2)}) copy-start(s32[3,1]{1,0:T(4,128)} %copy-done.9) | copy-start | bytes 40
  130.7 186.0 %all-gather.7.cloned.1.call-start = ((), (), s32[]{:S(2)}) async-start(), calls=%async_computation.1 | async-start | bytes 7299072 | tf_op jit(solution)/shard_map/all_gather | solution.py:225
  130.7 72.3 %collective-permute-start.1 = (bf16[1152,96]{1,0:T(8,128)(2,1)}, bf16[1152,96]{1,0:T(8,128)(2,1)S(1)}, u32[]{:S(2)}, u32[]{:S(2)}) collective-permute-start(bf16[1152,96]{1,0:T(8,128)(2,1)} %get-tuple-element.77), channel_id=1, source_target_pairs={{0,224},{32,192},{64,160},{96,128},{128,96},{160,64},{192,32},{224... | collective-permute-start | bytes 663560 | tf_op jit(solution)/shard_map/ppermute | solution.py:189
  234.7 9.0 %collective-permute-start.2 = (bf16[1152,96]{1,0:T(8,128)(2,1)S(1)}, bf16[1152,96]{1,0:T(8,128)(2,1)S(1)}, u32[]{:S(2)}, u32[]{:S(2)}) collective-permute-start(bf16[1152,96]{1,0:T(8,128)(2,1)S(1)} %shard_map.70), channel_id=1, source_target_pairs={{0,224},{32,192},{64,160},{96,128},{128,96},{160,64},{192,32},{224... | collective-permute-start | bytes 663560 | tf_op jit(solution)/shard_map/ppermute | solution.py:220
  245.8 1.3 copy-start.1
  254.0 67.0 %copy-start.5 = (bf16[2304,96]{0,1:T(8,128)(2,1)S(1)}, bf16[2304,96]{0,1:T(8,128)(2,1)}, u32[]{:S(2)}) copy-start(bf16[2304,96]{0,1:T(8,128)(2,1)} %param.8) | copy-start | bytes 1327108
Sparse Core Ops, SparseCore 0:
  32.1 92.7 all-gather.8
  130.8 111.8 all-gather.4
  245.9 70.7 all-gather.6

commit v5 on v4

--- a/solution.py
+++ b/solution.py
@@ -187,6 +187,7 @@
 
     partners = [(i, group_size - 1 - i) for i in range(group_size)]
     partner_queries = lax.ppermute(queries[half:], "gx", partners)
+    partner_residual = lax.ppermute(residual[half:], "gx", partners)
     partner_first = (group_size - 1 - group_index) * row_count + half
     partner_index = partner_first + jnp.arange(half, dtype=jnp.int32)
     partner_lows = starts_at[segment_of(ends_at, partner_index)]
@@ -215,21 +216,24 @@
     cache_pages = cache_pages.at[target, :, extended_position % PAGE].set(extended, mode="drop")
 
     key_columns = jnp.swapaxes(gathered, 1, 2)
-    key_columns, cache_pages, state = lax.optimization_barrier((key_columns, cache_pages, state))
-    partner_out = attend(partner_table, partner_queries, partner_lows, key_columns, None, True, row_count)
-    second_half = lax.ppermute(partner_out, "gx", partners)
+    key_columns, cache_pages, state, partner_queries, partner_residual = lax.optimization_barrier(
+        (key_columns, cache_pages, state, partner_queries, partner_residual)
+    )
     rest_table = block_table(q_first_rows, lo_first, lo_last, jnp.int32(0), jnp.minimum(first_row, key_count))
     first_half = attend(rest_table, queries[:half], lows[:half], key_columns, state, True, row_count)
-    updates = [
-        jnp.dot(
+    partner_out = attend(partner_table, partner_queries, partner_lows, key_columns, None, True, row_count)
+
+    def projected_rows(piece, rows_residual):
+        update = jnp.dot(
             lax.all_gather(piece, "gy", axis=1, tiled=True),
             weight_columns,
             preferred_element_type=jnp.float32,
         )
-        for piece in (first_half, second_half)
-    ]
-    update = jnp.concatenate(updates, axis=0)
-    hidden = (residual.astype(jnp.float32) + update).astype(jnp.bfloat16)
+        return (rows_residual.astype(jnp.float32) + update).astype(jnp.bfloat16)
+
+    hidden_first = projected_rows(first_half, residual[:half])
+    hidden_second = lax.ppermute(projected_rows(partner_out, partner_residual), "gx", partners)
+    hidden = jnp.concatenate([hidden_first, hidden_second], axis=0)
     return (hidden, cache_pages.reshape(pages_held, local_heads, PAGE * 2 * HD))
 
 

time: 331 us -> 313 us (0.946)
  starting transfers between devices: 62.2 us -> 12.9 us
  waiting for transfers between devices: 96.3 us -> 122 us
  local copies, waits for them, and re-layouts: 46.1 us -> 51.8 us
    ppermute x1, starting transfers between devices: 60.2 us -> 6.39 us  [per_device(): partner_queries = lax.ppermute(queries[half:], 'gx', partners)]
    all_gather x2, waiting for transfers between devices: 62.7 us -> 105 us  [projected_rows(): lax.all_gather(piece, 'gy', axis=1, tiled=True)]
    ppermute x1 -> x2, waiting for transfers between devices: 8.64 us -> 0.01 us  [the longest x1 0.01 us: per_device(): partner_residual = lax.ppermute(residual[half:], 'gx', partners)]
    all_gather x1, waiting for transfers between devices: 24.9 us -> 16.4 us  [per_device(): lax.all_gather(jnp.concatenate([local_kv, weight_rows], axis=0), 'gx', ax...]
    ppermute x1 -> x2, starting transfers between devices: 0.35 us -> 5.07 us  [the longest x1 3.12 us: per_device(): lax.ppermute(projected_rows(partner_out, partner_residual), 'gx', partners)]
  transfers between devices with their start and end apart: 6 -> 7, of which waited for: 3 -> 3; matrix products, arithmetic and copies ran while one was open for 25% -> 29% of each run, Pallas kernels for 11% -> 3%
where the time goes in v5:
time: 313 us; the launch traced here: 312 us
  waiting for transfers between devices  122 us (39%)
  other arithmetic  60.6 us (19%)
  local copies, waits for them, and re-layouts  51.8 us (17%)
  Pallas kernels  42.4 us (14%)
  between operations  14.2 us (5%)
  starting transfers between devices  12.9 us (4%)
  matrix products  8.61 us (3%)
    all_gather x2, waiting for transfers between devices, projected_rows(): lax.all_gather(piece, 'gy', axis=1, tiled=True)  105 us
    pallas_call x3, Pallas kernels, attend(): pl.pallas_call(kernel, grid_spec=pltpu.PrefetchScalarGridSpec(num_scalar_...  42.4 us
    unnamed x34, local copies, waits for them, and re-layouts  16.9 us
    all_gather x1, waiting for transfers between devices, per_device(): lax.all_gather(jnp.concatenate([local_kv, weight_rows], axis=0), 'gx', ax...  16.4 us
    gather x2, other arithmetic, per_device(): logical = page_base[extended_segment] + extended_position // PAGE  15.3 us
    gather x1, local copies, waits for them, and re-layouts, per_device(): page_table[logical] - group_index * pages_held  12.7 us
    gather x3, other arithmetic, per_device(): partner_lows = starts_at[segment_of(ends_at, partner_index)]  10.6 us
    dot_general x2, matrix products, projected_rows(): jnp.dot(lax.all_gather(piece, 'gy', axis=1, tiled=True), weight_columns,...  8.61 us
  transfers between devices with their start and end apart: 7, of which 3 were waited for; matrix products, arithmetic and copies ran while one was open for 29% of the time, Pallas kernels for 3%

profile of v5, /device:TPU:1, one launch (start us, length us, event | category | flops | bytes accessed | tf_op | source)
XLA Modules:
  0.0 312.1 jit_solution(11617712116407556812)
XLA Ops:
  9.7 4.4 %fusion.25 = (s32[2304]{0:T(1024)S(1)}, s32[2304,1]{0,1:T(1,128)S(1)}) fusion(s32[]{:T(128)} %bitcast.11, s32[]{:T(128)} %bitcast.12, s32[]{:T(128)} %bitcast.13, s32[]{:T(128)} %bitcast.14, s32[]{:T(128)} %bitcast.15, s32[]{:T(128)} %bitcast.17, s32[]{:T(128)} %bitcast.16, s32[2304]{0:T(1024)S(1)} %convert_reduce_fusion.1), kind=kLoop, calls=%fused_computation.123 | loop fusion | flops 34560 | bytes 27676 | tf_op jit(solution)/shard_map/gather | solution.py:180
  14.3 1.4 fusion.41
  16.5 6.1 %subtract_convert_fusion = (f32[2304]{0:T(1024)S(1)}, s32[2304]{0:T(1024)S(1)}) fusion(s32[]{:T(128)S(6)} %mul.94, pred[2304]{0:T(1024)(128)(4,1)S(1)} %get-tuple-element.43, pred[2304]{0:T(1024)(128)(4,1)S(1)} %get-tuple-element.42, pred[2304]{0:T(1024)(128)(4,1)S(1)} %get-tuple-element.41, pred[2304]{0:T(1024)(128)(4,1)S(1)} %get-tuple-element.40, ...), kind=kLoop, calls=%fused_computation.116 | loop fusion | flops 29952 | bytes 50732 | tf_op jit(solution)/shard_map/convert_element_type | solution.py:31
  22.6 6.3 %fusion.12 = (bf16[2304,1,48]{2,0,1:T(8,128)(2,1)S(1)}, bf16[2304,1,48]{2,0,1:T(8,128)(2,1)S(1)}, bf16[2304,1,48]{2,0,1:T(8,128)(2,1)S(1)}, bf16[2304,1,48]{2,0,1:T(8,128)(2,1)}) fusion(f32[2304,1,96]{2,0,1:T(8,128)S(1)} %get-tuple-element.130, f32[2304]{0:T(1024)S(1)} %get-tuple-element.63, f32[48]{0:T(128)S(1)} %multiply_power_fusion, ...), kind=kLoop, calls=%fused_computation.17 | loop fusion | flops 1880064 | bytes 2663616 | tf_op jit(solution)/shard_map/convert.5
  28.9 1.3 copy.133
  31.6 2.1 fusion.36
  33.7 1.0 maximum_bitcast_fusion
  34.8 1.0 fusion.21
  35.8 6.4 %collective-permute-start.1 = (bf16[1152,96]{1,0:T(8,128)(2,1)}, bf16[1152,96]{1,0:T(8,128)(2,1)}, u32[]{:S(2)}, u32[]{:S(2)}) collective-permute-start(bf16[1152,96]{1,0:T(8,128)(2,1)} %get-tuple-element.80), channel_id=1, source_target_pairs={{0,224},{32,192},{64,160},{96,128},{128,96},{160,64},{192,32},{224... | collective-permute-start | bytes 663560 | tf_op jit(solution)/shard_map/ppermute | solution.py:189
  42.2 1.4 slice.171
  43.6 1.3 collective-permute-start
  45.6 1.9 collective-permute-start.2
  47.8 4.4 %fusion.26 = (s32[1152]{0:T(1024)S(1)}, s32[1152,1]{0,1:T(1,128)S(1)}) fusion(s32[]{:T(128)} %bitcast.11, s32[]{:T(128)} %bitcast.12, s32[]{:T(128)} %bitcast.13, s32[]{:T(128)} %bitcast.14, s32[]{:T(128)} %bitcast.15, s32[]{:T(128)} %bitcast.17, s32[]{:T(128)} %bitcast.16, s32[1152]{0:T(1024)S(1)} %convert_reduce_fusion.2), kind=kLoop, calls=%fused_computation.129 | loop fusion | flops 17280 | bytes 13852 | tf_op jit(solution)/shard_map/gather | solution.py:193
  52.4 6.1 %select_select_fusion.3 = s32[1152]{0:T(1024)S(1)} fusion(pred[1152]{0:T(1024)(128)(4,1)S(1)} %get-tuple-element.53, pred[1152]{0:T(1024)(128)(4,1)S(1)} %get-tuple-element.52, pred[1152]{0:T(1024)(128)(4,1)S(1)} %get-tuple-element.51, pred[1152]{0:T(1024)(128)(4,1)S(1)} %get-tuple-element.50, pred[1152]{0:T(1024)(128)(4,1)S(1)} %get-tuple-element.49, ...), kind=kLoop, calls=%fused_computation.124 | loop fusion | flops 11520 | bytes 20776 | tf_op jit(solution)/shard_map/gather | solution.py:193
  59.7 8.8 %fusion.22 = (s32[2319]{0:T(1024)S(1)}, s32[2319]{0:T(1024)S(1)}, s32[2319,1]{0,1:T(1,128)S(1)}) fusion(s32[]{:T(128)} %bitcast.43, s32[]{:T(128)} %bitcast.44, s32[]{:T(128)} %bitcast.45, s32[]{:T(128)} %bitcast.46, s32[]{:T(128)} %bitcast.47, s32[]{:T(128)} %bitcast.49, s32[]{:T(128)} %bitcast.48, s32[]{:T(128)} %bitcast.17, s32[]{:T(128)} %bitcast.16, ...), kind=kLoop, calls=%fused_computation.118 | loop fusion | flops 48699 | bytes 37160 | tf_op jit(solution)/shard_map/gather | solution.py:210
  68.8 6.1 %select_select_fusion.1 = s32[2319]{0:T(1024)S(1)} fusion(pred[2319]{0:T(1024)(128)(4,1)S(1)} %get-tuple-element.33, pred[2319]{0:T(1024)(128)(4,1)S(1)} %get-tuple-element.32, pred[2319]{0:T(1024)(128)(4,1)S(1)} %get-tuple-element.31, pred[2319]{0:T(1024)(128)(4,1)S(1)} %get-tuple-element.30, pred[2319]{0:T(1024)(128)(4,1)S(1)} %get-tuple-element.29, ...), kind=kLoop, calls=%fused_computation.113 | loop fusion | flops 23190 | bytes 41782 | tf_op jit(solution)/shard_map/gather | solution.py:207
  74.9 6.5 %select_select_fusion = s32[2319]{0:T(1024)S(1)} fusion(pred[2319]{0:T(1024)(128)(4,1)S(1)} %get-tuple-element.33, pred[2319]{0:T(1024)(128)(4,1)S(1)} %get-tuple-element.32, pred[2319]{0:T(1024)(128)(4,1)S(1)} %get-tuple-element.31, pred[2319]{0:T(1024)(128)(4,1)S(1)} %get-tuple-element.30, pred[2319]{0:T(1024)(128)(4,1)S(1)} %get-tuple-element.29, ...), kind=kLoop, calls=%fused_computation.112 | loop fusion | flops 23190 | bytes 41782 | tf_op jit(solution)/shard_map/gather | solution.py:210
  81.6 12.7 %gather_fusion = s32[2319]{0:T(1024)S(1)} fusion(s32[1169]{0:T(1024)S(1)} %copy-done, s32[3072]{0:T(1024)S(1)} %pad_clamp_fusion), kind=kCustom, calls=%fused_computation | custom fusion | bytes 27828 | tf_op jit(solution)/shard_map/gather | solution.py:214
  97.8 5.9 %shard_map.68 = (f32[1152,1]{1,0:T(8,128)S(1)}, f32[1152,1]{1,0:T(8,128)S(1)}, f32[1152,96]{1,0:T(8,128)S(1)}) custom-call(s32[24]{0:T(128)S(1)} %reshape.526.table_ref, bf16[1152,96]{1,0:T(8,128)(2,1)S(1)} %get-tuple-element.81.q_ref, s32[1152,1]{1,0:T(8,128)S(1)} %slice.158.lo_ref, bf16[1,192,2304]{2,1,0:T(8,128)(2,1)S(1)} %get-tuple-element.82.kv_ref), custom_call_target="tpu_custom_call" | custom-call | tf_op jit(solution)/shard_map/pallas_call | solution.py:141
  104.5 2.2 maximum_bitcast_fusion.1
  106.8 2.4 copy.138
  109.2 14.4 %scatter_custom_fusion = bf16[2576,192]{1,0:T(8,128)(2,1)} fusion(s32[2319]{0:T(1024)} %broadcast_select_fusion, bf16[2319,192]{1,0:T(8,128)(2,1)} %copy.138, bf16[]{:T(256)} %constant.149.clone.1), kind=kCustom, calls=%fused_computation.25 | custom fusion | bytes 989696
  123.6 16.4 %all-gather.9.cloned.1.call-done = bf16[8,2496,192]{1,2,0:T(8,128)(2,1)} async-done(((bf16[1,2496,192]{1,2,0:T(8,128)(2,1)}), bf16[8,2496,192]{1,2,0:T(8,128)(2,1)}) %all-gather.9.cloned.1.call-update) | async-done | bytes 7667728 | tf_op jit(solution)/shard_map/all_gather | solution.py:173
  140.0 31.7 %shard_map.70 = bf16[1152,96]{1,0:T(8,128)(2,1)S(1)} custom-call(s32[24]{0:T(128)S(1)} %reshape.528.table_ref, bf16[1152,96]{1,0:T(8,128)(2,1)} %collective-permute-done.1.q_ref, s32[1152,1]{1,0:T(8,128)S(1)} %reshape.811.lo_ref, bf16[8,192,2496]{2,1,0:T(8,128)(2,1)} %bitcast.85), custom_call_target="tpu_custom_call" | custom-call | tf_op jit(solution)/shard_map/pallas_call | solution.py:141
  176.2 4.9 %shard_map.69 = bf16[1152,96]{1,0:T(8,128)(2,1)S(1)} custom-call(s32[24]{0:T(128)S(1)} %reshape.519.table_ref, bf16[1152,96]{1,0:T(8,128)(2,1)S(1)} %get-tuple-element.81.q_ref, s32[1152,1]{1,0:T(8,128)S(1)} %slice.158.lo_ref, bf16[8,192,2496]{2,1,0:T(8,128)(2,1)} %bitcast.86, f32[1152,1]{1,0:T(8,128)S(1)} %get-tuple-element.16.rest_0_, ...), custom_call_target="tpu_custom_call" | custom-call | tf_op jit(solution)/shard_map/pallas_call | solution.py:141
  182.0 1.2 slice.172
  184.5 2.5 reshape.530
  187.0 56.5 %all-gather.7.cloned.1.call-done = bf16[1152,3072]{0,1:T(8,128)(2,1)} async-done(((bf16[1152,96]{0,1:T(8,128)(2,1)}), bf16[1152,3072]{0,1:T(8,128)(2,1)}) %all-gather.7.cloned.1.call-update) | async-done | bytes 7077904 | tf_op jit(solution)/shard_map/all_gather | solution.py:228
  243.5 4.3 %fusion.44 = f32[1152,96]{0,1:T(8,128)S(1)} fusion(bf16[1152,3072]{0,1:T(8,128)(2,1)} %all-gather.7.cloned.1.call-done, bf16[3072,96]{1,0:T(8,128)(2,1)S(1)} %reshape.527), kind=kOutput, calls=%fused_computation.169 | convolution fusion | flops 679477248 | bytes 8110080 | tf_op jit(solution)/shard_map/dot_general | solution.py:227
  248.8 3.1 %collective-permute-start.3 = (bf16[1152,96]{0,1:T(8,128)(2,1)S(1)}, bf16[1152,96]{0,1:T(8,128)(2,1)S(1)}, u32[]{:S(2)}, u32[]{:S(2)}) collective-permute-start(bf16[1152,96]{0,1:T(8,128)(2,1)S(1)} %add_convert_fusion), channel_id=1, source_target_pairs={{0,224},{32,192},{64,160},{96,128},{128,96},{160,64},{192,32},{224... | collective-permute-start | bytes 663560 | tf_op jit(solution)/shard_map/ppermute | solution.py:235
  251.9 48.5 %all-gather.5.cloned.1.call-done = bf16[1152,3072]{0,1:T(8,128)(2,1)} async-done(((bf16[1152,96]{0,1:T(8,128)(2,1)}), bf16[1152,3072]{0,1:T(8,128)(2,1)}) %all-gather.5.cloned.1.call-update) | async-done | bytes 7077904 | tf_op jit(solution)/shard_map/all_gather | solution.py:228
  300.4 4.3 %fusion = bf16[1152,96]{0,1:T(8,128)(2,1)S(1)} fusion(bf16[1152,3072]{0,1:T(8,128)(2,1)} %all-gather.5.cloned.1.call-done, bf16[3072,96]{1,0:T(8,128)(2,1)S(1)} %reshape.527, bf16[2304,96]{0,1:T(8,128)(2,1)S(1)} %copy-done.7), kind=kOutput, calls=%fused_computation.3 | convolution fusion | flops 679809024 | bytes 8110080 | tf_op jit(solution)/shard_map/dot_general | solution.py:227
  (114 shorter events, 20.3 us)
Async XLA Ops:
  7.2 74.4 %copy-start = (s32[1169]{0:T(1024)S(1)}, s32[1169]{0:T(1024)}, u32[]{:S(2)}) copy-start(s32[1169]{0:T(1024)} %param.6) | copy-start | bytes 14032
  7.2 132.8 %all-gather.9.cloned.1.call-start = ((), (), s32[]{:S(2)}) async-start(), calls=%async_computation.2 | async-start | bytes 8847360 | tf_op jit(solution)/shard_map/all_gather | solution.py:173
  15.7 15.8 %copy-start.4 = (bf16[2304,1,96]{0,2,1:T(8,128)(2,1)}, bf16[2304,1,96]{0,2,1:T(8,128)(2,1)S(1)}, u32[]{:S(2)}) copy-start(bf16[2304,1,96]{0,2,1:T(8,128)(2,1)S(1)} %get-tuple-element.74) | copy-start | bytes 1327108
  28.9 2.3 copy-start.8
  30.3 3.4 %copy-start.5 = (bf16[2304,1,48]{0,2,1:T(8,128)(2,1)}, bf16[2304,1,48]{0,2,1:T(8,128)(2,1)S(1)}, u32[]{:S(2)}) copy-start(bf16[2304,1,48]{0,2,1:T(8,128)(2,1)S(1)} %copy.133) | copy-start | bytes 663556
  34.7 10.2 %copy-start.6 = (bf16[2304,96]{0,1:T(8,128)(2,1)S(1)}, bf16[2304,96]{0,1:T(8,128)(2,1)}, u32[]{:S(2)}) copy-start(bf16[2304,96]{0,1:T(8,128)(2,1)} %param.8) | copy-start | bytes 1327108
  34.7 208.8 %all-gather.7.cloned.1.call-start = ((), (), s32[]{:S(2)}) async-start(), calls=%async_computation.1 | async-start | bytes 7299072 | tf_op jit(solution)/shard_map/all_gather | solution.py:228
  35.8 87.8 %collective-permute-start.1 = (bf16[1152,96]{1,0:T(8,128)(2,1)}, bf16[1152,96]{1,0:T(8,128)(2,1)}, u32[]{:S(2)}, u32[]{:S(2)}) collective-permute-start(bf16[1152,96]{1,0:T(8,128)(2,1)} %get-tuple-element.80), channel_id=1, source_target_pairs={{0,224},{32,192},{64,160},{96,128},{128,96},{160,64},{192,32},{224... | collective-permute-start | bytes 663560 | tf_op jit(solution)/shard_map/ppermute | solution.py:189
  43.6 60.9 %collective-permute-start = (bf16[15,1,192]{0,2,1:T(8,128)(2,1)}, bf16[15,1,192]{0,2,1:T(8,128)(2,1)}, u32[]{:S(2)}, u32[]{:S(2)}) collective-permute-start(bf16[15,1,192]{0,2,1:T(8,128)(2,1)} %slice.171), channel_id=1, source_target_pairs={{32,0},{64,32},{96,64},{128,96},{160,128},{192,160},{224,192},{33,... | collective-permute-start | bytes 17288 | tf_op jit(solution)/shard_map/ppermute | solution.py:21
  45.6 78.0 %collective-permute-start.2 = (bf16[1152,96]{0,1:T(8,128)(2,1)}, bf16[1152,96]{0,1:T(8,128)(2,1)}, u32[]{:S(2)}, u32[]{:S(2)}) collective-permute-start(bf16[1152,96]{0,1:T(8,128)(2,1)} %slice.82), channel_id=1, source_target_pairs={{0,224},{32,192},{64,160},{96,128},{128,96},{160,64},{192,32},{224... | collective-permute-start | bytes 663560 | tf_op jit(solution)/shard_map/ppermute | solution.py:190
  81.6 12.9 %copy-start.13 = (s32[2]{0:T(128)S(1)}, s32[2]{0:T(128)}, u32[]{:S(2)}) copy-start(s32[2]{0:T(128)} %constant.157) | copy-start | bytes 28
  81.6 13.0 %copy-start.14 = (s32[2]{0:T(128)S(1)}, s32[2]{0:T(128)}, u32[]{:S(2)}) copy-start(s32[2]{0:T(128)} %constant.160) | copy-start | bytes 28
  94.3 2.3 copy-start.11
  96.5 1.0 copy-start.9
  97.3 0.5 copy-start.12
  103.7 0.8 copy-start.1
  140.0 35.4 %copy-start.10 = (s32[3,2]{1,0:T(4,128)S(1)}, s32[3,2]{1,0:T(4,128)}, u32[]{:S(2)}) copy-start(s32[3,2]{1,0:T(4,128)} %copy-done.9) | copy-start | bytes 76
  140.0 36.2 %copy-start.2 = (f32[1152,96]{1,0:T(8,128)S(1)}, f32[1152,96]{1,0:T(8,128)}, u32[]{:S(2)}) copy-start(f32[1152,96]{1,0:T(8,128)} %copy-done.1) | copy-start | bytes 1327108
  172.6 127.9 %all-gather.5.cloned.1.call-start = ((), (), s32[]{:S(2)}) async-start(), calls=%async_computation | async-start | bytes 7299072 | tf_op jit(solution)/shard_map/all_gather | solution.py:228
  183.1 1.3 copy-start.3
  187.0 113.5 %copy-start.7 = (bf16[2304,96]{0,1:T(8,128)(2,1)S(1)}, bf16[2304,96]{0,1:T(8,128)(2,1)}, u32[]{:S(2)}) copy-start(bf16[2304,96]{0,1:T(8,128)(2,1)} %param.8) | copy-start | bytes 1327108
  248.8 56.0 %collective-permute-start.3 = (bf16[1152,96]{0,1:T(8,128)(2,1)S(1)}, bf16[1152,96]{0,1:T(8,128)(2,1)S(1)}, u32[]{:S(2)}, u32[]{:S(2)}) collective-permute-start(bf16[1152,96]{0,1:T(8,128)(2,1)S(1)} %add_convert_fusion), channel_id=1, source_target_pairs={{0,224},{32,192},{64,160},{96,128},{128,96},{160,64},{192,32},{224... | collective-permute-start | bytes 663560 | tf_op jit(solution)/shard_map/ppermute | solution.py:235
Sparse Core Ops, SparseCore 0:
  34.8 105.0 all-gather.8
  172.7 70.7 all-gather.6
  246.0 54.3 all-gather.4

commit v6 on v5

--- a/solution.py
+++ b/solution.py
@@ -223,17 +223,16 @@
     first_half = attend(rest_table, queries[:half], lows[:half], key_columns, state, True, row_count)
     partner_out = attend(partner_table, partner_queries, partner_lows, key_columns, None, True, row_count)
 
-    def projected_rows(piece, rows_residual):
-        update = jnp.dot(
-            lax.all_gather(piece, "gy", axis=1, tiled=True),
-            weight_columns,
-            preferred_element_type=jnp.float32,
-        )
-        return (rows_residual.astype(jnp.float32) + update).astype(jnp.bfloat16)
-
-    hidden_first = projected_rows(first_half, residual[:half])
-    hidden_second = lax.ppermute(projected_rows(partner_out, partner_residual), "gx", partners)
-    hidden = jnp.concatenate([hidden_first, hidden_second], axis=0)
+    both = jnp.concatenate([first_half, partner_out], axis=0)
+    update = jnp.dot(
+        lax.all_gather(both, "gy", axis=1, tiled=True),
+        weight_columns,
+        preferred_element_type=jnp.float32,
+    )
+    both_residual = jnp.concatenate([residual[:half], partner_residual], axis=0)
+    projected = (both_residual.astype(jnp.float32) + update).astype(jnp.bfloat16)
+    hidden_second = lax.ppermute(projected[half:], "gx", partners)
+    hidden = jnp.concatenate([projected[:half], hidden_second], axis=0)
     return (hidden, cache_pages.reshape(pages_held, local_heads, PAGE * 2 * HD))
 
 

time: 313 us -> 312 us (level)
  Pallas kernels: 42.4 us -> 76.2 us
  waiting for transfers between devices: 122 us -> 93.7 us
    all_gather x2 -> x1, waiting for transfers between devices: 105 us -> 68.3 us  [per_device(): lax.all_gather(both, 'gy', axis=1, tiled=True)]
    pallas_call x3, Pallas kernels: 42.4 us -> 76.2 us  [attend(): pl.pallas_call(kernel, grid_spec=pltpu.PrefetchScalarGridSpec(num_scalar_...]
    ppermute x1, waiting for transfers between devices: 0.01 us -> 7.78 us  [per_device(): hidden_second = lax.ppermute(projected[half:], 'gx', partners)]
    ppermute x1, starting transfers between devices: 6.39 us -> 0.01 us  [per_device(): partner_queries = lax.ppermute(queries[half:], 'gx', partners)]
    ppermute x1, starting transfers between devices: 1.95 us -> 6.39 us  [per_device(): partner_residual = lax.ppermute(residual[half:], 'gx', partners)]
    dot_general x2 -> x1, matrix products: 8.61 us -> 7.59 us  [per_device(): jnp.dot(lax.all_gather(both, 'gy', axis=1, tiled=True), weight_columns, p...]
    unnamed x34 -> x32, local copies, waits for them, and re-layouts: 16.9 us -> 17.6 us
  transfers between devices with their start and end apart: 7 -> 6, of which waited for: 3 -> 3; matrix products, arithmetic and copies ran while one was open for 29% -> 25% of each run, Pallas kernels for 3% -> 2%
where the time goes in v6:
time: 312 us; the launch traced here: 311 us
  waiting for transfers between devices  93.7 us (30%)
  Pallas kernels  76.2 us (24%)
  other arithmetic  58.6 us (19%)
  local copies, waits for them, and re-layouts  49.3 us (16%)
  between operations  14.5 us (5%)
  starting transfers between devices  11.1 us (4%)
  matrix products  7.59 us (2%)
    pallas_call x3, Pallas kernels, attend(): pl.pallas_call(kernel, grid_spec=pltpu.PrefetchScalarGridSpec(num_scalar_...  76.2 us
    all_gather x1, waiting for transfers between devices, per_device(): lax.all_gather(both, 'gy', axis=1, tiled=True)  68.3 us
    all_gather x1, waiting for transfers between devices, per_device(): lax.all_gather(jnp.concatenate([local_kv, weight_rows], axis=0), 'gx', ax...  17.6 us
    unnamed x32, local copies, waits for them, and re-layouts  17.6 us
    gather x2, other arithmetic, per_device(): logical = page_base[extended_segment] + extended_position // PAGE  14.9 us
    gather x1, local copies, waits for them, and re-layouts, per_device(): page_table[logical] - group_index * pages_held  12.7 us
    gather x3, other arithmetic, per_device(): partner_lows = starts_at[segment_of(ends_at, partner_index)]  10.6 us
    ppermute x1, waiting for transfers between devices, per_device(): hidden_second = lax.ppermute(projected[half:], 'gx', partners)  7.78 us
  transfers between devices with their start and end apart: 6, of which 3 were waited for; matrix products, arithmetic and copies ran while one was open for 25% of the time, Pallas kernels for 2%

profile of v6, /device:TPU:1, one launch (start us, length us, event | category | flops | bytes accessed | tf_op | source)
XLA Modules:
  0.0 311.1 jit_solution(6802390023442111192)
XLA Ops:
  9.7 4.4 %fusion.25 = (s32[2304]{0:T(1024)S(1)}, s32[2304,1]{0,1:T(1,128)S(1)}) fusion(s32[]{:T(128)} %bitcast.13, s32[]{:T(128)} %bitcast.14, s32[]{:T(128)} %bitcast.15, s32[]{:T(128)} %bitcast.16, s32[]{:T(128)} %bitcast.17, s32[]{:T(128)} %bitcast.19, s32[]{:T(128)} %bitcast.18, s32[2304]{0:T(1024)S(1)} %convert_reduce_fusion.1), kind=kLoop, calls=%fused_computation.123 | loop fusion | flops 34560 | bytes 27676 | tf_op jit(solution)/shard_map/gather | solution.py:164
  14.3 1.0 copy.127
  15.5 1.4 fusion.41
  17.7 6.2 %subtract_convert_fusion = (f32[2304]{0:T(1024)S(1)}, s32[2304]{0:T(1024)S(1)}) fusion(s32[]{:T(128)S(6)} %mul.94, pred[2304]{0:T(1024)(128)(4,1)S(1)} %get-tuple-element.43, pred[2304]{0:T(1024)(128)(4,1)S(1)} %get-tuple-element.42, pred[2304]{0:T(1024)(128)(4,1)S(1)} %get-tuple-element.41, pred[2304]{0:T(1024)(128)(4,1)S(1)} %get-tuple-element.40, ...), kind=kLoop, calls=%fused_computation.116 | loop fusion | flops 29952 | bytes 50732 | tf_op jit(solution)/shard_map/convert_element_type | solution.py:31
  23.9 6.3 %fusion.16 = (bf16[2304,1,48]{2,0,1:T(8,128)(2,1)S(1)}, bf16[2304,1,48]{2,0,1:T(8,128)(2,1)S(1)}, bf16[2304,1,48]{2,0,1:T(8,128)(2,1)}, bf16[2304,1,48]{2,0,1:T(8,128)(2,1)S(1)}) fusion(f32[2304,1,96]{2,0,1:T(8,128)S(1)} %get-tuple-element.133, f32[2304]{0:T(1024)S(1)} %get-tuple-element.63, f32[48]{0:T(128)S(1)} %multiply_power_fusion, ...), kind=kLoop, calls=%fused_computation.21 | loop fusion | flops 1880064 | bytes 2663616 | tf_op jit(solution)/shard_map/convert.3
  30.2 1.3 copy.126
  32.4 2.0 fusion.36
  34.5 1.0 maximum_bitcast_fusion
  36.4 6.4 %collective-permute-start.2 = (bf16[1152,96]{0,1:T(8,128)(2,1)}, bf16[1152,96]{0,1:T(8,128)(2,1)}, u32[]{:S(2)}, u32[]{:S(2)}) collective-permute-start(bf16[1152,96]{0,1:T(8,128)(2,1)} %get-tuple-element.88), channel_id=1, source_target_pairs={{0,224},{32,192},{64,160},{96,128},{128,96},{160,64},{192,32},{224... | collective-permute-start | bytes 663560 | tf_op jit(solution)/shard_map/ppermute | solution.py:190
  42.8 1.0 fusion.21
  43.8 1.4 slice.173
  45.2 1.5 collective-permute-start
  46.8 4.3 %fusion.26 = (s32[1152]{0:T(1024)S(1)}, s32[1152,1]{0,1:T(1,128)S(1)}) fusion(s32[]{:T(128)} %bitcast.13, s32[]{:T(128)} %bitcast.14, s32[]{:T(128)} %bitcast.15, s32[]{:T(128)} %bitcast.16, s32[]{:T(128)} %bitcast.17, s32[]{:T(128)} %bitcast.19, s32[]{:T(128)} %bitcast.18, s32[1152]{0:T(1024)S(1)} %convert_reduce_fusion.2), kind=kLoop, calls=%fused_computation.129 | loop fusion | flops 17280 | bytes 13852 | tf_op jit(solution)/shard_map/gather | solution.py:193
  51.3 6.2 %select_select_fusion.3 = s32[1152]{0:T(1024)S(1)} fusion(pred[1152]{0:T(1024)(128)(4,1)S(1)} %get-tuple-element.53, pred[1152]{0:T(1024)(128)(4,1)S(1)} %get-tuple-element.52, pred[1152]{0:T(1024)(128)(4,1)S(1)} %get-tuple-element.51, pred[1152]{0:T(1024)(128)(4,1)S(1)} %get-tuple-element.50, pred[1152]{0:T(1024)(128)(4,1)S(1)} %get-tuple-element.49, ...), kind=kLoop, calls=%fused_computation.124 | loop fusion | flops 11520 | bytes 20776 | tf_op jit(solution)/shard_map/gather | solution.py:193
  59.0 8.7 %fusion.22 = (s32[2319]{0:T(1024)S(1)}, s32[2319]{0:T(1024)S(1)}, s32[2319,1]{0,1:T(1,128)S(1)}) fusion(s32[]{:T(128)} %bitcast.36, s32[]{:T(128)} %bitcast.37, s32[]{:T(128)} %bitcast.38, s32[]{:T(128)} %bitcast.39, s32[]{:T(128)} %bitcast.40, s32[]{:T(128)} %bitcast.42, s32[]{:T(128)} %bitcast.41, s32[]{:T(128)} %bitcast.19, s32[]{:T(128)} %bitcast.18, ...), kind=kLoop, calls=%fused_computation.118 | loop fusion | flops 48699 | bytes 37160 | tf_op jit(solution)/shard_map/gather | solution.py:210
  68.0 6.2 %select_select_fusion.1 = s32[2319]{0:T(1024)S(1)} fusion(pred[2319]{0:T(1024)(128)(4,1)S(1)} %get-tuple-element.33, pred[2319]{0:T(1024)(128)(4,1)S(1)} %get-tuple-element.32, pred[2319]{0:T(1024)(128)(4,1)S(1)} %get-tuple-element.31, pred[2319]{0:T(1024)(128)(4,1)S(1)} %get-tuple-element.30, pred[2319]{0:T(1024)(128)(4,1)S(1)} %get-tuple-element.29, ...), kind=kLoop, calls=%fused_computation.113 | loop fusion | flops 23190 | bytes 41782 | tf_op jit(solution)/shard_map/gather | solution.py:207
  74.1 6.2 %select_select_fusion = s32[2319]{0:T(1024)S(1)} fusion(pred[2319]{0:T(1024)(128)(4,1)S(1)} %get-tuple-element.33, pred[2319]{0:T(1024)(128)(4,1)S(1)} %get-tuple-element.32, pred[2319]{0:T(1024)(128)(4,1)S(1)} %get-tuple-element.31, pred[2319]{0:T(1024)(128)(4,1)S(1)} %get-tuple-element.30, pred[2319]{0:T(1024)(128)(4,1)S(1)} %get-tuple-element.29, ...), kind=kLoop, calls=%fused_computation.112 | loop fusion | flops 23190 | bytes 41782 | tf_op jit(solution)/shard_map/gather | solution.py:210
  80.5 12.7 %gather_fusion = s32[2319]{0:T(1024)S(1)} fusion(s32[1169]{0:T(1024)S(1)} %copy-done, s32[3072]{0:T(1024)S(1)} %pad_clamp_fusion), kind=kCustom, calls=%fused_computation | custom fusion | bytes 27828 | tf_op jit(solution)/shard_map/gather | solution.py:214
  97.7 5.9 %shard_map.68 = (f32[1152,1]{1,0:T(8,128)S(1)}, f32[1152,1]{1,0:T(8,128)S(1)}, f32[1152,96]{1,0:T(8,128)S(1)}) custom-call(s32[24]{0:T(128)S(1)} %copy-done.3, bf16[1152,96]{1,0:T(8,128)(2,1)S(1)} %get-tuple-element.81.q_ref, s32[1152,1]{1,0:T(8,128)S(1)} %slice.166.lo_ref, bf16[1,192,2304]{2,1,0:T(8,128)(2,1)S(1)} %get-tuple-element.82.kv_ref), custom_call_target="tpu_custom_call" | custom-call | tf_op jit(solution)/shard_map/pallas_call | solution.py:141
  104.4 1.9 maximum_bitcast_fusion.1
  106.2 2.3 copy.130
  108.6 14.4 %scatter_custom_fusion = bf16[2576,192]{1,0:T(8,128)(2,1)} fusion(s32[2319]{0:T(1024)} %broadcast_select_fusion, bf16[2319,192]{1,0:T(8,128)(2,1)} %copy.130, bf16[]{:T(256)} %constant.143.clone.1), kind=kCustom, calls=%fused_computation.25 | custom fusion | bytes 989696
  123.0 17.6 %all-gather.6.cloned.1.call-done = bf16[8,2496,192]{1,2,0:T(8,128)(2,1)} async-done(((bf16[1,2496,192]{1,2,0:T(8,128)(2,1)}), bf16[8,2496,192]{1,2,0:T(8,128)(2,1)}) %all-gather.6.cloned.1.call-update) | async-done | bytes 7667728 | tf_op jit(solution)/shard_map/all_gather | solution.py:173
  140.6 65.5 %shard_map.70 = bf16[1152,96]{1,0:T(8,128)(2,1)S(1)} custom-call(s32[24]{0:T(128)S(1)} %reshape.527.table_ref, bf16[1152,96]{1,0:T(8,128)(2,1)} %collective-permute-done.1.q_ref, s32[1152,1]{1,0:T(8,128)S(1)} %reshape.811.lo_ref, bf16[8,192,2496]{2,1,0:T(8,128)(2,1)} %bitcast.84), custom_call_target="tpu_custom_call" | custom-call | tf_op jit(solution)/shard_map/pallas_call | solution.py:141
  206.1 4.9 %shard_map.69 = bf16[1152,96]{1,0:T(8,128)(2,1)S(1)} custom-call(s32[24]{0:T(128)S(1)} %reshape.526.table_ref, bf16[1152,96]{1,0:T(8,128)(2,1)S(1)} %get-tuple-element.81.q_ref, s32[1152,1]{1,0:T(8,128)S(1)} %slice.166.lo_ref, bf16[8,192,2496]{2,1,0:T(8,128)(2,1)} %bitcast.85, f32[1152,1]{1,0:T(8,128)S(1)} %get-tuple-element.17.rest_0_, ...), custom_call_target="tpu_custom_call" | custom-call | tf_op jit(solution)/shard_map/pallas_call | solution.py:141
  211.1 1.0 copy.147
  212.1 1.2 slice.180
  214.1 68.3 %all-gather.4.cloned.1.call-done = bf16[2304,3072]{0,1:T(8,128)(2,1)} async-done(((bf16[2304,96]{0,1:T(8,128)(2,1)}), bf16[2304,3072]{0,1:T(8,128)(2,1)}) %all-gather.4.cloned.1.call-update) | async-done | bytes 14155792 | tf_op jit(solution)/shard_map/all_gather | solution.py:228
  282.4 7.6 %fusion = bf16[2304,96]{0,1:T(8,128)(2,1)S(1)} fusion(bf16[2304,3072]{0,1:T(8,128)(2,1)} %all-gather.4.cloned.1.call-done, bf16[3072,96]{1,0:T(8,128)(2,1)S(1)} %reshape.529, bf16[1152,96]{0,1:T(8,128)(2,1)} %collective-permute-done.2, bf16[1152,96]{0,1:T(8,128)(2,1)S(1)} %copy-done.11), kind=kOutput, calls=%fused_computation.3 | convolution fusion | flops 1360281600 | bytes 15630336 | tf_op jit(solution)/shard_map/dot_general | solution.py:227
  290.0 3.1 %collective-permute-start.3 = (bf16[1152,96]{0,1:T(8,128)(2,1)S(1)}, bf16[1152,96]{0,1:T(8,128)(2,1)S(1)}, u32[]{:S(2)}, u32[]{:S(2)}) collective-permute-start(bf16[1152,96]{0,1:T(8,128)(2,1)S(1)} %get-tuple-element.86), channel_id=1, source_target_pairs={{0,224},{32,192},{64,160},{96,128},{128,96},{160,64},{192,32},{224... | collective-permute-start | bytes 663560 | tf_op jit(solution)/shard_map/ppermute | solution.py:234
  293.2 2.5 reshape.530
  295.7 7.8 %collective-permute-done.3 = bf16[1152,96]{0,1:T(8,128)(2,1)S(1)} collective-permute-done((bf16[1152,96]{0,1:T(8,128)(2,1)S(1)}, bf16[1152,96]{0,1:T(8,128)(2,1)S(1)}, u32[]{:S(2)}, u32[]{:S(2)}) %collective-permute-start.3) | collective-permute-done | bytes 221216 | tf_op jit(solution)/shard_map/ppermute | solution.py:234
  (108 shorter events, 14.5 us)
Async XLA Ops:
  7.2 73.3 %copy-start = (s32[1169]{0:T(1024)S(1)}, s32[1169]{0:T(1024)}, u32[]{:S(2)}) copy-start(s32[1169]{0:T(1024)} %param.6) | copy-start | bytes 14032
  7.2 133.4 %all-gather.6.cloned.1.call-start = ((), (), s32[]{:S(2)}) async-start(), calls=%async_computation.1 | async-start | bytes 8847360 | tf_op jit(solution)/shard_map/all_gather | solution.py:173
  16.9 15.5 %copy-start.5 = (bf16[2304,1,96]{0,2,1:T(8,128)(2,1)}, bf16[2304,1,96]{0,2,1:T(8,128)(2,1)S(1)}, u32[]{:S(2)}) copy-start(bf16[2304,1,96]{0,2,1:T(8,128)(2,1)S(1)} %get-tuple-element.75) | copy-start | bytes 1327108
  31.5 3.0 copy-start.7
  34.5 1.1 copy-start.10
  35.5 246.9 %all-gather.4.cloned.1.call-start = ((), (), s32[]{:S(2)}) async-start(), calls=%async_computation | async-start | bytes 14598144 | tf_op jit(solution)/shard_map/all_gather | solution.py:228
  36.4 86.6 %collective-permute-start.2 = (bf16[1152,96]{0,1:T(8,128)(2,1)}, bf16[1152,96]{0,1:T(8,128)(2,1)}, u32[]{:S(2)}, u32[]{:S(2)}) collective-permute-start(bf16[1152,96]{0,1:T(8,128)(2,1)} %get-tuple-element.88), channel_id=1, source_target_pairs={{0,224},{32,192},{64,160},{96,128},{128,96},{160,64},{192,32},{224... | collective-permute-start | bytes 663560 | tf_op jit(solution)/shard_map/ppermute | solution.py:190
  43.8 79.2 %collective-permute-start.1 = (bf16[1152,96]{1,0:T(8,128)(2,1)}, bf16[1152,96]{1,0:T(8,128)(2,1)}, u32[]{:S(2)}, u32[]{:S(2)}) collective-permute-start(bf16[1152,96]{1,0:T(8,128)(2,1)} %get-tuple-element.80), channel_id=1, source_target_pairs={{0,224},{32,192},{64,160},{96,128},{128,96},{160,64},{192,32},{224... | collective-permute-start | bytes 663560 | tf_op jit(solution)/shard_map/ppermute | solution.py:189
  45.2 59.1 %collective-permute-start = (bf16[15,1,192]{0,2,1:T(8,128)(2,1)}, bf16[15,1,192]{0,2,1:T(8,128)(2,1)}, u32[]{:S(2)}, u32[]{:S(2)}) collective-permute-start(bf16[15,1,192]{0,2,1:T(8,128)(2,1)} %slice.173), channel_id=1, source_target_pairs={{32,0},{64,32},{96,64},{128,96},{160,128},{192,160},{224,192},{33,... | collective-permute-start | bytes 17288 | tf_op jit(solution)/shard_map/ppermute | solution.py:21
  80.5 12.9 %copy-start.12 = (s32[2]{0:T(128)S(1)}, s32[2]{0:T(128)}, u32[]{:S(2)}) copy-start(s32[2]{0:T(128)} %constant.157) | copy-start | bytes 28
  80.5 13.0 %copy-start.13 = (s32[2]{0:T(128)S(1)}, s32[2]{0:T(128)}, u32[]{:S(2)}) copy-start(s32[2]{0:T(128)} %constant.160) | copy-start | bytes 28
  96.8 7.6 %copy-start.6 = (bf16[2304,1,96]{0,2,1:T(8,128)(2,1)S(1)}, bf16[2304,1,96]{0,2,1:T(8,128)(2,1)}, u32[]{:S(2)}) copy-start(bf16[2304,1,96]{0,2,1:T(8,128)(2,1)} %copy-done.5) | copy-start | bytes 1327108
  97.0 0.7 copy-start.3
  97.7 6.7 %copy-start.8 = (bf16[2304,1,48]{0,2,1:T(8,128)(2,1)S(1)}, bf16[2304,1,48]{0,2,1:T(8,128)(2,1)}, u32[]{:S(2)}) copy-start(bf16[2304,1,48]{0,2,1:T(8,128)(2,1)} %copy-done.7) | copy-start | bytes 663556
  97.7 6.7 %copy-start.9 = (bf16[2304,1,48]{0,2,1:T(8,128)(2,1)S(1)}, bf16[2304,1,48]{0,2,1:T(8,128)(2,1)}, u32[]{:S(2)}) copy-start(bf16[2304,1,48]{0,2,1:T(8,128)(2,1)} %copy.125) | copy-start | bytes 663556
  103.6 0.8 copy-start.1
  140.6 65.5 %copy-start.2 = (f32[1152,96]{1,0:T(8,128)S(1)}, f32[1152,96]{1,0:T(8,128)}, u32[]{:S(2)}) copy-start(f32[1152,96]{1,0:T(8,128)} %copy-done.1) | copy-start | bytes 1327108
  213.3 69.1 %copy-start.11 = (bf16[1152,96]{0,1:T(8,128)(2,1)S(1)}, bf16[1152,96]{0,1:T(8,128)(2,1)}, u32[]{:S(2)}) copy-start(bf16[1152,96]{0,1:T(8,128)(2,1)} %get-tuple-element.87) | copy-start | bytes 663556
  282.4 10.8 %copy-start.4 = (bf16[2576,192]{1,0:T(8,128)(2,1)S(1)}, bf16[2576,192]{1,0:T(8,128)(2,1)}, u32[]{:S(2)}) copy-start(bf16[2576,192]{1,0:T(8,128)(2,1)} %scatter_custom_fusion) | copy-start | bytes 2967556
  290.0 13.4 %collective-permute-start.3 = (bf16[1152,96]{0,1:T(8,128)(2,1)S(1)}, bf16[1152,96]{0,1:T(8,128)(2,1)S(1)}, u32[]{:S(2)}, u32[]{:S(2)}) collective-permute-start(bf16[1152,96]{0,1:T(8,128)(2,1)S(1)} %get-tuple-element.86), channel_id=1, source_target_pairs={{0,224},{32,192},{64,160},{96,128},{128,96},{160,64},{192,32},{224... | collective-permute-start | bytes 663560 | tf_op jit(solution)/shard_map/ppermute | solution.py:234
Sparse Core Ops, SparseCore 0:
  35.6 104.8 all-gather.5
  212.3 70.0 all-gather.3

commit v7 on v6

--- a/solution.py
+++ b/solution.py
@@ -11,7 +11,7 @@
 HD = 96
 PAGE = 16
 BQ = 384
-BK = 768
+BK = 1152
 NEG = -1e30
 
 

time: 312 us -> 327 us (1.048)
  waiting for transfers between devices: 93.7 us -> 162 us
  Pallas kernels: 76.2 us -> 23.1 us
    all_gather x1, waiting for transfers between devices: 68.3 us -> 137 us  [per_device(): lax.all_gather(both, 'gy', axis=1, tiled=True)]
    pallas_call x3, Pallas kernels: 76.2 us -> 23.1 us  [attend(): pl.pallas_call(kernel, grid_spec=pltpu.PrefetchScalarGridSpec(num_scalar_...]
  transfers between devices with their start and end apart: 6 -> 6, of which waited for: 3 -> 3; matrix products, arithmetic and copies ran while one was open for 25% -> 23% of each run, Pallas kernels for 2% -> 2%
where the time goes in v7:
time: 327 us; the launch traced here: 326 us
  waiting for transfers between devices  162 us (50%)
  other arithmetic  58.6 us (18%)
  local copies, waits for them, and re-layouts  49.4 us (15%)
  Pallas kernels  23.1 us (7%)
  between operations  14.5 us (4%)
  starting transfers between devices  11.1 us (3%)
  matrix products  7.59 us (2%)
    all_gather x1, waiting for transfers between devices, per_device(): lax.all_gather(both, 'gy', axis=1, tiled=True)  137 us
    pallas_call x3, Pallas kernels, attend(): pl.pallas_call(kernel, grid_spec=pltpu.PrefetchScalarGridSpec(num_scalar_...  23.1 us
    unnamed x32, local copies, waits for them, and re-layouts  17.6 us
    all_gather x1, waiting for transfers between devices, per_device(): lax.all_gather(jnp.concatenate([local_kv, weight_rows], axis=0), 'gx', ax...  16.9 us
    gather x2, other arithmetic, per_device(): logical = page_base[extended_segment] + extended_position // PAGE  14.9 us
    gather x1, local copies, waits for them, and re-layouts, per_device(): page_table[logical] - group_index * pages_held  12.7 us
    gather x3, other arithmetic, per_device(): partner_lows = starts_at[segment_of(ends_at, partner_index)]  10.6 us
    ppermute x1, waiting for transfers between devices, per_device(): hidden_second = lax.ppermute(projected[half:], 'gx', partners)  7.78 us
  transfers between devices with their start and end apart: 6, of which 3 were waited for; matrix products, arithmetic and copies ran while one was open for 23% of the time, Pallas kernels for 2%

profile of v7, /device:TPU:1, one launch (start us, length us, event | category | flops | bytes accessed | tf_op | source)
XLA Modules:
  0.0 325.9 jit_solution(15366874931870988523)
XLA Ops:
  9.7 4.4 %fusion.25 = (s32[2304]{0:T(1024)S(1)}, s32[2304,1]{0,1:T(1,128)S(1)}) fusion(s32[]{:T(128)} %bitcast.13, s32[]{:T(128)} %bitcast.14, s32[]{:T(128)} %bitcast.15, s32[]{:T(128)} %bitcast.16, s32[]{:T(128)} %bitcast.17, s32[]{:T(128)} %bitcast.19, s32[]{:T(128)} %bitcast.18, s32[2304]{0:T(1024)S(1)} %convert_reduce_fusion.1), kind=kLoop, calls=%fused_computation.123 | loop fusion | flops 34560 | bytes 27676 | tf_op jit(solution)/shard_map/gather | solution.py:164
  14.3 1.0 copy.127
  15.5 1.4 fusion.41
  17.7 6.2 %subtract_convert_fusion = (f32[2304]{0:T(1024)S(1)}, s32[2304]{0:T(1024)S(1)}) fusion(s32[]{:T(128)S(6)} %mul.94, pred[2304]{0:T(1024)(128)(4,1)S(1)} %get-tuple-element.43, pred[2304]{0:T(1024)(128)(4,1)S(1)} %get-tuple-element.42, pred[2304]{0:T(1024)(128)(4,1)S(1)} %get-tuple-element.41, pred[2304]{0:T(1024)(128)(4,1)S(1)} %get-tuple-element.40, ...), kind=kLoop, calls=%fused_computation.116 | loop fusion | flops 29952 | bytes 50732 | tf_op jit(solution)/shard_map/convert_element_type | solution.py:31
  23.9 6.3 %fusion.16 = (bf16[2304,1,48]{2,0,1:T(8,128)(2,1)S(1)}, bf16[2304,1,48]{2,0,1:T(8,128)(2,1)S(1)}, bf16[2304,1,48]{2,0,1:T(8,128)(2,1)}, bf16[2304,1,48]{2,0,1:T(8,128)(2,1)S(1)}) fusion(f32[2304,1,96]{2,0,1:T(8,128)S(1)} %get-tuple-element.133, f32[2304]{0:T(1024)S(1)} %get-tuple-element.63, f32[48]{0:T(128)S(1)} %multiply_power_fusion, ...), kind=kLoop, calls=%fused_computation.21 | loop fusion | flops 1880064 | bytes 2663616 | tf_op jit(solution)/shard_map/convert.3
  30.2 1.3 copy.126
  32.4 2.0 fusion.36
  34.5 1.0 maximum_bitcast_fusion
  36.4 6.4 %collective-permute-start.2 = (bf16[1152,96]{0,1:T(8,128)(2,1)}, bf16[1152,96]{0,1:T(8,128)(2,1)}, u32[]{:S(2)}, u32[]{:S(2)}) collective-permute-start(bf16[1152,96]{0,1:T(8,128)(2,1)} %get-tuple-element.88), channel_id=1, source_target_pairs={{0,224},{32,192},{64,160},{96,128},{128,96},{160,64},{192,32},{224... | collective-permute-start | bytes 663560 | tf_op jit(solution)/shard_map/ppermute | solution.py:190
  42.8 1.0 fusion.21
  43.8 1.4 slice.173
  45.2 1.5 collective-permute-start
  46.8 4.3 %fusion.26 = (s32[1152]{0:T(1024)S(1)}, s32[1152,1]{0,1:T(1,128)S(1)}) fusion(s32[]{:T(128)} %bitcast.13, s32[]{:T(128)} %bitcast.14, s32[]{:T(128)} %bitcast.15, s32[]{:T(128)} %bitcast.16, s32[]{:T(128)} %bitcast.17, s32[]{:T(128)} %bitcast.19, s32[]{:T(128)} %bitcast.18, s32[1152]{0:T(1024)S(1)} %convert_reduce_fusion.2), kind=kLoop, calls=%fused_computation.129 | loop fusion | flops 17280 | bytes 13852 | tf_op jit(solution)/shard_map/gather | solution.py:193
  51.3 6.2 %select_select_fusion.3 = s32[1152]{0:T(1024)S(1)} fusion(pred[1152]{0:T(1024)(128)(4,1)S(1)} %get-tuple-element.53, pred[1152]{0:T(1024)(128)(4,1)S(1)} %get-tuple-element.52, pred[1152]{0:T(1024)(128)(4,1)S(1)} %get-tuple-element.51, pred[1152]{0:T(1024)(128)(4,1)S(1)} %get-tuple-element.50, pred[1152]{0:T(1024)(128)(4,1)S(1)} %get-tuple-element.49, ...), kind=kLoop, calls=%fused_computation.124 | loop fusion | flops 11520 | bytes 20776 | tf_op jit(solution)/shard_map/gather | solution.py:193
  59.0 8.7 %fusion.22 = (s32[2319]{0:T(1024)S(1)}, s32[2319]{0:T(1024)S(1)}, s32[2319,1]{0,1:T(1,128)S(1)}) fusion(s32[]{:T(128)} %bitcast.36, s32[]{:T(128)} %bitcast.37, s32[]{:T(128)} %bitcast.38, s32[]{:T(128)} %bitcast.39, s32[]{:T(128)} %bitcast.40, s32[]{:T(128)} %bitcast.42, s32[]{:T(128)} %bitcast.41, s32[]{:T(128)} %bitcast.19, s32[]{:T(128)} %bitcast.18, ...), kind=kLoop, calls=%fused_computation.118 | loop fusion | flops 48699 | bytes 37160 | tf_op jit(solution)/shard_map/gather | solution.py:210
  68.0 6.2 %select_select_fusion.1 = s32[2319]{0:T(1024)S(1)} fusion(pred[2319]{0:T(1024)(128)(4,1)S(1)} %get-tuple-element.33, pred[2319]{0:T(1024)(128)(4,1)S(1)} %get-tuple-element.32, pred[2319]{0:T(1024)(128)(4,1)S(1)} %get-tuple-element.31, pred[2319]{0:T(1024)(128)(4,1)S(1)} %get-tuple-element.30, pred[2319]{0:T(1024)(128)(4,1)S(1)} %get-tuple-element.29, ...), kind=kLoop, calls=%fused_computation.113 | loop fusion | flops 23190 | bytes 41782 | tf_op jit(solution)/shard_map/gather | solution.py:207
  74.1 6.2 %select_select_fusion = s32[2319]{0:T(1024)S(1)} fusion(pred[2319]{0:T(1024)(128)(4,1)S(1)} %get-tuple-element.33, pred[2319]{0:T(1024)(128)(4,1)S(1)} %get-tuple-element.32, pred[2319]{0:T(1024)(128)(4,1)S(1)} %get-tuple-element.31, pred[2319]{0:T(1024)(128)(4,1)S(1)} %get-tuple-element.30, pred[2319]{0:T(1024)(128)(4,1)S(1)} %get-tuple-element.29, ...), kind=kLoop, calls=%fused_computation.112 | loop fusion | flops 23190 | bytes 41782 | tf_op jit(solution)/shard_map/gather | solution.py:210
  80.5 12.7 %gather_fusion = s32[2319]{0:T(1024)S(1)} fusion(s32[1169]{0:T(1024)S(1)} %copy-done, s32[3072]{0:T(1024)S(1)} %pad_clamp_fusion), kind=kCustom, calls=%fused_computation | custom fusion | bytes 27828 | tf_op jit(solution)/shard_map/gather | solution.py:214
  97.7 6.6 %shard_map.68 = (f32[1152,1]{1,0:T(8,128)S(1)}, f32[1152,1]{1,0:T(8,128)S(1)}, f32[1152,96]{1,0:T(8,128)S(1)}) custom-call(s32[24]{0:T(128)S(1)} %copy-done.3, bf16[1152,96]{1,0:T(8,128)(2,1)S(1)} %get-tuple-element.81.q_ref, s32[1152,1]{1,0:T(8,128)S(1)} %slice.166.lo_ref, bf16[1,192,2304]{2,1,0:T(8,128)(2,1)S(1)} %get-tuple-element.82.kv_ref), custom_call_target="tpu_custom_call" | custom-call | tf_op jit(solution)/shard_map/pallas_call | solution.py:141
  105.1 1.9 maximum_bitcast_fusion.1
  107.0 2.3 copy.130
  109.3 14.4 %scatter_custom_fusion = bf16[2576,192]{1,0:T(8,128)(2,1)} fusion(s32[2319]{0:T(1024)} %broadcast_select_fusion, bf16[2319,192]{1,0:T(8,128)(2,1)} %copy.130, bf16[]{:T(256)} %constant.142.clone.1), kind=kCustom, calls=%fused_computation.25 | custom fusion | bytes 989696
  123.7 16.9 %all-gather.6.cloned.1.call-done = bf16[8,2496,192]{1,2,0:T(8,128)(2,1)} async-done(((bf16[1,2496,192]{1,2,0:T(8,128)(2,1)}), bf16[8,2496,192]{1,2,0:T(8,128)(2,1)}) %all-gather.6.cloned.1.call-update) | async-done | bytes 7667728 | tf_op jit(solution)/shard_map/all_gather | solution.py:173
  140.6 11.4 %shard_map.70 = bf16[1152,96]{1,0:T(8,128)(2,1)S(1)} custom-call(s32[24]{0:T(128)S(1)} %reshape.527.table_ref, bf16[1152,96]{1,0:T(8,128)(2,1)} %collective-permute-done.1.q_ref, s32[1152,1]{1,0:T(8,128)S(1)} %reshape.811.lo_ref, bf16[8,192,2496]{2,1,0:T(8,128)(2,1)} %bitcast.84), custom_call_target="tpu_custom_call" | custom-call | tf_op jit(solution)/shard_map/pallas_call | solution.py:141
  152.0 5.1 %shard_map.69 = bf16[1152,96]{1,0:T(8,128)(2,1)S(1)} custom-call(s32[24]{0:T(128)S(1)} %reshape.526.table_ref, bf16[1152,96]{1,0:T(8,128)(2,1)S(1)} %get-tuple-element.81.q_ref, s32[1152,1]{1,0:T(8,128)S(1)} %slice.166.lo_ref, bf16[8,192,2496]{2,1,0:T(8,128)(2,1)} %bitcast.85, f32[1152,1]{1,0:T(8,128)S(1)} %get-tuple-element.17.rest_0_, ...), custom_call_target="tpu_custom_call" | custom-call | tf_op jit(solution)/shard_map/pallas_call | solution.py:141
  157.3 1.0 copy.147
  158.3 1.2 slice.180
  160.3 136.9 %all-gather.4.cloned.1.call-done = bf16[2304,3072]{0,1:T(8,128)(2,1)} async-done(((bf16[2304,96]{0,1:T(8,128)(2,1)}), bf16[2304,3072]{0,1:T(8,128)(2,1)}) %all-gather.4.cloned.1.call-update) | async-done | bytes 14155792 | tf_op jit(solution)/shard_map/all_gather | solution.py:228
  297.2 7.6 %fusion = bf16[2304,96]{0,1:T(8,128)(2,1)S(1)} fusion(bf16[2304,3072]{0,1:T(8,128)(2,1)} %all-gather.4.cloned.1.call-done, bf16[3072,96]{1,0:T(8,128)(2,1)S(1)} %reshape.529, bf16[1152,96]{0,1:T(8,128)(2,1)} %collective-permute-done.2, bf16[1152,96]{0,1:T(8,128)(2,1)S(1)} %copy-done.11), kind=kOutput, calls=%fused_computation.3 | convolution fusion | flops 1360281600 | bytes 15630336 | tf_op jit(solution)/shard_map/dot_general | solution.py:227
  304.8 3.1 collective-permute-start.3
  308.0 2.5 reshape.530
  310.5 7.8 %collective-permute-done.3 = bf16[1152,96]{0,1:T(8,128)(2,1)S(1)} collective-permute-done((bf16[1152,96]{0,1:T(8,128)(2,1)S(1)}, bf16[1152,96]{0,1:T(8,128)(2,1)S(1)}, u32[]{:S(2)}, u32[]{:S(2)}) %collective-permute-start.3) | collective-permute-done | bytes 221216 | tf_op jit(solution)/shard_map/ppermute | solution.py:234
  (108 shorter events, 14.5 us)
Async XLA Ops:
  7.2 73.3 %copy-start = (s32[1169]{0:T(1024)S(1)}, s32[1169]{0:T(1024)}, u32[]{:S(2)}) copy-start(s32[1169]{0:T(1024)} %param.6) | copy-start | bytes 14032
  7.2 133.4 %all-gather.6.cloned.1.call-start = ((), (), s32[]{:S(2)}) async-start(), calls=%async_computation.1 | async-start | bytes 8847360 | tf_op jit(solution)/shard_map/all_gather | solution.py:173
  16.9 15.5 %copy-start.5 = (bf16[2304,1,96]{0,2,1:T(8,128)(2,1)}, bf16[2304,1,96]{0,2,1:T(8,128)(2,1)S(1)}, u32[]{:S(2)}) copy-start(bf16[2304,1,96]{0,2,1:T(8,128)(2,1)S(1)} %get-tuple-element.75) | copy-start | bytes 1327108
  31.5 3.0 copy-start.7
  34.5 1.1 copy-start.10
  35.5 261.7 %all-gather.4.cloned.1.call-start = ((), (), s32[]{:S(2)}) async-start(), calls=%async_computation | async-start | bytes 14598144 | tf_op jit(solution)/shard_map/all_gather | solution.py:228
  36.4 87.3 %collective-permute-start.2 = (bf16[1152,96]{0,1:T(8,128)(2,1)}, bf16[1152,96]{0,1:T(8,128)(2,1)}, u32[]{:S(2)}, u32[]{:S(2)}) collective-permute-start(bf16[1152,96]{0,1:T(8,128)(2,1)} %get-tuple-element.88), channel_id=1, source_target_pairs={{0,224},{32,192},{64,160},{96,128},{128,96},{160,64},{192,32},{224... | collective-permute-start | bytes 663560 | tf_op jit(solution)/shard_map/ppermute | solution.py:190
  43.8 79.9 %collective-permute-start.1 = (bf16[1152,96]{1,0:T(8,128)(2,1)}, bf16[1152,96]{1,0:T(8,128)(2,1)}, u32[]{:S(2)}, u32[]{:S(2)}) collective-permute-start(bf16[1152,96]{1,0:T(8,128)(2,1)} %get-tuple-element.80), channel_id=1, source_target_pairs={{0,224},{32,192},{64,160},{96,128},{128,96},{160,64},{192,32},{224... | collective-permute-start | bytes 663560 | tf_op jit(solution)/shard_map/ppermute | solution.py:189
  45.2 59.8 %collective-permute-start = (bf16[15,1,192]{0,2,1:T(8,128)(2,1)}, bf16[15,1,192]{0,2,1:T(8,128)(2,1)}, u32[]{:S(2)}, u32[]{:S(2)}) collective-permute-start(bf16[15,1,192]{0,2,1:T(8,128)(2,1)} %slice.173), channel_id=1, source_target_pairs={{32,0},{64,32},{96,64},{128,96},{160,128},{192,160},{224,192},{33,... | collective-permute-start | bytes 17288 | tf_op jit(solution)/shard_map/ppermute | solution.py:21
  80.5 12.9 %copy-start.12 = (s32[2]{0:T(128)S(1)}, s32[2]{0:T(128)}, u32[]{:S(2)}) copy-start(s32[2]{0:T(128)} %constant.155) | copy-start | bytes 28
  80.5 13.0 %copy-start.13 = (s32[2]{0:T(128)S(1)}, s32[2]{0:T(128)}, u32[]{:S(2)}) copy-start(s32[2]{0:T(128)} %constant.158) | copy-start | bytes 28
  96.8 8.3 %copy-start.6 = (bf16[2304,1,96]{0,2,1:T(8,128)(2,1)S(1)}, bf16[2304,1,96]{0,2,1:T(8,128)(2,1)}, u32[]{:S(2)}) copy-start(bf16[2304,1,96]{0,2,1:T(8,128)(2,1)} %copy-done.5) | copy-start | bytes 1327108
  97.0 0.7 copy-start.3
  97.7 7.4 %copy-start.8 = (bf16[2304,1,48]{0,2,1:T(8,128)(2,1)S(1)}, bf16[2304,1,48]{0,2,1:T(8,128)(2,1)}, u32[]{:S(2)}) copy-start(bf16[2304,1,48]{0,2,1:T(8,128)(2,1)} %copy-done.7) | copy-start | bytes 663556
  97.7 7.4 %copy-start.9 = (bf16[2304,1,48]{0,2,1:T(8,128)(2,1)S(1)}, bf16[2304,1,48]{0,2,1:T(8,128)(2,1)}, u32[]{:S(2)}) copy-start(bf16[2304,1,48]{0,2,1:T(8,128)(2,1)} %copy.125) | copy-start | bytes 663556
  104.3 0.8 copy-start.1
  140.6 11.4 %copy-start.2 = (f32[1152,96]{1,0:T(8,128)S(1)}, f32[1152,96]{1,0:T(8,128)}, u32[]{:S(2)}) copy-start(f32[1152,96]{1,0:T(8,128)} %copy-done.1) | copy-start | bytes 1327108
  159.5 137.7 %copy-start.11 = (bf16[1152,96]{0,1:T(8,128)(2,1)S(1)}, bf16[1152,96]{0,1:T(8,128)(2,1)}, u32[]{:S(2)}) copy-start(bf16[1152,96]{0,1:T(8,128)(2,1)} %get-tuple-element.87) | copy-start | bytes 663556
  297.2 10.8 %copy-start.4 = (bf16[2576,192]{1,0:T(8,128)(2,1)S(1)}, bf16[2576,192]{1,0:T(8,128)(2,1)}, u32[]{:S(2)}) copy-start(bf16[2576,192]{1,0:T(8,128)(2,1)} %scatter_custom_fusion) | copy-start | bytes 2967556
  304.8 13.4 %collective-permute-start.3 = (bf16[1152,96]{0,1:T(8,128)(2,1)S(1)}, bf16[1152,96]{0,1:T(8,128)(2,1)S(1)}, u32[]{:S(2)}, u32[]{:S(2)}) collective-permute-start(bf16[1152,96]{0,1:T(8,128)(2,1)S(1)} %get-tuple-element.86), channel_id=1, source_target_pairs={{0,224},{32,192},{64,160},{96,128},{128,96},{160,64},{192,32},{224... | collective-permute-start | bytes 663560 | tf_op jit(solution)/shard_map/ppermute | solution.py:234
Sparse Core Ops, SparseCore 0:
  35.6 104.8 all-gather.5
  158.4 138.6 all-gather.3

commit v8 on v7

--- a/solution.py
+++ b/solution.py
@@ -11,7 +11,7 @@
 HD = 96
 PAGE = 16
 BQ = 384
-BK = 1152
+BK = 384
 NEG = -1e30
 
 

time: 327 us -> 360 us (1.10)
  waiting for transfers between devices: 162 us -> 201 us
  Pallas kernels: 23.1 us -> 18.7 us
    all_gather x1, waiting for transfers between devices: 137 us -> 175 us  [per_device(): lax.all_gather(both, 'gy', axis=1, tiled=True)]
    pallas_call x3, Pallas kernels: 23.1 us -> 18.7 us  [attend(): pl.pallas_call(kernel, grid_spec=pltpu.PrefetchScalarGridSpec(num_scalar_...]
  transfers between devices with their start and end apart: 6 -> 6, of which waited for: 3 -> 3; matrix products, arithmetic and copies ran while one was open for 23% -> 21% of each run, Pallas kernels for 2% -> 1%
where the time goes in v8:
time: 360 us; the launch traced here: 361 us
  waiting for transfers between devices  201 us (56%)
  other arithmetic  58.6 us (16%)
  local copies, waits for them, and re-layouts  49.3 us (14%)
  Pallas kernels  18.7 us (5%)
  between operations  14.5 us (4%)
  starting transfers between devices  11.1 us (3%)
  matrix products  7.59 us (2%)
    all_gather x1, waiting for transfers between devices, per_device(): lax.all_gather(both, 'gy', axis=1, tiled=True)  175 us
    pallas_call x3, Pallas kernels, attend(): pl.pallas_call(kernel, grid_spec=pltpu.PrefetchScalarGridSpec(num_scalar_...  18.7 us
    all_gather x1, waiting for transfers between devices, per_device(): lax.all_gather(jnp.concatenate([local_kv, weight_rows], axis=0), 'gx', ax...  18.4 us
    unnamed x32, local copies, waits for them, and re-layouts  17.6 us
    gather x2, other arithmetic, per_device(): logical = page_base[extended_segment] + extended_position // PAGE  14.9 us
    gather x1, local copies, waits for them, and re-layouts, per_device(): page_table[logical] - group_index * pages_held  12.7 us
    gather x3, other arithmetic, per_device(): partner_lows = starts_at[segment_of(ends_at, partner_index)]  10.6 us
    ppermute x1, waiting for transfers between devices, per_device(): hidden_second = lax.ppermute(projected[half:], 'gx', partners)  7.78 us
  transfers between devices with their start and end apart: 6, of which 3 were waited for; matrix products, arithmetic and copies ran while one was open for 21% of the time, Pallas kernels for 1%

profile of v8, /device:TPU:1, one launch (start us, length us, event | category | flops | bytes accessed | tf_op | source)
XLA Modules:
  0.0 360.7 jit_solution(3904167776551343757)
XLA Ops:
  9.7 4.4 %fusion.25 = (s32[2304]{0:T(1024)S(1)}, s32[2304,1]{0,1:T(1,128)S(1)}) fusion(s32[]{:T(128)} %bitcast.13, s32[]{:T(128)} %bitcast.14, s32[]{:T(128)} %bitcast.15, s32[]{:T(128)} %bitcast.16, s32[]{:T(128)} %bitcast.17, s32[]{:T(128)} %bitcast.19, s32[]{:T(128)} %bitcast.18, s32[2304]{0:T(1024)S(1)} %convert_reduce_fusion.1), kind=kLoop, calls=%fused_computation.123 | loop fusion | flops 34560 | bytes 27676 | tf_op jit(solution)/shard_map/gather | solution.py:164
  14.3 1.0 copy.127
  15.5 1.4 fusion.41
  17.7 6.2 %subtract_convert_fusion = (f32[2304]{0:T(1024)S(1)}, s32[2304]{0:T(1024)S(1)}) fusion(s32[]{:T(128)S(6)} %mul.94, pred[2304]{0:T(1024)(128)(4,1)S(1)} %get-tuple-element.43, pred[2304]{0:T(1024)(128)(4,1)S(1)} %get-tuple-element.42, pred[2304]{0:T(1024)(128)(4,1)S(1)} %get-tuple-element.41, pred[2304]{0:T(1024)(128)(4,1)S(1)} %get-tuple-element.40, ...), kind=kLoop, calls=%fused_computation.116 | loop fusion | flops 29952 | bytes 50732 | tf_op jit(solution)/shard_map/convert_element_type | solution.py:31
  23.9 6.3 %fusion.16 = (bf16[2304,1,48]{2,0,1:T(8,128)(2,1)S(1)}, bf16[2304,1,48]{2,0,1:T(8,128)(2,1)S(1)}, bf16[2304,1,48]{2,0,1:T(8,128)(2,1)}, bf16[2304,1,48]{2,0,1:T(8,128)(2,1)S(1)}) fusion(f32[2304,1,96]{2,0,1:T(8,128)S(1)} %get-tuple-element.133, f32[2304]{0:T(1024)S(1)} %get-tuple-element.63, f32[48]{0:T(128)S(1)} %multiply_power_fusion, ...), kind=kLoop, calls=%fused_computation.21 | loop fusion | flops 1880064 | bytes 2663616 | tf_op jit(solution)/shard_map/convert.3
  30.2 1.3 copy.126
  32.4 2.0 fusion.36
  34.5 1.0 maximum_bitcast_fusion
  36.4 6.4 %collective-permute-start.2 = (bf16[1152,96]{0,1:T(8,128)(2,1)}, bf16[1152,96]{0,1:T(8,128)(2,1)}, u32[]{:S(2)}, u32[]{:S(2)}) collective-permute-start(bf16[1152,96]{0,1:T(8,128)(2,1)} %get-tuple-element.88), channel_id=1, source_target_pairs={{0,224},{32,192},{64,160},{96,128},{128,96},{160,64},{192,32},{224... | collective-permute-start | bytes 663560 | tf_op jit(solution)/shard_map/ppermute | solution.py:190
  42.8 1.0 fusion.21
  43.8 1.4 slice.173
  45.2 1.5 collective-permute-start
  46.8 4.3 %fusion.26 = (s32[1152]{0:T(1024)S(1)}, s32[1152,1]{0,1:T(1,128)S(1)}) fusion(s32[]{:T(128)} %bitcast.13, s32[]{:T(128)} %bitcast.14, s32[]{:T(128)} %bitcast.15, s32[]{:T(128)} %bitcast.16, s32[]{:T(128)} %bitcast.17, s32[]{:T(128)} %bitcast.19, s32[]{:T(128)} %bitcast.18, s32[1152]{0:T(1024)S(1)} %convert_reduce_fusion.2), kind=kLoop, calls=%fused_computation.129 | loop fusion | flops 17280 | bytes 13852 | tf_op jit(solution)/shard_map/gather | solution.py:193
  51.3 6.2 %select_select_fusion.3 = s32[1152]{0:T(1024)S(1)} fusion(pred[1152]{0:T(1024)(128)(4,1)S(1)} %get-tuple-element.53, pred[1152]{0:T(1024)(128)(4,1)S(1)} %get-tuple-element.52, pred[1152]{0:T(1024)(128)(4,1)S(1)} %get-tuple-element.51, pred[1152]{0:T(1024)(128)(4,1)S(1)} %get-tuple-element.50, pred[1152]{0:T(1024)(128)(4,1)S(1)} %get-tuple-element.49, ...), kind=kLoop, calls=%fused_computation.124 | loop fusion | flops 11520 | bytes 20776 | tf_op jit(solution)/shard_map/gather | solution.py:193
  59.0 8.7 %fusion.22 = (s32[2319]{0:T(1024)S(1)}, s32[2319]{0:T(1024)S(1)}, s32[2319,1]{0,1:T(1,128)S(1)}) fusion(s32[]{:T(128)} %bitcast.36, s32[]{:T(128)} %bitcast.37, s32[]{:T(128)} %bitcast.38, s32[]{:T(128)} %bitcast.39, s32[]{:T(128)} %bitcast.40, s32[]{:T(128)} %bitcast.42, s32[]{:T(128)} %bitcast.41, s32[]{:T(128)} %bitcast.19, s32[]{:T(128)} %bitcast.18, ...), kind=kLoop, calls=%fused_computation.118 | loop fusion | flops 48699 | bytes 37160 | tf_op jit(solution)/shard_map/gather | solution.py:210
  68.0 6.2 %select_select_fusion.1 = s32[2319]{0:T(1024)S(1)} fusion(pred[2319]{0:T(1024)(128)(4,1)S(1)} %get-tuple-element.33, pred[2319]{0:T(1024)(128)(4,1)S(1)} %get-tuple-element.32, pred[2319]{0:T(1024)(128)(4,1)S(1)} %get-tuple-element.31, pred[2319]{0:T(1024)(128)(4,1)S(1)} %get-tuple-element.30, pred[2319]{0:T(1024)(128)(4,1)S(1)} %get-tuple-element.29, ...), kind=kLoop, calls=%fused_computation.113 | loop fusion | flops 23190 | bytes 41782 | tf_op jit(solution)/shard_map/gather | solution.py:207
  74.1 6.2 %select_select_fusion = s32[2319]{0:T(1024)S(1)} fusion(pred[2319]{0:T(1024)(128)(4,1)S(1)} %get-tuple-element.33, pred[2319]{0:T(1024)(128)(4,1)S(1)} %get-tuple-element.32, pred[2319]{0:T(1024)(128)(4,1)S(1)} %get-tuple-element.31, pred[2319]{0:T(1024)(128)(4,1)S(1)} %get-tuple-element.30, pred[2319]{0:T(1024)(128)(4,1)S(1)} %get-tuple-element.29, ...), kind=kLoop, calls=%fused_computation.112 | loop fusion | flops 23190 | bytes 41782 | tf_op jit(solution)/shard_map/gather | solution.py:210
  80.5 12.7 %gather_fusion = s32[2319]{0:T(1024)S(1)} fusion(s32[1169]{0:T(1024)S(1)} %copy-done, s32[3072]{0:T(1024)S(1)} %pad_clamp_fusion), kind=kCustom, calls=%fused_computation | custom fusion | bytes 27828 | tf_op jit(solution)/shard_map/gather | solution.py:214
  97.7 5.0 %shard_map.68 = (f32[1152,1]{1,0:T(8,128)S(1)}, f32[1152,1]{1,0:T(8,128)S(1)}, f32[1152,96]{1,0:T(8,128)S(1)}) custom-call(s32[24]{0:T(128)S(1)} %copy-done.3, bf16[1152,96]{1,0:T(8,128)(2,1)S(1)} %get-tuple-element.81.q_ref, s32[1152,1]{1,0:T(8,128)S(1)} %slice.166.lo_ref, bf16[1,192,2304]{2,1,0:T(8,128)(2,1)S(1)} %get-tuple-element.82.kv_ref), custom_call_target="tpu_custom_call" | custom-call | tf_op jit(solution)/shard_map/pallas_call | solution.py:141
  103.6 1.9 maximum_bitcast_fusion.1
  105.4 2.3 copy.130
  107.7 14.4 %scatter_custom_fusion = bf16[2576,192]{1,0:T(8,128)(2,1)} fusion(s32[2319]{0:T(1024)} %broadcast_select_fusion, bf16[2319,192]{1,0:T(8,128)(2,1)} %copy.130, bf16[]{:T(256)} %constant.142.clone.1), kind=kCustom, calls=%fused_computation.25 | custom fusion | bytes 989696
  122.1 18.4 %all-gather.6.cloned.1.call-done = bf16[8,2496,192]{1,2,0:T(8,128)(2,1)} async-done(((bf16[1,2496,192]{1,2,0:T(8,128)(2,1)}), bf16[8,2496,192]{1,2,0:T(8,128)(2,1)}) %all-gather.6.cloned.1.call-update) | async-done | bytes 7667728 | tf_op jit(solution)/shard_map/all_gather | solution.py:173
  140.6 8.8 %shard_map.70 = bf16[1152,96]{1,0:T(8,128)(2,1)S(1)} custom-call(s32[24]{0:T(128)S(1)} %reshape.527.table_ref, bf16[1152,96]{1,0:T(8,128)(2,1)} %collective-permute-done.1.q_ref, s32[1152,1]{1,0:T(8,128)S(1)} %reshape.811.lo_ref, bf16[8,192,2496]{2,1,0:T(8,128)(2,1)} %bitcast.84), custom_call_target="tpu_custom_call" | custom-call | tf_op jit(solution)/shard_map/pallas_call | solution.py:141
  149.4 4.9 %shard_map.69 = bf16[1152,96]{1,0:T(8,128)(2,1)S(1)} custom-call(s32[24]{0:T(128)S(1)} %reshape.526.table_ref, bf16[1152,96]{1,0:T(8,128)(2,1)S(1)} %get-tuple-element.81.q_ref, s32[1152,1]{1,0:T(8,128)S(1)} %slice.166.lo_ref, bf16[8,192,2496]{2,1,0:T(8,128)(2,1)} %bitcast.85, f32[1152,1]{1,0:T(8,128)S(1)} %get-tuple-element.17.rest_0_, ...), custom_call_target="tpu_custom_call" | custom-call | tf_op jit(solution)/shard_map/pallas_call | solution.py:141
  154.4 1.0 copy.147
  155.5 1.2 slice.180
  157.4 174.6 %all-gather.4.cloned.1.call-done = bf16[2304,3072]{0,1:T(8,128)(2,1)} async-done(((bf16[2304,96]{0,1:T(8,128)(2,1)}), bf16[2304,3072]{0,1:T(8,128)(2,1)}) %all-gather.4.cloned.1.call-update) | async-done | bytes 14155792 | tf_op jit(solution)/shard_map/all_gather | solution.py:228
  332.0 7.6 %fusion = bf16[2304,96]{0,1:T(8,128)(2,1)S(1)} fusion(bf16[2304,3072]{0,1:T(8,128)(2,1)} %all-gather.4.cloned.1.call-done, bf16[3072,96]{1,0:T(8,128)(2,1)S(1)} %reshape.529, bf16[1152,96]{0,1:T(8,128)(2,1)} %collective-permute-done.2, bf16[1152,96]{0,1:T(8,128)(2,1)S(1)} %copy-done.11), kind=kOutput, calls=%fused_computation.3 | convolution fusion | flops 1360281600 | bytes 15630336 | tf_op jit(solution)/shard_map/dot_general | solution.py:227
  339.6 3.1 collective-permute-start.3
  342.8 2.5 reshape.530
  345.3 7.8 %collective-permute-done.3 = bf16[1152,96]{0,1:T(8,128)(2,1)S(1)} collective-permute-done((bf16[1152,96]{0,1:T(8,128)(2,1)S(1)}, bf16[1152,96]{0,1:T(8,128)(2,1)S(1)}, u32[]{:S(2)}, u32[]{:S(2)}) %collective-permute-start.3) | collective-permute-done | bytes 221216 | tf_op jit(solution)/shard_map/ppermute | solution.py:234
  (108 shorter events, 14.5 us)
Async XLA Ops:
  7.2 73.3 %copy-start = (s32[1169]{0:T(1024)S(1)}, s32[1169]{0:T(1024)}, u32[]{:S(2)}) copy-start(s32[1169]{0:T(1024)} %param.6) | copy-start | bytes 14032
  7.2 133.4 %all-gather.6.cloned.1.call-start = ((), (), s32[]{:S(2)}) async-start(), calls=%async_computation.1 | async-start | bytes 8847360 | tf_op jit(solution)/shard_map/all_gather | solution.py:173
  16.9 15.5 %copy-start.5 = (bf16[2304,1,96]{0,2,1:T(8,128)(2,1)}, bf16[2304,1,96]{0,2,1:T(8,128)(2,1)S(1)}, u32[]{:S(2)}) copy-start(bf16[2304,1,96]{0,2,1:T(8,128)(2,1)S(1)} %get-tuple-element.75) | copy-start | bytes 1327108
  31.5 3.0 copy-start.7
  34.5 1.1 copy-start.10
  35.5 296.5 %all-gather.4.cloned.1.call-start = ((), (), s32[]{:S(2)}) async-start(), calls=%async_computation | async-start | bytes 14598144 | tf_op jit(solution)/shard_map/all_gather | solution.py:228
  36.4 85.7 %collective-permute-start.2 = (bf16[1152,96]{0,1:T(8,128)(2,1)}, bf16[1152,96]{0,1:T(8,128)(2,1)}, u32[]{:S(2)}, u32[]{:S(2)}) collective-permute-start(bf16[1152,96]{0,1:T(8,128)(2,1)} %get-tuple-element.88), channel_id=1, source_target_pairs={{0,224},{32,192},{64,160},{96,128},{128,96},{160,64},{192,32},{224... | collective-permute-start | bytes 663560 | tf_op jit(solution)/shard_map/ppermute | solution.py:190
  43.8 78.3 %collective-permute-start.1 = (bf16[1152,96]{1,0:T(8,128)(2,1)}, bf16[1152,96]{1,0:T(8,128)(2,1)}, u32[]{:S(2)}, u32[]{:S(2)}) collective-permute-start(bf16[1152,96]{1,0:T(8,128)(2,1)} %get-tuple-element.80), channel_id=1, source_target_pairs={{0,224},{32,192},{64,160},{96,128},{128,96},{160,64},{192,32},{224... | collective-permute-start | bytes 663560 | tf_op jit(solution)/shard_map/ppermute | solution.py:189
  45.2 58.3 %collective-permute-start = (bf16[15,1,192]{0,2,1:T(8,128)(2,1)}, bf16[15,1,192]{0,2,1:T(8,128)(2,1)}, u32[]{:S(2)}, u32[]{:S(2)}) collective-permute-start(bf16[15,1,192]{0,2,1:T(8,128)(2,1)} %slice.173), channel_id=1, source_target_pairs={{32,0},{64,32},{96,64},{128,96},{160,128},{192,160},{224,192},{33,... | collective-permute-start | bytes 17288 | tf_op jit(solution)/shard_map/ppermute | solution.py:21
  80.5 12.9 %copy-start.12 = (s32[2]{0:T(128)S(1)}, s32[2]{0:T(128)}, u32[]{:S(2)}) copy-start(s32[2]{0:T(128)} %constant.155) | copy-start | bytes 28
  80.5 13.0 %copy-start.13 = (s32[2]{0:T(128)S(1)}, s32[2]{0:T(128)}, u32[]{:S(2)}) copy-start(s32[2]{0:T(128)} %constant.158) | copy-start | bytes 28
  96.8 6.7 %copy-start.6 = (bf16[2304,1,96]{0,2,1:T(8,128)(2,1)S(1)}, bf16[2304,1,96]{0,2,1:T(8,128)(2,1)}, u32[]{:S(2)}) copy-start(bf16[2304,1,96]{0,2,1:T(8,128)(2,1)} %copy-done.5) | copy-start | bytes 1327108
  97.0 0.7 copy-start.3
  97.7 5.9 %copy-start.8 = (bf16[2304,1,48]{0,2,1:T(8,128)(2,1)S(1)}, bf16[2304,1,48]{0,2,1:T(8,128)(2,1)}, u32[]{:S(2)}) copy-start(bf16[2304,1,48]{0,2,1:T(8,128)(2,1)} %copy-done.7) | copy-start | bytes 663556
  97.7 5.9 %copy-start.9 = (bf16[2304,1,48]{0,2,1:T(8,128)(2,1)S(1)}, bf16[2304,1,48]{0,2,1:T(8,128)(2,1)}, u32[]{:S(2)}) copy-start(bf16[2304,1,48]{0,2,1:T(8,128)(2,1)} %copy.125) | copy-start | bytes 663556
  102.7 0.8 copy-start.1
  140.6 8.8 %copy-start.2 = (f32[1152,96]{1,0:T(8,128)S(1)}, f32[1152,96]{1,0:T(8,128)}, u32[]{:S(2)}) copy-start(f32[1152,96]{1,0:T(8,128)} %copy-done.1) | copy-start | bytes 1327108
  156.7 175.3 %copy-start.11 = (bf16[1152,96]{0,1:T(8,128)(2,1)S(1)}, bf16[1152,96]{0,1:T(8,128)(2,1)}, u32[]{:S(2)}) copy-start(bf16[1152,96]{0,1:T(8,128)(2,1)} %get-tuple-element.87) | copy-start | bytes 663556
  332.0 10.8 %copy-start.4 = (bf16[2576,192]{1,0:T(8,128)(2,1)S(1)}, bf16[2576,192]{1,0:T(8,128)(2,1)}, u32[]{:S(2)}) copy-start(bf16[2576,192]{1,0:T(8,128)(2,1)} %scatter_custom_fusion) | copy-start | bytes 2967556
  339.6 13.4 %collective-permute-start.3 = (bf16[1152,96]{0,1:T(8,128)(2,1)S(1)}, bf16[1152,96]{0,1:T(8,128)(2,1)S(1)}, u32[]{:S(2)}, u32[]{:S(2)}) collective-permute-start(bf16[1152,96]{0,1:T(8,128)(2,1)S(1)} %get-tuple-element.86), channel_id=1, source_target_pairs={{0,224},{32,192},{64,160},{96,128},{128,96},{160,64},{192,32},{224... | collective-permute-start | bytes 663560 | tf_op jit(solution)/shard_map/ppermute | solution.py:234
Sparse Core Ops, SparseCore 0:
  35.6 104.8 all-gather.5
  155.6 176.3 all-gather.3

commit v9 on v6

--- a/solution.py
+++ b/solution.py
@@ -220,10 +220,20 @@
         (key_columns, cache_pages, state, partner_queries, partner_residual)
     )
     rest_table = block_table(q_first_rows, lo_first, lo_last, jnp.int32(0), jnp.minimum(first_row, key_count))
-    first_half = attend(rest_table, queries[:half], lows[:half], key_columns, state, True, row_count)
-    partner_out = attend(partner_table, partner_queries, partner_lows, key_columns, None, True, row_count)
-
-    both = jnp.concatenate([first_half, partner_out], axis=0)
+    fresh = (
+        jnp.full((half, 1), NEG, jnp.float32),
+        jnp.zeros((half, 1), jnp.float32),
+        jnp.zeros((half, HD), jnp.float32),
+    )
+    both = attend(
+        jnp.concatenate([rest_table, partner_table]),
+        jnp.concatenate([queries[:half], partner_queries], axis=0),
+        jnp.concatenate([lows[:half], partner_lows], axis=0),
+        key_columns,
+        tuple(jnp.concatenate([mine, new], axis=0) for mine, new in zip(state, fresh)),
+        True,
+        row_count,
+    )
     update = jnp.dot(
         lax.all_gather(both, "gy", axis=1, tiled=True),
         weight_columns,

time: 312 us -> 317 us (1.016)
  waiting for transfers between devices: 93.7 us -> 111 us
  Pallas kernels: 76.2 us -> 61.6 us
    all_gather x1, waiting for transfers between devices: 68.3 us -> 85.8 us  [per_device(): lax.all_gather(both, 'gy', axis=1, tiled=True)]
    pallas_call x3 -> x2, Pallas kernels: 76.2 us -> 61.6 us  [attend(): pl.pallas_call(kernel, grid_spec=pltpu.PrefetchScalarGridSpec(num_scalar_...]
    unnamed x32 -> x34, local copies, waits for them, and re-layouts: 17.6 us -> 18.7 us
  transfers between devices with their start and end apart: 6 -> 6, of which waited for: 3 -> 3; matrix products, arithmetic and copies ran while one was open for 25% -> 24% of each run, Pallas kernels for 2% -> 2%
where the time goes in v9:
time: 317 us; the launch traced here: 316 us
  waiting for transfers between devices  111 us (35%)
  Pallas kernels  61.6 us (19%)
  other arithmetic  60 us (19%)
  local copies, waits for them, and re-layouts  50.4 us (16%)
  between operations  14.5 us (5%)
  starting transfers between devices  11.1 us (4%)
  matrix products  7.59 us (2%)
    all_gather x1, waiting for transfers between devices, per_device(): lax.all_gather(both, 'gy', axis=1, tiled=True)  85.8 us
    pallas_call x2, Pallas kernels, attend(): pl.pallas_call(kernel, grid_spec=pltpu.PrefetchScalarGridSpec(num_scalar_...  61.6 us
    unnamed x34, local copies, waits for them, and re-layouts  18.7 us
    all_gather x1, waiting for transfers between devices, per_device(): lax.all_gather(jnp.concatenate([local_kv, weight_rows], axis=0), 'gx', ax...  17.4 us
    gather x2, other arithmetic, per_device(): logical = page_base[extended_segment] + extended_position // PAGE  15.1 us
    gather x1, local copies, waits for them, and re-layouts, per_device(): page_table[logical] - group_index * pages_held  12.7 us
    gather x3, other arithmetic, per_device(): partner_lows = starts_at[segment_of(ends_at, partner_index)]  10.8 us
    ppermute x1, waiting for transfers between devices, per_device(): hidden_second = lax.ppermute(projected[half:], 'gx', partners)  7.78 us
  transfers between devices with their start and end apart: 6, of which 3 were waited for; matrix products, arithmetic and copies ran while one was open for 24% of the time, Pallas kernels for 2%

profile of v9, /device:TPU:1, one launch (start us, length us, event | category | flops | bytes accessed | tf_op | source)
XLA Modules:
  0.0 316.2 jit_solution(3317891257651755747)
XLA Ops:
  9.7 4.5 %fusion.25 = (s32[2304]{0:T(1024)S(1)}, s32[2304,1]{0,1:T(1,128)S(1)}) fusion(s32[]{:T(128)} %bitcast.13, s32[]{:T(128)} %bitcast.14, s32[]{:T(128)} %bitcast.15, s32[]{:T(128)} %bitcast.16, s32[]{:T(128)} %bitcast.17, s32[]{:T(128)} %bitcast.19, s32[]{:T(128)} %bitcast.18, s32[2304]{0:T(1024)S(1)} %convert_reduce_fusion.1), kind=kLoop, calls=%fused_computation.123 | loop fusion | flops 34560 | bytes 27676 | tf_op jit(solution)/shard_map/gather | solution.py:164
  14.4 1.0 copy.122
  15.6 1.4 fusion.41
  17.8 6.2 %subtract_convert_fusion = (f32[2304]{0:T(1024)S(1)}, s32[2304]{0:T(1024)S(1)}) fusion(s32[]{:T(128)S(6)} %mul.94, pred[2304]{0:T(1024)(128)(4,1)S(1)} %get-tuple-element.43, pred[2304]{0:T(1024)(128)(4,1)S(1)} %get-tuple-element.42, pred[2304]{0:T(1024)(128)(4,1)S(1)} %get-tuple-element.41, pred[2304]{0:T(1024)(128)(4,1)S(1)} %get-tuple-element.40, ...), kind=kLoop, calls=%fused_computation.116 | loop fusion | flops 29952 | bytes 50732 | tf_op jit(solution)/shard_map/convert_element_type | solution.py:31
  24.0 6.3 %fusion.16 = (bf16[2304,1,48]{2,0,1:T(8,128)(2,1)S(1)}, bf16[2304,1,48]{2,0,1:T(8,128)(2,1)S(1)}, bf16[2304,1,48]{2,0,1:T(8,128)(2,1)}, bf16[2304,1,48]{2,0,1:T(8,128)(2,1)S(1)}) fusion(f32[2304,1,96]{2,0,1:T(8,128)S(1)} %get-tuple-element.133, f32[2304]{0:T(1024)S(1)} %get-tuple-element.59, f32[48]{0:T(128)S(1)} %multiply_power_fusion, ...), kind=kLoop, calls=%fused_computation.21 | loop fusion | flops 1880064 | bytes 2663616 | tf_op jit(solution)/shard_map/convert.3
  30.3 1.3 copy.121
  32.6 2.0 fusion.36
  34.6 1.0 maximum_bitcast_fusion
  36.5 6.4 %collective-permute-start.2 = (bf16[1152,96]{0,1:T(8,128)(2,1)}, bf16[1152,96]{0,1:T(8,128)(2,1)}, u32[]{:S(2)}, u32[]{:S(2)}) collective-permute-start(bf16[1152,96]{0,1:T(8,128)(2,1)} %get-tuple-element.88), channel_id=1, source_target_pairs={{0,224},{32,192},{64,160},{96,128},{128,96},{160,64},{192,32},{224... | collective-permute-start | bytes 663560 | tf_op jit(solution)/shard_map/ppermute | solution.py:190
  42.9 1.0 fusion.21
  43.9 1.4 slice.172
  45.4 1.5 collective-permute-start
  46.9 4.5 %fusion.26 = (s32[1152]{0:T(1024)S(1)}, s32[1152,1]{0,1:T(1,128)S(1)}) fusion(s32[]{:T(128)} %bitcast.13, s32[]{:T(128)} %bitcast.14, s32[]{:T(128)} %bitcast.15, s32[]{:T(128)} %bitcast.16, s32[]{:T(128)} %bitcast.17, s32[]{:T(128)} %bitcast.19, s32[]{:T(128)} %bitcast.18, s32[1152]{0:T(1024)S(1)} %convert_reduce_fusion.2), kind=kLoop, calls=%fused_computation.130 | loop fusion | flops 17280 | bytes 13852 | tf_op jit(solution)/shard_map/gather | solution.py:193
  51.6 6.2 %select_select_fusion.3 = s32[1152]{0:T(1024)S(1)} fusion(pred[1152]{0:T(1024)(128)(4,1)S(1)} %get-tuple-element.53, pred[1152]{0:T(1024)(128)(4,1)S(1)} %get-tuple-element.52, pred[1152]{0:T(1024)(128)(4,1)S(1)} %get-tuple-element.51, pred[1152]{0:T(1024)(128)(4,1)S(1)} %get-tuple-element.50, pred[1152]{0:T(1024)(128)(4,1)S(1)} %get-tuple-element.49, ...), kind=kLoop, calls=%fused_computation.125 | loop fusion | flops 11520 | bytes 20776 | tf_op jit(solution)/shard_map/gather | solution.py:193
  60.4 8.8 %fusion.22 = (s32[2319]{0:T(1024)S(1)}, s32[2319]{0:T(1024)S(1)}, s32[2319,1]{0,1:T(1,128)S(1)}) fusion(s32[]{:T(128)} %bitcast.36, s32[]{:T(128)} %bitcast.37, s32[]{:T(128)} %bitcast.38, s32[]{:T(128)} %bitcast.39, s32[]{:T(128)} %bitcast.40, s32[]{:T(128)} %bitcast.42, s32[]{:T(128)} %bitcast.41, s32[]{:T(128)} %bitcast.19, s32[]{:T(128)} %bitcast.18, ...), kind=kLoop, calls=%fused_computation.118 | loop fusion | flops 48699 | bytes 37160 | tf_op jit(solution)/shard_map/gather | solution.py:210
  69.5 6.2 %select_select_fusion.1 = s32[2319]{0:T(1024)S(1)} fusion(pred[2319]{0:T(1024)(128)(4,1)S(1)} %get-tuple-element.33, pred[2319]{0:T(1024)(128)(4,1)S(1)} %get-tuple-element.32, pred[2319]{0:T(1024)(128)(4,1)S(1)} %get-tuple-element.31, pred[2319]{0:T(1024)(128)(4,1)S(1)} %get-tuple-element.30, pred[2319]{0:T(1024)(128)(4,1)S(1)} %get-tuple-element.29, ...), kind=kLoop, calls=%fused_computation.113 | loop fusion | flops 23190 | bytes 41782 | tf_op jit(solution)/shard_map/gather | solution.py:207
  75.7 6.2 %select_select_fusion = s32[2319]{0:T(1024)S(1)} fusion(pred[2319]{0:T(1024)(128)(4,1)S(1)} %get-tuple-element.33, pred[2319]{0:T(1024)(128)(4,1)S(1)} %get-tuple-element.32, pred[2319]{0:T(1024)(128)(4,1)S(1)} %get-tuple-element.31, pred[2319]{0:T(1024)(128)(4,1)S(1)} %get-tuple-element.30, pred[2319]{0:T(1024)(128)(4,1)S(1)} %get-tuple-element.29, ...), kind=kLoop, calls=%fused_computation.112 | loop fusion | flops 23190 | bytes 41782 | tf_op jit(solution)/shard_map/gather | solution.py:210
  82.1 12.7 %gather_fusion = s32[2319]{0:T(1024)S(1)} fusion(s32[1169]{0:T(1024)S(1)} %copy-done, s32[3072]{0:T(1024)S(1)} %pad_clamp_fusion), kind=kCustom, calls=%fused_computation | custom fusion | bytes 27828 | tf_op jit(solution)/shard_map/gather | solution.py:214
  97.2 5.9 %shard_map.68 = (f32[1152,1]{1,0:T(8,128)S(1)}, f32[1152,1]{1,0:T(8,128)S(1)}, f32[1152,96]{1,0:T(8,128)S(1)}) custom-call(s32[24]{0:T(128)S(1)} %reshape.525.table_ref, bf16[1152,96]{1,0:T(8,128)(2,1)S(1)} %get-tuple-element.81.q_ref, s32[1152,1]{1,0:T(8,128)S(1)} %copy.131.lo_ref, bf16[1,192,2304]{2,1,0:T(8,128)(2,1)S(1)} %get-tuple-element.82.kv_ref), custom_call_target="tpu_custom_call" | custom-call | tf_op jit(solution)/shard_map/pallas_call | solution.py:141
  104.7 1.9 maximum_bitcast_fusion.1
  106.5 2.3 copy.125
  108.9 14.4 %scatter_custom_fusion = bf16[2576,192]{1,0:T(8,128)(2,1)} fusion(s32[2319]{0:T(1024)} %broadcast_select_fusion, bf16[2319,192]{1,0:T(8,128)(2,1)} %copy.125, bf16[]{:T(256)} %constant.146.clone.1), kind=kCustom, calls=%fused_computation.25 | custom fusion | bytes 989696
  123.3 17.4 %all-gather.6.cloned.1.call-done = bf16[8,2496,192]{1,2,0:T(8,128)(2,1)} async-done(((bf16[1,2496,192]{1,2,0:T(8,128)(2,1)}), bf16[8,2496,192]{1,2,0:T(8,128)(2,1)}) %all-gather.6.cloned.1.call-update) | async-done | bytes 7667728 | tf_op jit(solution)/shard_map/all_gather | solution.py:173
  140.7 1.1 pad_maximum_fusion.1.q_ref
  143.0 55.8 %shard_map.69 = bf16[2304,96]{1,0:T(8,128)(2,1)S(1)} custom-call(s32[48]{0:T(128)S(1)} %pad_add_fusion.2.table_ref, bf16[2304,96]{1,0:T(8,128)(2,1)S(1)} %pad_maximum_fusion.1.q_ref, s32[2304,1]{1,0:T(8,128)S(1)} %copy.140.lo_ref, bf16[8,192,2496]{2,1,0:T(8,128)(2,1)} %bitcast.84, f32[2304,1]{1,0:T(8,128)S(1)} %concatenate.68.rest_0_, ...), custom_call_target="tpu_custom_call" | custom-call | tf_op jit(solution)/shard_map/pallas_call | solution.py:141
  198.8 1.0 copy.141
  199.8 1.2 slice.179
  201.8 85.8 %all-gather.4.cloned.1.call-done = bf16[2304,3072]{0,1:T(8,128)(2,1)} async-done(((bf16[2304,96]{0,1:T(8,128)(2,1)}), bf16[2304,3072]{0,1:T(8,128)(2,1)}) %all-gather.4.cloned.1.call-update) | async-done | bytes 14155792 | tf_op jit(solution)/shard_map/all_gather | solution.py:238
  287.6 7.6 %fusion = bf16[2304,96]{0,1:T(8,128)(2,1)S(1)} fusion(bf16[2304,3072]{0,1:T(8,128)(2,1)} %all-gather.4.cloned.1.call-done, bf16[3072,96]{1,0:T(8,128)(2,1)S(1)} %reshape.529, bf16[1152,96]{0,1:T(8,128)(2,1)} %collective-permute-done.2, bf16[1152,96]{0,1:T(8,128)(2,1)S(1)} %copy-done.12), kind=kOutput, calls=%fused_computation.3 | convolution fusion | flops 1360281600 | bytes 15630336 | tf_op jit(solution)/shard_map/dot_general | solution.py:237
  295.2 3.1 collective-permute-start.3
  298.3 2.5 reshape.530
  300.8 7.8 %collective-permute-done.3 = bf16[1152,96]{0,1:T(8,128)(2,1)S(1)} collective-permute-done((bf16[1152,96]{0,1:T(8,128)(2,1)S(1)}, bf16[1152,96]{0,1:T(8,128)(2,1)S(1)}, u32[]{:S(2)}, u32[]{:S(2)}) %collective-permute-start.3) | collective-permute-done | bytes 221216 | tf_op jit(solution)/shard_map/ppermute | solution.py:244
  (116 shorter events, 15.4 us)
Async XLA Ops:
  7.2 74.9 %copy-start = (s32[1169]{0:T(1024)S(1)}, s32[1169]{0:T(1024)}, u32[]{:S(2)}) copy-start(s32[1169]{0:T(1024)} %param.6) | copy-start | bytes 14032
  7.2 133.5 %all-gather.6.cloned.1.call-start = ((), (), s32[]{:S(2)}) async-start(), calls=%async_computation.1 | async-start | bytes 8847360 | tf_op jit(solution)/shard_map/all_gather | solution.py:173
  17.0 15.5 %copy-start.6 = (bf16[2304,1,96]{0,2,1:T(8,128)(2,1)}, bf16[2304,1,96]{0,2,1:T(8,128)(2,1)S(1)}, u32[]{:S(2)}) copy-start(bf16[2304,1,96]{0,2,1:T(8,128)(2,1)S(1)} %get-tuple-element.75) | copy-start | bytes 1327108
  31.6 3.0 copy-start.8
  34.6 1.1 copy-start.11
  35.6 251.9 %all-gather.4.cloned.1.call-start = ((), (), s32[]{:S(2)}) async-start(), calls=%async_computation | async-start | bytes 14598144 | tf_op jit(solution)/shard_map/all_gather | solution.py:238
  36.5 86.8 %collective-permute-start.2 = (bf16[1152,96]{0,1:T(8,128)(2,1)}, bf16[1152,96]{0,1:T(8,128)(2,1)}, u32[]{:S(2)}, u32[]{:S(2)}) collective-permute-start(bf16[1152,96]{0,1:T(8,128)(2,1)} %get-tuple-element.88), channel_id=1, source_target_pairs={{0,224},{32,192},{64,160},{96,128},{128,96},{160,64},{192,32},{224... | collective-permute-start | bytes 663560 | tf_op jit(solution)/shard_map/ppermute | solution.py:190
  43.9 79.4 %collective-permute-start.1 = (bf16[1152,96]{1,0:T(8,128)(2,1)}, bf16[1152,96]{1,0:T(8,128)(2,1)}, u32[]{:S(2)}, u32[]{:S(2)}) collective-permute-start(bf16[1152,96]{1,0:T(8,128)(2,1)} %get-tuple-element.80), channel_id=1, source_target_pairs={{0,224},{32,192},{64,160},{96,128},{128,96},{160,64},{192,32},{224... | collective-permute-start | bytes 663560 | tf_op jit(solution)/shard_map/ppermute | solution.py:189
  45.4 59.3 %collective-permute-start = (bf16[15,1,192]{0,2,1:T(8,128)(2,1)}, bf16[15,1,192]{0,2,1:T(8,128)(2,1)}, u32[]{:S(2)}, u32[]{:S(2)}) collective-permute-start(bf16[15,1,192]{0,2,1:T(8,128)(2,1)} %slice.172), channel_id=1, source_target_pairs={{32,0},{64,32},{96,64},{128,96},{160,128},{192,160},{224,192},{33,... | collective-permute-start | bytes 17288 | tf_op jit(solution)/shard_map/ppermute | solution.py:21
  82.1 12.9 %copy-start.13 = (s32[2]{0:T(128)S(1)}, s32[2]{0:T(128)}, u32[]{:S(2)}) copy-start(s32[2]{0:T(128)} %constant.168) | copy-start | bytes 28
  82.1 13.0 %copy-start.14 = (s32[2]{0:T(128)S(1)}, s32[2]{0:T(128)}, u32[]{:S(2)}) copy-start(s32[2]{0:T(128)} %constant.171) | copy-start | bytes 28
  97.1 7.5 %copy-start.7 = (bf16[2304,1,96]{0,2,1:T(8,128)(2,1)S(1)}, bf16[2304,1,96]{0,2,1:T(8,128)(2,1)}, u32[]{:S(2)}) copy-start(bf16[2304,1,96]{0,2,1:T(8,128)(2,1)} %copy-done.6) | copy-start | bytes 1327108
  97.1 7.5 %copy-start.9 = (bf16[2304,1,48]{0,2,1:T(8,128)(2,1)S(1)}, bf16[2304,1,48]{0,2,1:T(8,128)(2,1)}, u32[]{:S(2)}) copy-start(bf16[2304,1,48]{0,2,1:T(8,128)(2,1)} %copy-done.8) | copy-start | bytes 663556
  97.1 7.5 %copy-start.10 = (bf16[2304,1,48]{0,2,1:T(8,128)(2,1)S(1)}, bf16[2304,1,48]{0,2,1:T(8,128)(2,1)}, u32[]{:S(2)}) copy-start(bf16[2304,1,48]{0,2,1:T(8,128)(2,1)} %copy.120) | copy-start | bytes 663556
  103.0 0.8 copy-start.1
  103.8 0.8 copy-start.3
  108.9 32.9 %copy-start.4 = (f32[1152,1]{1,0:T(8,128)S(1)}, f32[1152,1]{1,0:T(8,128)}, u32[]{:S(2)}) copy-start(f32[1152,1]{1,0:T(8,128)} %copy-done.3) | copy-start | bytes 13828
  141.8 1.1 copy-start.2
  201.4 86.2 %copy-start.12 = (bf16[1152,96]{0,1:T(8,128)(2,1)S(1)}, bf16[1152,96]{0,1:T(8,128)(2,1)}, u32[]{:S(2)}) copy-start(bf16[1152,96]{0,1:T(8,128)(2,1)} %get-tuple-element.87) | copy-start | bytes 663556
  287.6 10.8 %copy-start.5 = (bf16[2576,192]{1,0:T(8,128)(2,1)S(1)}, bf16[2576,192]{1,0:T(8,128)(2,1)}, u32[]{:S(2)}) copy-start(bf16[2576,192]{1,0:T(8,128)(2,1)} %scatter_custom_fusion) | copy-start | bytes 2967556
  295.2 13.4 %collective-permute-start.3 = (bf16[1152,96]{0,1:T(8,128)(2,1)S(1)}, bf16[1152,96]{0,1:T(8,128)(2,1)S(1)}, u32[]{:S(2)}, u32[]{:S(2)}) collective-permute-start(bf16[1152,96]{0,1:T(8,128)(2,1)S(1)} %get-tuple-element.86), channel_id=1, source_target_pairs={{0,224},{32,192},{64,160},{96,128},{128,96},{160,64},{192,32},{224... | collective-permute-start | bytes 663560 | tf_op jit(solution)/shard_map/ppermute | solution.py:244
Sparse Core Ops, SparseCore 0:
  35.8 104.8 all-gather.5
  199.9 87.5 all-gather.3
